TPU v7x, 128 devices: a whole 4x4x4 slice. The times are simulated.
128 devices in a mesh: dp: 4 (over y_hi, core), head: 4 (over x), ctx: 8 (over z, y_lo).
Axes of the slice: x: 4, y: 4 (y_hi: 2, y_lo: 2; y = y_hi * 2 + y_lo), z: 4, core: 2. Of those that a mesh axis runs over, the one named last changes fastest.
Arguments:
- video: bfloat16 [16, 64, 24576], P('dp', 'head', 'ctx'), parts along dimension 0, may hold values from -6 to 6
- cache: bfloat16 [8, 64, 24576], P('dp', 'head', 'ctx'), parts along dimension 0, may hold values from -6 to 6
- conv_weight: bfloat16 [3, 3, 288, 192], replicated, may hold values from -0.125 to 0.125
- conv_bias: float32 [192], replicated, may hold values from -3 to 3
- down_weight: bfloat16 [768, 192], replicated, may hold values from -0.21875 to 0.21875
- patch_weight: bfloat16 [768, 5120], P(None, ('head', 'ctx')), may hold values from -0.21875 to 0.21875
- step_index: int32 [4], P('dp'), parts along dimension 0, may hold values from 0 to 999
- mod_weight: bfloat16 [256, 10240], P(None, ('head', 'ctx')), may hold values from -1 to 1
- qkv_weight: bfloat16 [5120, 20, 3, 128], P('ctx', 'head'), may hold values from -0.078125 to 0.078125
Outputs:
- attended: bfloat16 [16384, 2560], P(('dp', 'ctx'), 'head'), parts along dimension 0
There are 4 independent parts, one for each index of `dp`. A program takes and returns all parts, laid end to end along the dimension named above; an argument that names none is the same for every part. Nothing has to cross between parts.
All inputs are finite; a program needn't handle non-finite values.
Results may differ from a plain program's by a relative error of at most 0.015.
The roundings to bfloat16 on the way count: a program that leaves them out, or rounds other values in their place, can miss the bound.
Values may be sent and summed in bfloat16 or wider, within the bound.
No kernel may reach another device: no remote copies, remote signals or barrier semaphores. Data moves between devices by JAX's collectives and lax.ppermute only.
A program may use at most 128 MiB of HBM per device.

v0:
```python
import jax
import jax.numpy as jnp
from jax import lax
from jax.sharding import PartitionSpec as P

D = 5120
HDIM = 128
FREQ = 256


def with_halo(cells, sides, width):
    for axis, dim in sides:
        count = lax.axis_size(axis)
        ends = count - 1
        head = lax.slice_in_dim(cells, 0, width, axis=dim)
        tail = lax.slice_in_dim(cells, cells.shape[dim] - width, cells.shape[dim], axis=dim)
        cells = jnp.concatenate(
            [
                lax.ppermute(tail, axis, [(i, (i + 1) % count) for i in range(ends)]),
                cells,
                lax.ppermute(head, axis, [((i + 1) % count, i) for i in range(ends)]),
            ],
            axis=dim,
        )
    return cells


def gather_rows(cells, axis):
    count = lax.axis_size(axis)
    me = lax.axis_index(axis)
    parts = [cells] + [
        lax.ppermute(cells, axis, [(i, (i + s) % count) for i in range(count)])
        for s in range(1, count)
    ]
    stacked = jnp.stack(parts)
    return jnp.take(stacked, (me - jnp.arange(count)) % count, axis=0)


def split3(value):
    parts = []
    rest = value
    for _ in range(3):
        part = lax.reduce_precision(rest, exponent_bits=8, mantissa_bits=7)
        parts.append(part.astype(jnp.bfloat16))
        rest = rest - part
    return jnp.stack(parts)


def join3(parts):
    return (parts[0].astype(jnp.float32) + parts[1].astype(jnp.float32)) + parts[2].astype(jnp.float32)


def silu_act(value):
    return value * jax.nn.sigmoid(value)


def shards(
    video,
    cache,
    conv_weight,
    conv_bias,
    down_weight,
    patch_weight,
    step_index,
    mod_weight,
    qkv_weight,
):
    cin = conv_weight.shape[2] // 3
    cmid = conv_weight.shape[3]
    frame_count = video.shape[0]
    tile_rows = video.shape[1]
    tile_cols = video.shape[2] // cin
    n_ctx = lax.axis_size("ctx")
    c_idx = lax.axis_index("ctx")
    heads_here = qkv_weight.shape[1]
    out_cols = heads_here * 3 * HDIM
    local = qkv_weight.reshape(qkv_weight.shape[0], out_cols)
    rows = local.shape[0]
    half_rows = rows // 2
    quarter_rows = half_rows // 2
    core = lax.axis_index("dp") % 2
    mine = lax.dynamic_slice_in_dim(local, core * half_rows, half_rows, 0)
    n_dp = lax.axis_size("dp")

    def send(cells, step):
        return lax.ppermute(cells, "ctx", [(i, step(i)) for i in range(n_ctx)])

    def swap(cells):
        return lax.ppermute(cells, "dp", [(i, i ^ 1) for i in range(n_dp)])

    up = lambda i: (i + 2) % n_ctx
    down = lambda i: (i + n_ctx - 2) % n_ctx
    across = lambda i: i ^ 1
    from_up = (c_idx + n_ctx - 2) % n_ctx
    from_down = (c_idx + 2) % n_ctx
    opposite = (c_idx + 4) % n_ctx
    a_up = send(mine, up)
    a_down = send(mine, down)
    a_across = send(mine, across)
    b_up = send(a_up[:quarter_rows], up)
    b_down = send(a_down[quarter_rows:], down)
    b_across_up = send(a_across, up)
    b_across_down = send(a_across, down)
    c_first = send(b_up, across)
    c_second = send(b_down, across)
    stages = [
        [(a_up, from_up, 0), (a_down, from_down, 0), (a_across, c_idx ^ 1, 0)],
        [(b_up, opposite, 0), (b_down, opposite, quarter_rows),
         (b_across_up, from_up ^ 1, 0), (b_across_down, from_down ^ 1, 0)],
        [(c_first, opposite ^ 1, 0), (c_second, opposite ^ 1, quarter_rows)],
    ]
    stages = [
        (stage, ours, swap(ours))
        for stage, ours in ((s, jnp.concatenate([cells for cells, _, _ in s], 0)) for s in stages)
    ]
    frames = jnp.concatenate([cache, video], 0).reshape(frame_count + 2, tile_rows, tile_cols, cin)
    padded = with_halo(frames, (("head", 1), ("ctx", 2)), 1)
    total = jnp.zeros((frame_count, tile_rows, tile_cols, cmid), jnp.float32)
    for time_tap in range(3):
        for row_tap in range(3):
            slab = padded[time_tap : time_tap + frame_count, row_tap : row_tap + tile_rows]
            stacked = jnp.concatenate(
                [slab[:, :, col_tap : col_tap + tile_cols] for col_tap in range(3)], -1
            )
            total = total + jnp.einsum(
                "fyxc,cd->fyxd",
                stacked,
                conv_weight[time_tap, row_tap],
                preferred_element_type=jnp.float32,
            )
    hidden = silu_act(total + conv_bias).astype(jnp.bfloat16)
    stacked = (
        hidden.reshape(frame_count, tile_rows // 2, 2, tile_cols // 2, 2, cmid)
        .transpose(0, 1, 3, 2, 4, 5)
        .reshape(-1, 4 * cmid)
    )
    reduced = silu_act(jnp.dot(stacked, down_weight, preferred_element_type=jnp.float32)).astype(
        jnp.bfloat16
    )
    reduced = reduced.reshape(frame_count, tile_rows // 2, tile_cols // 2, cmid)
    patches = reduced.reshape(frame_count, tile_rows // 4, 2, tile_cols // 4, 2, cmid).transpose(
        0, 1, 3, 2, 4, 5
    )
    patches = patches.reshape(-1, 4 * cmid)
    patches, stages[0] = lax.optimization_barrier((patches, stages[0]))
    half = FREQ // 2
    freqs = jnp.exp(-jnp.log(10000.0) * jnp.arange(half, dtype=jnp.float32) / half)
    angles = step_index[0].astype(jnp.float32) * freqs
    timing = jnp.concatenate([jnp.cos(angles), jnp.sin(angles)]).astype(jnp.bfloat16)
    mod_share = jnp.dot(timing[None, :], mod_weight, preferred_element_type=jnp.float32)[0]
    n_head = lax.axis_size("head")
    n_ctx = lax.axis_size("ctx")
    h_idx = lax.axis_index("head")
    c_idx = lax.axis_index("ctx")
    quarter = D // n_head
    share_width = patch_weight.shape[1]
    share_parts = split3(mod_share).reshape(-1, share_width)
    carried = lax.all_gather(
        jnp.concatenate([patch_weight, share_parts], 0), "ctx", axis=1, tiled=True
    )
    weight_quarter = carried[: patch_weight.shape[0]]
    row_share = (
        carried[patch_weight.shape[0] :]
        .reshape(-1, n_ctx, share_width)
        .transpose(1, 0, 2)
        .reshape(n_ctx, 3, -1)
        .transpose(1, 0, 2)
        .reshape(3, -1)
    )
    row_parts = join3(row_share)
    block_patches = gather_rows(patches, "head").reshape(-1, patches.shape[1])
    embedded = jnp.dot(block_patches, weight_quarter, preferred_element_type=jnp.float32)
    embedded, stages[1] = lax.optimization_barrier((embedded, stages[1]))
    token_count = embedded.shape[0]
    riding = gather_rows(jnp.concatenate([jnp.sum(embedded * embedded, -1), row_parts]), "head")
    squares = riding[:, :token_count]
    modulation = riding[:, token_count:].reshape(-1)
    scale = lax.dynamic_slice_in_dim(modulation, h_idx * quarter, quarter)
    shift = lax.dynamic_slice_in_dim(modulation, D + h_idx * quarter, quarter)
    inverse = lax.rsqrt(jnp.sum(squares, 0) / D + 1e-06)[:, None]
    normed_quarter = (embedded * inverse * (1.0 + scale) + shift).astype(jnp.bfloat16)
    normed = lax.all_gather(normed_quarter, "head", axis=1, tiled=True)
    group_rows = normed.shape[0]
    heads_here = qkv_weight.shape[1]
    out_cols = heads_here * 3 * HDIM
    qkv = None
    for number, (stage, ours, theirs) in enumerate(stages):
        weights = [local] if number == 0 else []
        columns = [lax.dynamic_slice_in_dim(normed, c_idx * rows, rows, 1)] if number == 0 else []
        weights += [ours, theirs]
        for side in (core, 1 - core):
            for cells, block, offset in stage:
                columns.append(
                    lax.dynamic_slice_in_dim(
                        normed, block * rows + side * half_rows + offset, cells.shape[0], 1
                    )
                )
        part = jnp.dot(
            jnp.concatenate(columns, 1),
            jnp.concatenate(weights, 0),
            preferred_element_type=jnp.float32,
        )
        qkv = part if qkv is None else qkv + part
    qkv = qkv.astype(jnp.bfloat16).reshape(group_rows, heads_here, 3, HDIM)
    active = min(heads_here, n_ctx)
    received = [lax.dynamic_index_in_dim(qkv, jnp.minimum(c_idx, active - 1), 1, keepdims=False)]
    for s in range(1, n_ctx):
        target = jnp.minimum((c_idx + s) % n_ctx, active - 1)
        received.append(
            lax.ppermute(
                lax.dynamic_index_in_dim(qkv, target, 1, keepdims=False),
                "ctx",
                [(b, (b + s) % n_ctx) for b in range(n_ctx) if (b + s) % n_ctx < active],
            )
        )
    triple = jnp.stack(received)
    keys = triple[:, :, 1].reshape(-1, HDIM)
    values = triple[:, :, 2].reshape(-1, HDIM)
    inv_root = 1.0 / jnp.sqrt(jnp.float32(HDIM))

    def one_block(query):
        scores = jnp.dot(query, keys.T, preferred_element_type=jnp.float32) * inv_root
        best = jnp.maximum(jnp.float32(-1e30), jnp.max(scores, -1))
        probs = jnp.exp(scores - best[:, None])
        denom = jnp.sum(probs, -1)
        accum = jnp.dot(probs.astype(jnp.bfloat16), values, preferred_element_type=jnp.float32)
        return (accum / denom[:, None]).astype(jnp.bfloat16)

    attended = lax.map(one_block, triple[:, :, 0])
    returned = [attended[0]]
    for s in range(1, n_ctx):
        returned.append(
            lax.ppermute(attended[s], "ctx", [(d, (d - s) % n_ctx) for d in range(active)])
        )
    by_head = jnp.take(jnp.stack(returned), (jnp.arange(heads_here) - c_idx) % n_ctx, axis=0)
    return by_head.transpose(1, 0, 2).reshape(group_rows, heads_here * HDIM)


def solution(mesh):
    return jax.shard_map(
        shards,
        mesh=mesh,
        in_specs=(
            P("dp", "head", "ctx"),
            P("dp", "head", "ctx"),
            P(),
            P(),
            P(),
            P(None, ("head", "ctx")),
            P("dp"),
            P(None, ("head", "ctx")),
            P("ctx", "head", None, None),
        ),
        out_specs=P(("dp", "ctx"), "head"),
        check_vma=False,
    )
```

profile of v0, /device:TPU:0, one launch (start us, length us, event | category | flops | bytes accessed | tf_op | source)
XLA Modules:
  0.0 412.6 jit_solution(12301624210742114540)
XLA Ops:
  6.5 3.9 copy.47
  24.6 4.0 collective-permute-start
  48.3 5.5 %collective-permute-done.2 = bf16[6,18,1,96]{3,2,1,0:T(2,128)(2,1)S(1)} collective-permute-done((bf16[6,18,1,96]{3,2,1,0:T(2,128)(2,1)S(1)}, bf16[6,18,1,96]{3,2,1,0:T(2,128)(2,1)S(1)}, u32[]{:S(2)}, u32[]{:S(2)}) %collective-permute-start.2) | collective-permute-done | bytes 20768 | tf_op jit(solution)/shard_map/ppermute | solution.py:19
  64.6 14.0 %collective-permute-start.12 = (bf16[160,1920]{1,0:T(8,128)(2,1)S(1)}, bf16[160,1920]{1,0:T(8,128)(2,1)S(1)}, u32[]{:S(2)}, u32[]{:S(2)}) collective-permute-start(bf16[160,1920]{1,0:T(8,128)(2,1)S(1)} %slice.376), channel_id=1, source_target_pairs={{0,6},{1,7},{2,0},{3,1},{4,2},{5,3},{6,4},{7,5},{8,14},{9,15},{10,... | collective-permute-start | bytes 1843208 | tf_op jit(solution)/shard_map/ppermute | solution.py:86
  89.2 3.7 collective-permute-done.11
  94.9 22.1 %collective-permute-done.13 = bf16[320,1920]{1,0:T(8,128)(2,1)S(1)} collective-permute-done((bf16[320,1920]{1,0:T(8,128)(2,1)}, bf16[320,1920]{1,0:T(8,128)(2,1)S(1)}, u32[]{:S(2)}, u32[]{:S(2)}) %collective-permute-start.13) | collective-permute-done | bytes 1228832 | tf_op jit(solution)/shard_map/ppermute | solution.py:86
  147.6 5.3 %collective-permute-done.9 = bf16[128,768]{1,0:T(8,128)(2,1)S(1)} collective-permute-done((bf16[128,768]{1,0:T(8,128)(2,1)S(1)}, bf16[128,768]{1,0:T(8,128)(2,1)S(1)}, u32[]{:S(2)}, u32[]{:S(2)}) %collective-permute-start.9) | collective-permute-done | bytes 196640 | tf_op jit(solution)/shard_map/ppermute | solution.py:32
  173.1 7.4 %collective-permute-start.19 = (bf16[160,1920]{1,0:T(8,128)(2,1)S(1)}, bf16[160,1920]{1,0:T(8,128)(2,1)}, u32[]{:S(2)}, u32[]{:S(2)}) collective-permute-start(bf16[160,1920]{1,0:T(8,128)(2,1)S(1)} %copy-done.11), channel_id=1, source_target_pairs={{0,1},{1,0},{2,3},{3,2},{4,5},{5,4},{6,7},{7,6},{8,9},{9,8},{10,11... | collective-permute-start | bytes 1843208 | tf_op jit(solution)/shard_map/ppermute | solution.py:86
  183.6 11.8 %collective-permute-done.19 = bf16[160,1920]{1,0:T(8,128)(2,1)} collective-permute-done((bf16[160,1920]{1,0:T(8,128)(2,1)S(1)}, bf16[160,1920]{1,0:T(8,128)(2,1)}, u32[]{:S(2)}, u32[]{:S(2)}) %collective-permute-start.19) | collective-permute-done | bytes 614432 | tf_op jit(solution)/shard_map/ppermute | solution.py:86
  195.4 11.0 %collective-permute-done.20 = bf16[160,1920]{1,0:T(8,128)(2,1)} collective-permute-done((bf16[160,1920]{1,0:T(8,128)(2,1)}, bf16[160,1920]{1,0:T(8,128)(2,1)}, u32[]{:S(2)}, u32[]{:S(2)}) %collective-permute-start.20) | collective-permute-done | bytes 614432 | tf_op jit(solution)/shard_map/ppermute | solution.py:86
  209.3 27.2 %all-gather.5.cloned.1.call-done = bf16[512,5120]{1,0:T(8,128)(2,1)} async-done(((bf16[512,1280]{1,0:T(8,128)(2,1)}), bf16[512,5120]{1,0:T(8,128)(2,1)}) %all-gather.5.cloned.1.call-update) | async-done | bytes 5242896 | tf_op jit(solution)/shard_map/all_gather | solution.py:182
  238.5 6.8 %constant_dynamic-slice_fusion.12 = (bf16[512,320]{1,0:T(8,128)(2,1)S(1)}, bf16[512,320]{1,0:T(8,128)(2,1)}, bf16[512,320]{1,0:T(8,128)(2,1)}, bf16[512,320]{1,0...) fusion(bf16[512,5120]{1,0:T(8,128)(2,1)} %all-gather.5.cloned.1, ...), kind=kLoop, calls=%fused_computation.239 | loop fusion | bytes 6553640 | tf_op jit(solution)/shard_map/dynamic_slice | solution.py:194
  245.3 4.2 %concatenate.125 = bf16[512,2560]{1,0:T(8,128)(2,1)S(1)} concatenate(bf16[512,640]{1,0:T(8,128)(2,1)} %constant_dynamic-slice_fusion.26, bf16[512,320]{1,0:T(8,128)(2,1)} %get-tuple-element.94, bf16[512,320]{1,0:T(8,128)(2,1)} %get-tuple-element.93, bf16[512,320]{1,0:T(8,128)(2,1)} %get-tuple-element.92, bf16[512,320]{1,0:T(8,128)(2,1)} %get-tuple-element.91, ...), dimensions={1} | concatenate | bytes 5242880 | tf_op jit(solution)/shard_map/concatenate | solution.py:199
  249.5 4.3 %constant_dynamic-slice_fusion.14 = (bf16[512,160]{1,0:T(8,128)(2,1)S(1)}, bf16[512,160]{1,0:T(8,128)(2,1)}, bf16[512,160]{1,0:T(8,128)(2,1)}, bf16[512,160]{1,0...) fusion(bf16[512,5120]{1,0:T(8,128)(2,1)} %all-gather.5.cloned.1, ...), kind=kLoop, calls=%fused_computation.241 | loop fusion | bytes 2621472 | tf_op jit(solution)/shard_map/dynamic_slice | solution.py:194
  253.9 4.9 %concatenate.127 = bf16[512,1920]{1,0:T(8,128)(2,1)} concatenate(bf16[512,160]{1,0:T(8,128)(2,1)} %get-tuple-element.102, bf16[512,160]{1,0:T(8,128)(2,1)} %get-tuple-element.101, bf16[512,320]{1,0:T(8,128)(2,1)} %get-tuple-element.88, bf16[512,320]{1,0:T(8,128)(2,1)} %get-tuple-element.87, bf16[512,160]{1,0:T(8,128)(2,1)} %get-tuple-element.100, ...), dimensions={1} | concatenate | bytes 3932160 | tf_op jit(solution)/shard_map/concatenate | solution.py:199
  258.8 8.6 %fusion.21 = f32[512,1920]{1,0:T(8,128)S(1)} fusion(bf16[512,2560]{1,0:T(8,128)(2,1)S(1)} %concatenate.125, bf16[960,1920]{1,0:T(8,128)(2,1)} %collective-permute-done.7, bf16[960,1920]{1,0:T(8,128)(2,1)} %constant_dynamic-update-slice_fusion.9, bf16[640,1920]{1,0:T(8,128)(2,1)} %copy.53), kind=kOutput, calls=%fused_computation.18 | convolution fusion | flops 5062656000 | bytes 16384000 | tf_op jit(solution)/shard_map/dot_general | solution.py:198
  267.5 3.6 fusion.33
  271.2 9.0 %add_convert_fusion = bf16[512,1920]{1,0:T(8,128)(2,1)} fusion(f32[512,1920]{1,0:T(8,128)S(1)} %fusion.33, f32[512,1920]{1,0:T(8,128)S(1)} %fusion.21, bf16[512,1920]{1,0:T(8,128)(2,1)S(1)} %copy-done.4, bf16[960,1920]{1,0:T(8,128)(2,1)} %collective-permute-done.15, bf16[960,1920]{1,0:T(8,128)(2,1)} %constant_dynamic-update-slice_fusion.12), kind=kOutput, calls=%fused_computation.28 | convolution fusion | flops 3792568320 | bytes 19169280 | tf_op jit(solution)/shard_map/dot_general | solution.py:198
  292.8 3.6 collective-permute-start.23
  307.0 19.6 %collective-permute-done.23 = bf16[512,3,128]{2,0,1:T(8,128)(2,1)} collective-permute-done((bf16[512,3,128]{2,0,1:T(8,128)(2,1)}, bf16[512,3,128]{2,0,1:T(8,128)(2,1)}, u32[]{:S(2)}, u32[]{:S(2)}) %collective-permute-start.23) | collective-permute-done | bytes 393248 | tf_op jit(solution)/shard_map/ppermute | solution.py:210
  331.2 12.2 %collective-permute-done.28 = bf16[512,3,128]{2,0,1:T(8,128)(2,1)S(1)} collective-permute-done((bf16[512,3,128]{2,0,1:T(8,128)(2,1)S(1)}, bf16[512,3,128]{2,0,1:T(8,128)(2,1)S(1)}, u32[]{:S(2)}, u32[]{:S(2)}) %collective-permute-start.28) | collective-permute-done | bytes 393248 | tf_op jit(solution)/shard_map/ppermute | solution.py:210
  344.8 35.1 %while.10 = (s32[]{:T(128)}, bf16[8,512,128]{2,1,0:T(8,128)(2,1)S(1)}, bf16[8,512,128]{2,1,0:T(8,128)(2,1)S(1)}, bf16[4096,128]{1,0:T(8,128)(2,1)S(1)}, bf16[4096,128]{1,0:T(8,128)(2,1)}, /*index=5*/s32[]{:T(128)}) while((s32[]{:T(128)}, bf16[8,512,128]{2,1,0:T(8,128)(2,1)S(1)}, bf16[8,512,128]{2,1,0:T(8,128)(2,1)S(1)}, ...), condition=%wide.region_5.6_spmd, body=%wide.region_2.5_spmd.sunk | while | flops 1090649600 | bytes 31733864 | solution.py:229
  385.9 7.5 %collective-permute-start.32 = (bf16[512,128]{1,0:T(8,128)(2,1)S(1)}, bf16[512,128]{1,0:T(8,128)(2,1)S(1)}, u32[]{:S(2)}, u32[]{:S(2)}) collective-permute-start(bf16[512,128]{1,0:T(8,128)(2,1)S(1)} %get-tuple-element.117), channel_id=1, source_target_pairs={{0,4},{1,5},{2,6},{3,7},{4,0},{8,12},{9,13},{10,14},{11,15},{12,8}... | collective-permute-start | bytes 393224 | tf_op jit(solution)/shard_map/ppermute | solution.py:233
  396.1 3.9 collective-permute-start.35
  (275 shorter events, 192.7 us)
Async XLA Ops:
  6.5 138.3 %all-gather.3.cloned.1.call-start = ((), (), s32[]{:S(2)}) async-start(), calls=%async_computation | async-start | bytes 2580480 | tf_op jit(solution)/shard_map/all_gather | solution.py:158
  14.7 46.0 %collective-permute-start.4 = (bf16[320,1920]{1,0:T(8,128)(2,1)}, bf16[320,1920]{1,0:T(8,128)(2,1)}, u32[]{:S(2)}, u32[]{:S(2)}) collective-permute-start(bf16[320,1920]{1,0:T(8,128)(2,1)} %copy.48), channel_id=1, source_target_pairs={{0,2},{1,3},{2,4},{3,5},{4,6},{5,7},{6,0},{7,1},{8,10},{9,11},{10,... | collective-permute-start | bytes 3686408 | tf_op jit(solution)/shard_map/ppermute | solution.py:86
  16.7 46.8 %collective-permute-start.5 = (bf16[320,1920]{1,0:T(8,128)(2,1)}, bf16[320,1920]{1,0:T(8,128)(2,1)}, u32[]{:S(2)}, u32[]{:S(2)}) collective-permute-start(bf16[320,1920]{1,0:T(8,128)(2,1)} %copy.48), channel_id=1, source_target_pairs={{0,6},{1,7},{2,0},{3,1},{4,2},{5,3},{6,4},{7,5},{8,14},{9,15},{10,... | collective-permute-start | bytes 3686408 | tf_op jit(solution)/shard_map/ppermute | solution.py:86
  18.9 59.7 %collective-permute-start.6 = (bf16[320,1920]{1,0:T(8,128)(2,1)}, bf16[320,1920]{1,0:T(8,128)(2,1)}, u32[]{:S(2)}, u32[]{:S(2)}) collective-permute-start(bf16[320,1920]{1,0:T(8,128)(2,1)} %copy.48), channel_id=1, source_target_pairs={{0,1},{1,0},{2,3},{3,2},{4,5},{5,4},{6,7},{7,6},{8,9},{9,8},{10,11... | collective-permute-start | bytes 3686408 | tf_op jit(solution)/shard_map/ppermute | solution.py:86
  24.6 17.3 %collective-permute-start = (bf16[6,1,32,96]{3,2,1,0:T(8,128)(2,1)}, bf16[6,1,32,96]{3,2,1,0:T(8,128)(2,1)}, u32[]{:S(2)}, u32[]{:S(2)}) collective-permute-start(bf16[6,1,32,96]{3,2,1,0:T(8,128)(2,1)} %get-tuple-element.150), channel_id=1, source_target_pairs={{0,8},{8,16},{16,24},{1,9},{9,17},{17,25},{2,10},{10,18},{18,26},{... | collective-permute-start | bytes 110600 | tf_op jit(solution)/shard_map/ppermute | solution.py:19
  33.8 202.7 %all-gather.5.cloned.1.call-start = ((), (), s32[]{:S(2)}) async-start(), calls=%async_computation.1 | async-start | bytes 6553600 | tf_op jit(solution)/shard_map/all_gather | solution.py:182
  61.9 31.1 %collective-permute-start.11 = (bf16[160,1920]{1,0:T(8,128)(2,1)S(1)}, bf16[160,1920]{1,0:T(8,128)(2,1)S(1)}, u32[]{:S(2)}, u32[]{:S(2)}) collective-permute-start(bf16[160,1920]{1,0:T(8,128)(2,1)S(1)} %slice.375), channel_id=1, source_target_pairs={{0,2},{1,3},{2,4},{3,5},{4,6},{5,7},{6,0},{7,1},{8,10},{9,11},{10,... | collective-permute-start | bytes 1843208 | tf_op jit(solution)/shard_map/ppermute | solution.py:86
  64.6 29.3 %collective-permute-start.12 = (bf16[160,1920]{1,0:T(8,128)(2,1)S(1)}, bf16[160,1920]{1,0:T(8,128)(2,1)S(1)}, u32[]{:S(2)}, u32[]{:S(2)}) collective-permute-start(bf16[160,1920]{1,0:T(8,128)(2,1)S(1)} %slice.376), channel_id=1, source_target_pairs={{0,6},{1,7},{2,0},{3,1},{4,2},{5,3},{6,4},{7,5},{8,14},{9,15},{10,... | collective-permute-start | bytes 1843208 | tf_op jit(solution)/shard_map/ppermute | solution.py:86
  78.6 38.4 %collective-permute-start.13 = (bf16[320,1920]{1,0:T(8,128)(2,1)}, bf16[320,1920]{1,0:T(8,128)(2,1)S(1)}, u32[]{:S(2)}, u32[]{:S(2)}) collective-permute-start(bf16[320,1920]{1,0:T(8,128)(2,1)} %collective-permute-done.6), channel_id=1, source_target_pairs={{0,2},{1,3},{2,4},{3,5},{4,6},{5,7},{6,0},{7,1},{8,10},{9,11},{10,... | collective-permute-start | bytes 3686408 | tf_op jit(solution)/shard_map/ppermute | solution.py:86
  81.5 36.7 %collective-permute-start.14 = (bf16[320,1920]{1,0:T(8,128)(2,1)}, bf16[320,1920]{1,0:T(8,128)(2,1)S(1)}, u32[]{:S(2)}, u32[]{:S(2)}) collective-permute-start(bf16[320,1920]{1,0:T(8,128)(2,1)} %collective-permute-done.6), channel_id=1, source_target_pairs={{0,6},{1,7},{2,0},{3,1},{4,2},{5,3},{6,4},{7,5},{8,14},{9,15},{10,... | collective-permute-start | bytes 3686408 | tf_op jit(solution)/shard_map/ppermute | solution.py:86
  89.2 49.8 %collective-permute-start.7 = (bf16[960,1920]{1,0:T(8,128)(2,1)}, bf16[960,1920]{1,0:T(8,128)(2,1)}, u32[]{:S(2)}, u32[]{:S(2)}) collective-permute-start(bf16[960,1920]{1,0:T(8,128)(2,1)} %constant_dynamic-update-slice_fusion.9), channel_id=1, source_target_pairs={{0,32},{32,0},{64,96},{96,64},{1,33},{33,1},{65,97},{97,65},{2,34}... | collective-permute-start | bytes 11059208 | tf_op jit(solution)/shard_map/ppermute | solution.py:89
  119.3 41.1 %collective-permute-start.15 = (bf16[960,1920]{1,0:T(8,128)(2,1)}, bf16[960,1920]{1,0:T(8,128)(2,1)}, u32[]{:S(2)}, u32[]{:S(2)}) collective-permute-start(bf16[960,1920]{1,0:T(8,128)(2,1)} %constant_dynamic-update-slice_fusion.12), channel_id=1, source_target_pairs={{0,32},{32,0},{64,96},{96,64},{1,33},{33,1},{65,97},{97,65},{2,34}... | collective-permute-start | bytes 11059208 | tf_op jit(solution)/shard_map/ppermute | solution.py:89
  173.1 22.3 %collective-permute-start.19 = (bf16[160,1920]{1,0:T(8,128)(2,1)S(1)}, bf16[160,1920]{1,0:T(8,128)(2,1)}, u32[]{:S(2)}, u32[]{:S(2)}) collective-permute-start(bf16[160,1920]{1,0:T(8,128)(2,1)S(1)} %copy-done.11), channel_id=1, source_target_pairs={{0,1},{1,0},{2,3},{3,2},{4,5},{5,4},{6,7},{7,6},{8,9},{9,8},{10,11... | collective-permute-start | bytes 1843208 | tf_op jit(solution)/shard_map/ppermute | solution.py:86
  180.5 25.9 %collective-permute-start.20 = (bf16[160,1920]{1,0:T(8,128)(2,1)}, bf16[160,1920]{1,0:T(8,128)(2,1)}, u32[]{:S(2)}, u32[]{:S(2)}) collective-permute-start(bf16[160,1920]{1,0:T(8,128)(2,1)} %copy-done.12), channel_id=1, source_target_pairs={{0,1},{1,0},{2,3},{3,2},{4,5},{5,4},{6,7},{7,6},{8,9},{9,8},{10,11... | collective-permute-start | bytes 1843208 | tf_op jit(solution)/shard_map/ppermute | solution.py:86
  208.8 58.6 %collective-permute-start.21 = (bf16[320,1920]{1,0:T(8,128)(2,1)}, bf16[320,1920]{1,0:T(8,128)(2,1)}, u32[]{:S(2)}, u32[]{:S(2)}) collective-permute-start(bf16[320,1920]{1,0:T(8,128)(2,1)} %pad_maximum_fusion.2), channel_id=1, source_target_pairs={{0,32},{32,0},{64,96},{96,64},{1,33},{33,1},{65,97},{97,65},{2,34}... | collective-permute-start | bytes 3686408 | tf_op jit(solution)/shard_map/ppermute | solution.py:89
  286.2 18.5 %collective-permute-start.22 = (bf16[512,3,128]{2,0,1:T(8,128)(2,1)}, bf16[512,3,128]{2,0,1:T(8,128)(2,1)}, u32[]{:S(2)}, u32[]{:S(2)}) collective-permute-start(bf16[512,3,128]{2,0,1:T(8,128)(2,1)} %bitcast.49), channel_id=1, source_target_pairs={{0,1},{1,2},{2,3},{3,4},{7,0},{8,9},{9,10},{10,11},{11,12},{15,8},... | collective-permute-start | bytes 1179656 | tf_op jit(solution)/shard_map/ppermute | solution.py:210
  292.8 33.8 %collective-permute-start.23 = (bf16[512,3,128]{2,0,1:T(8,128)(2,1)}, bf16[512,3,128]{2,0,1:T(8,128)(2,1)}, u32[]{:S(2)}, u32[]{:S(2)}) collective-permute-start(bf16[512,3,128]{2,0,1:T(8,128)(2,1)} %bitcast.51), channel_id=1, source_target_pairs={{0,2},{1,3},{2,4},{6,0},{7,1},{8,10},{9,11},{10,12},{14,8},{15,9},... | collective-permute-start | bytes 1179656 | tf_op jit(solution)/shard_map/ppermute | solution.py:210
  297.4 31.6 %collective-permute-start.24 = (bf16[512,3,128]{2,0,1:T(8,128)(2,1)}, bf16[512,3,128]{2,0,1:T(8,128)(2,1)}, u32[]{:S(2)}, u32[]{:S(2)}) collective-permute-start(bf16[512,3,128]{2,0,1:T(8,128)(2,1)} %bitcast.53), channel_id=1, source_target_pairs={{0,3},{1,4},{5,0},{6,1},{7,2},{8,11},{9,12},{13,8},{14,9},{15,10},... | collective-permute-start | bytes 1179656 | tf_op jit(solution)/shard_map/ppermute | solution.py:210
  300.5 29.5 %collective-permute-start.25 = (bf16[512,3,128]{2,0,1:T(8,128)(2,1)}, bf16[512,3,128]{2,0,1:T(8,128)(2,1)}, u32[]{:S(2)}, u32[]{:S(2)}) collective-permute-start(bf16[512,3,128]{2,0,1:T(8,128)(2,1)} %bitcast.55), channel_id=1, source_target_pairs={{0,4},{4,0},{5,1},{6,2},{7,3},{8,12},{12,8},{13,9},{14,10},{15,11}... | collective-permute-start | bytes 1179656 | tf_op jit(solution)/shard_map/ppermute | solution.py:210
  302.8 28.2 %collective-permute-start.26 = (bf16[512,3,128]{2,0,1:T(8,128)(2,1)S(1)}, bf16[512,3,128]{2,0,1:T(8,128)(2,1)S(1)}, u32[]{:S(2)}, u32[]{:S(2)}) collective-permute-start(bf16[512,3,128]{2,0,1:T(8,128)(2,1)S(1)} %bitcast.187), channel_id=1, source_target_pairs={{3,0},{4,1},{5,2},{6,3},{7,4},{11,8},{12,9},{13,10},{14,11},{15,12... | collective-permute-start | bytes 1179656 | tf_op jit(solution)/shard_map/ppermute | solution.py:210
  304.6 26.5 %collective-permute-start.27 = (bf16[512,3,128]{2,0,1:T(8,128)(2,1)S(1)}, bf16[512,3,128]{2,0,1:T(8,128)(2,1)S(1)}, u32[]{:S(2)}, u32[]{:S(2)}) collective-permute-start(bf16[512,3,128]{2,0,1:T(8,128)(2,1)S(1)} %bitcast.186), channel_id=1, source_target_pairs={{2,0},{3,1},{4,2},{5,3},{6,4},{10,8},{11,9},{12,10},{13,11},{14,12... | collective-permute-start | bytes 1179656 | tf_op jit(solution)/shard_map/ppermute | solution.py:210
  326.6 16.8 %collective-permute-start.28 = (bf16[512,3,128]{2,0,1:T(8,128)(2,1)S(1)}, bf16[512,3,128]{2,0,1:T(8,128)(2,1)S(1)}, u32[]{:S(2)}, u32[]{:S(2)}) collective-permute-start(bf16[512,3,128]{2,0,1:T(8,128)(2,1)S(1)} %bitcast.185), channel_id=1, source_target_pairs={{1,0},{2,1},{3,2},{4,3},{5,4},{9,8},{10,9},{11,10},{12,11},{13,12}... | collective-permute-start | bytes 1179656 | tf_op jit(solution)/shard_map/ppermute | solution.py:210
  383.9 16.1 %collective-permute-start.31 = (bf16[512,128]{1,0:T(8,128)(2,1)S(1)}, bf16[512,128]{1,0:T(8,128)(2,1)S(1)}, u32[]{:S(2)}, u32[]{:S(2)}) collective-permute-start(bf16[512,128]{1,0:T(8,128)(2,1)S(1)} %get-tuple-element.118), channel_id=1, source_target_pairs={{0,5},{1,6},{2,7},{3,0},{4,1},{8,13},{9,14},{10,15},{11,8},{12,9},... | collective-permute-start | bytes 393224 | tf_op jit(solution)/shard_map/ppermute | solution.py:233
  385.9 14.7 %collective-permute-start.32 = (bf16[512,128]{1,0:T(8,128)(2,1)S(1)}, bf16[512,128]{1,0:T(8,128)(2,1)S(1)}, u32[]{:S(2)}, u32[]{:S(2)}) collective-permute-start(bf16[512,128]{1,0:T(8,128)(2,1)S(1)} %get-tuple-element.117), channel_id=1, source_target_pairs={{0,4},{1,5},{2,6},{3,7},{4,0},{8,12},{9,13},{10,14},{11,15},{12,8}... | collective-permute-start | bytes 393224 | tf_op jit(solution)/shard_map/ppermute | solution.py:233
  (45 other events, 435.3 us)
Sparse Core Ops, SparseCore 0:
  33.9 59.6 all-gather.2
  173.2 63.2 all-gather.4
where the time goes:
time: 421 us; the launch traced here: 413 us
  waiting for transfers between devices  125 us (30%)
  local copies, waits for them, and re-layouts  98.2 us (23%)
  starting transfers between devices  87 us (21%)
  matrix products  59.7 us (14%)
  other arithmetic  26.7 us (6%)
  between operations  15.3 us (4%)
    ppermute x9, waiting for transfers between devices, send(): return lax.ppermute(cells, 'ctx', [(i, step(i)) for i in range(n_ctx)])  48.7 us
    ppermute x9, starting transfers between devices, send(): return lax.ppermute(cells, 'ctx', [(i, step(i)) for i in range(n_ctx)])  32.1 us
    ppermute x7, waiting for transfers between devices, shards(): lax.ppermute(lax.dynamic_index_in_dim(qkv, target, 1, keepdims=False), 'c...  31.9 us
    all_gather x1, waiting for transfers between devices, shards(): normed = lax.all_gather(normed_quarter, 'head', axis=1, tiled=True)  27.2 us
    dot_general x3, matrix products, shards(): jnp.dot(jnp.concatenate(columns, 1), jnp.concatenate(weights, 0), preferr...  21.3 us
    unnamed x68, local copies, waits for them, and re-layouts  20.4 us
    ppermute x7, starting transfers between devices, shards(): lax.ppermute(attended[s], 'ctx', [(d, (d - s) % n_ctx) for d in range(act...  19.8 us
    ppermute x7, starting transfers between devices, shards(): lax.ppermute(lax.dynamic_index_in_dim(qkv, target, 1, keepdims=False), 'c...  15.2 us
  transfers between devices with their start and end apart: 38, of which 17 were waited for; matrix products, arithmetic and copies ran while one was open for 27% of the time, Pallas kernels for 0%

commit v1 on v0

--- a/solution.py
+++ b/solution.py
@@ -142,7 +142,6 @@
         0, 1, 3, 2, 4, 5
     )
     patches = patches.reshape(-1, 4 * cmid)
-    patches, stages[0] = lax.optimization_barrier((patches, stages[0]))
     half = FREQ // 2
     freqs = jnp.exp(-jnp.log(10000.0) * jnp.arange(half, dtype=jnp.float32) / half)
     angles = step_index[0].astype(jnp.float32) * freqs
@@ -170,7 +169,6 @@
     row_parts = join3(row_share)
     block_patches = gather_rows(patches, "head").reshape(-1, patches.shape[1])
     embedded = jnp.dot(block_patches, weight_quarter, preferred_element_type=jnp.float32)
-    embedded, stages[1] = lax.optimization_barrier((embedded, stages[1]))
     token_count = embedded.shape[0]
     riding = gather_rows(jnp.concatenate([jnp.sum(embedded * embedded, -1), row_parts]), "head")
     squares = riding[:, :token_count]

time: 421 us -> 411 us (0.976)
  starting transfers between devices: 87 us -> 67.8 us
  waiting for transfers between devices: 125 us -> 141 us
  local copies, waits for them, and re-layouts: 98.2 us -> 85.9 us
  other arithmetic: 26.7 us -> 35.9 us
    ppermute x9, waiting for transfers between devices: 48.7 us -> 76.2 us  [send(): return lax.ppermute(cells, 'ctx', [(i, step(i)) for i in range(n_ctx)])]
    all_gather x1, waiting for transfers between devices: 27.2 us -> 0.01 us  [shards(): normed = lax.all_gather(normed_quarter, 'head', axis=1, tiled=True)]
    ppermute x9, starting transfers between devices: 32.1 us -> 11.9 us  [send(): return lax.ppermute(cells, 'ctx', [(i, step(i)) for i in range(n_ctx)])]
    all_gather x1, waiting for transfers between devices: 0.01 us -> 13.8 us  [shards(): lax.all_gather(jnp.concatenate([patch_weight, share_parts], 0), 'ctx', ax...]
    concatenate x1 -> x3, other arithmetic: 2.41 us -> 14.7 us  [shards(): jnp.concatenate([cells for cells, _, _ in s], 0)]
    slice x6, local copies, waits for them, and re-layouts: 8.45 us -> 2.17 us  [shards(): slab[:, :, col_tap:col_tap + tile_cols]]
    ppermute x2, waiting for transfers between devices: 5.52 us -> 0.01 us  [with_halo(): lax.ppermute(tail, axis, [(i, (i + 1) % count) for i in range(ends)])]
    concatenate x2, local copies, waits for them, and re-layouts: 3.57 us -> 8.33 us  [shards(): jnp.concatenate(weights, 0)]
  transfers between devices with their start and end apart: 38 -> 38, of which waited for: 17 -> 16; matrix products, arithmetic and copies ran while one was open for 27% -> 30% of each run, Pallas kernels for 0% -> 0%
where the time goes in v1:
time: 411 us; the launch traced here: 406 us
  waiting for transfers between devices  141 us (34%)
  local copies, waits for them, and re-layouts  85.9 us (21%)
  starting transfers between devices  67.8 us (16%)
  matrix products  59 us (14%)
  other arithmetic  35.9 us (9%)
  between operations  15.5 us (4%)
    ppermute x9, waiting for transfers between devices, send(): return lax.ppermute(cells, 'ctx', [(i, step(i)) for i in range(n_ctx)])  76.2 us
    ppermute x7, waiting for transfers between devices, shards(): lax.ppermute(lax.dynamic_index_in_dim(qkv, target, 1, keepdims=False), 'c...  34.7 us
    dot_general x3, matrix products, shards(): jnp.dot(jnp.concatenate(columns, 1), jnp.concatenate(weights, 0), preferr...  22.6 us
    unnamed x91, local copies, waits for them, and re-layouts  22.3 us
    ppermute x7, starting transfers between devices, shards(): lax.ppermute(attended[s], 'ctx', [(d, (d - s) % n_ctx) for d in range(act...  19 us
    concatenate x3, other arithmetic, shards(): jnp.concatenate([cells for cells, _, _ in s], 0)  14.7 us
    ppermute x7, starting transfers between devices, shards(): lax.ppermute(lax.dynamic_index_in_dim(qkv, target, 1, keepdims=False), 'c...  13.9 us
    all_gather x1, waiting for transfers between devices, shards(): lax.all_gather(jnp.concatenate([patch_weight, share_parts], 0), 'ctx', ax...  13.8 us
  transfers between devices with their start and end apart: 38, of which 16 were waited for; matrix products, arithmetic and copies ran while one was open for 30% of the time, Pallas kernels for 0%

profile of v1, /device:TPU:0, one launch (start us, length us, event | category | flops | bytes accessed | tf_op | source)
XLA Modules:
  0.0 405.9 jit_solution(1501326123293183864)
XLA Ops:
  10.1 4.1 %collective-permute-start = (bf16[6,1,32,96]{3,2,1,0:T(8,128)(2,1)}, bf16[6,1,32,96]{3,2,1,0:T(8,128)(2,1)}, u32[]{:S(2)}, u32[]{:S(2)}) collective-permute-start(bf16[6,1,32,96]{3,2,1,0:T(8,128)(2,1)} %get-tuple-element.110), channel_id=1, source_target_pairs={{0,8},{8,16},{16,24},{1,9},{9,17},{17,25},{2,10},{10,18},{18,26},{... | collective-permute-start | bytes 110600 | tf_op jit(solution)/shard_map/ppermute | solution.py:19
  22.6 3.5 collective-permute-start.2
  57.8 4.0 collective-permute-done.5
  63.7 13.8 %all-gather.3.cloned.1.call-done = bf16[774,1280]{0,1:T(8,128)(2,1)} async-done(((bf16[774,160]{0,1:T(8,128)(2,1)}), bf16[774,1280]{0,1:T(8,128)(2,1)}) %all-gather.3.cloned.1.call-update) | async-done | bytes 1981456 | tf_op jit(solution)/shard_map/all_gather | solution.py:157
  93.0 3.9 copy.52
  104.4 24.1 %collective-permute-done.12 = bf16[320,1920]{1,0:T(8,128)(2,1)S(1)} collective-permute-done((bf16[320,1920]{1,0:T(8,128)(2,1)}, bf16[320,1920]{1,0:T(8,128)(2,1)S(1)}, u32[]{:S(2)}, u32[]{:S(2)}) %collective-permute-start.12) | collective-permute-done | bytes 1228832 | tf_op jit(solution)/shard_map/ppermute | solution.py:86
  135.2 6.4 %pad_maximum_fusion = bf16[960,1920]{1,0:T(8,128)(2,1)} fusion(bf16[320,1920]{1,0:T(8,128)(2,1)S(1)} %collective-permute-done.12, bf16[320,1920]{1,0:T(8,128)(2,1)S(1)} %collective-permute-done.11, bf16[320,1920]{1,0:T(8,128)(2,1)S(1)} %collective-permute-done.10), kind=kLoop, calls=%fused_computation.35 | loop fusion | flops 11059200 | bytes 7372800 | tf_op jit(solution)/shard_map/concatenate | solution.py:114
  141.8 27.5 %collective-permute-done.14 = bf16[160,1920]{1,0:T(8,128)(2,1)S(1)} collective-permute-done((bf16[160,1920]{1,0:T(8,128)(2,1)S(1)}, bf16[160,1920]{1,0:T(8,128)(2,1)S(1)}, u32[]{:S(2)}, u32[]{:S(2)}) %collective-permute-start.14) | collective-permute-done | bytes 614432 | tf_op jit(solution)/shard_map/ppermute | solution.py:86
  169.5 7.1 %pad_maximum_fusion.1 = bf16[960,1920]{1,0:T(8,128)(2,1)} fusion(bf16[320,1920]{1,0:T(8,128)(2,1)S(1)} %collective-permute-done.17, bf16[320,1920]{1,0:T(8,128)(2,1)S(1)} %collective-permute-done.16, bf16[160,1920]{1,0:T(8,128)(2,1)S(1)} %collective-permute-done.15, bf16[160,1920]{1,0:T(8,128)(2,1)S(1)} %collective-permute-done.14), kind=kLoop, calls=%fused_computation.36 | loop fusion | flops 14745600 | bytes 7372800 | tf_op jit(solution)/shard_map/concatenate | solution.py:114
  191.0 11.8 %collective-permute-done.19 = bf16[160,1920]{1,0:T(8,128)(2,1)S(1)} collective-permute-done((bf16[160,1920]{1,0:T(8,128)(2,1)S(1)}, bf16[160,1920]{1,0:T(8,128)(2,1)S(1)}, u32[]{:S(2)}, u32[]{:S(2)}) %collective-permute-start.19) | collective-permute-done | bytes 614432 | tf_op jit(solution)/shard_map/ppermute | solution.py:86
  202.8 12.6 %collective-permute-done.20 = bf16[160,1920]{1,0:T(8,128)(2,1)S(1)} collective-permute-done((bf16[160,1920]{1,0:T(8,128)(2,1)S(1)}, bf16[160,1920]{1,0:T(8,128)(2,1)S(1)}, u32[]{:S(2)}, u32[]{:S(2)}) %collective-permute-start.20) | collective-permute-done | bytes 614432 | tf_op jit(solution)/shard_map/ppermute | solution.py:86
  219.0 4.2 %constant_dynamic-update-slice_fusion.9 = bf16[2560,1920]{1,0:T(8,128)(2,1)} fusion(bf16[2560,1920]{1,0:T(8,128)(2,1)} %constant_dynamic-update-slice_fusion.10, bf16[960,1920]{1,0:T(8,128)(2,1)} %collective-permute-done.13), kind=kLoop, calls=%fused_computation.201 | loop fusion | bytes 7372800 | tf_op jit(solution)/shard_map/concatenate | solution.py:198
  223.2 4.1 %constant_dynamic-update-slice_fusion.14 = bf16[1920,1920]{1,0:T(8,128)(2,1)} fusion(bf16[1920,1920]{1,0:T(8,128)(2,1)} %constant_dynamic-update-slice_fusion.15, bf16[960,1920]{1,0:T(8,128)(2,1)} %collective-permute-done.18), kind=kLoop, calls=%fused_computation.206 | loop fusion | bytes 7372800 | tf_op jit(solution)/shard_map/concatenate | solution.py:198
  227.3 4.2 %constant_dynamic-slice_fusion.11 = (bf16[512,160]{1,0:T(8,128)(2,1)}, bf16[512,160]{1,0:T(8,128)(2,1)}, bf16[512,160]{1,0:T(8,128)(2,1)}, bf16[512,160]{1,0:T(8...) fusion(bf16[512,5120]{1,0:T(8,128)(2,1)} %all-gather.5.cloned.1, ...), kind=kLoop, calls=%fused_computation.233 | loop fusion | bytes 2621472 | tf_op jit(solution)/shard_map/dynamic_slice | solution.py:192
  231.5 6.3 %constant_dynamic-slice_fusion.12 = (bf16[512,320]{1,0:T(8,128)(2,1)S(1)}, bf16[512,320]{1,0:T(8,128)(2,1)S(1)}, bf16[512,320]{1,0:T(8,128)(2,1)S(1)}, bf16[512,...) fusion(bf16[512,5120]{1,0:T(8,128)(2,1)} %all-gather.5.cloned.1, ...), kind=kLoop, calls=%fused_computation.234 | loop fusion | bytes 6553640 | tf_op jit(solution)/shard_map/dynamic_slice | solution.py:192
  237.9 4.2 %concatenate.128 = bf16[512,1920]{1,0:T(8,128)(2,1)S(1)} concatenate(bf16[512,160]{1,0:T(8,128)(2,1)} %get-tuple-element.52, bf16[512,160]{1,0:T(8,128)(2,1)} %get-tuple-element.51, bf16[512,320]{1,0:T(8,128)(2,1)} %get-tuple-element.56, bf16[512,320]{1,0:T(8,128)(2,1)S(1)} %get-tuple-element.55, bf16[512,160]{1,0:T(8,128)(2,1)} %get-tuple-element.50, ...), dimensions={1} | concatenate | bytes 3932160 | tf_op jit(solution)/shard_map/concatenate | solution.py:197
  242.1 9.6 %fusion.155 = f32[512,1920]{1,0:T(8,128)} fusion(bf16[512,1920]{1,0:T(8,128)(2,1)S(1)} %concatenate.128, bf16[1920,1920]{1,0:T(8,128)(2,1)} %constant_dynamic-update-slice_fusion.14), kind=kOutput, calls=%fused_computation.306 | convolution fusion | flops 3774873600 | bytes 13271040 | tf_op jit(solution)/shard_map/dot_general | solution.py:196
  253.7 4.1 %concatenate.125 = bf16[512,2560]{1,0:T(8,128)(2,1)S(1)} concatenate(bf16[512,640]{1,0:T(8,128)(2,1)} %constant_dynamic-slice_fusion.27, bf16[512,320]{1,0:T(8,128)(2,1)} %get-tuple-element.62, bf16[512,320]{1,0:T(8,128)(2,1)} %get-tuple-element.61, bf16[512,320]{1,0:T(8,128)(2,1)} %get-tuple-element.60, bf16[512,320]{1,0:T(8,128)(2,1)} %get-tuple-element.59, ...), dimensions={1} | concatenate | bytes 5242880 | tf_op jit(solution)/shard_map/concatenate | solution.py:197
  257.9 8.5 %fusion.154 = f32[512,1920]{1,0:T(8,128)S(1)} fusion(bf16[512,2560]{1,0:T(8,128)(2,1)S(1)} %concatenate.125, bf16[2560,1920]{1,0:T(8,128)(2,1)} %constant_dynamic-update-slice_fusion.9), kind=kOutput, calls=%fused_computation.305 | convolution fusion | flops 5033164800 | bytes 16384000 | tf_op jit(solution)/shard_map/dot_general | solution.py:196
  266.4 4.5 %add_convert_fusion = bf16[512,1920]{1,0:T(8,128)(2,1)} fusion(f32[512,1920]{1,0:T(8,128)S(1)} %fusion.154, f32[512,1920]{1,0:T(8,128)S(1)} %copy-done.33, bf16[320,1920]{1,0:T(8,128)(2,1)} %collective-permute-done.21, bf16[160,1920]{1,0:T(8,128)(2,1)S(1)} %copy-done.23, bf16[160,1920]{1,0:T(8,128)(2,1)S(1)} %copy-done.21, ...), kind=kOutput, calls=%fused_computation.18 | convolution fusion | flops 1271234560 | bytes 12943360 | tf_op jit(solution)/shard_map/dot_general | solution.py:196
  296.5 21.6 %collective-permute-done.23 = bf16[512,3,128]{2,0,1:T(8,128)(2,1)} collective-permute-done((bf16[512,3,128]{2,0,1:T(8,128)(2,1)}, bf16[512,3,128]{2,0,1:T(8,128)(2,1)}, u32[]{:S(2)}, u32[]{:S(2)}) %collective-permute-start.23) | collective-permute-done | bytes 393248 | tf_op jit(solution)/shard_map/ppermute | solution.py:208
  322.7 13.0 %collective-permute-done.28 = bf16[512,3,128]{2,0,1:T(8,128)(2,1)S(1)} collective-permute-done((bf16[512,3,128]{2,0,1:T(8,128)(2,1)S(1)}, bf16[512,3,128]{2,0,1:T(8,128)(2,1)S(1)}, u32[]{:S(2)}, u32[]{:S(2)}) %collective-permute-start.28) | collective-permute-done | bytes 393248 | tf_op jit(solution)/shard_map/ppermute | solution.py:208
  337.1 35.3 %while.10 = (s32[]{:T(128)}, bf16[8,512,128]{2,1,0:T(8,128)(2,1)S(1)}, bf16[8,512,128]{2,1,0:T(8,128)(2,1)S(1)}, bf16[4096,128]{1,0:T(8,128)(2,1)S(1)}, bf16[4096,128]{1,0:T(8,128)(2,1)}, /*index=5*/s32[]{:T(128)}) while((s32[]{:T(128)}, bf16[8,512,128]{2,1,0:T(8,128)(2,1)S(1)}, bf16[8,512,128]{2,1,0:T(8,128)(2,1)S(1)}, ...), condition=%wide.region_5.6_spmd, body=%wide.region_2.5_spmd.sunk | while | flops 1090649600 | bytes 31733864 | solution.py:227
  378.3 7.5 %collective-permute-start.32 = (bf16[512,128]{1,0:T(8,128)(2,1)S(1)}, bf16[512,128]{1,0:T(8,128)(2,1)S(1)}, u32[]{:S(2)}, u32[]{:S(2)}) collective-permute-start(bf16[512,128]{1,0:T(8,128)(2,1)S(1)} %get-tuple-element.77), channel_id=1, source_target_pairs={{0,4},{1,5},{2,6},{3,7},{4,0},{8,12},{9,13},{10,14},{11,15},{12,8}... | collective-permute-start | bytes 393224 | tf_op jit(solution)/shard_map/ppermute | solution.py:231
  (300 shorter events, 179.4 us)
Async XLA Ops:
  6.5 70.9 %all-gather.3.cloned.1.call-start = ((), (), s32[]{:S(2)}) async-start(), calls=%async_computation | async-start | bytes 2580480 | tf_op jit(solution)/shard_map/all_gather | solution.py:157
  17.4 209.9 %all-gather.5.cloned.1.call-start = ((), (), s32[]{:S(2)}) async-start(), calls=%async_computation.1 | async-start | bytes 6553600 | tf_op jit(solution)/shard_map/all_gather | solution.py:180
  101.2 27.4 %collective-permute-start.12 = (bf16[320,1920]{1,0:T(8,128)(2,1)}, bf16[320,1920]{1,0:T(8,128)(2,1)S(1)}, u32[]{:S(2)}, u32[]{:S(2)}) collective-permute-start(bf16[320,1920]{1,0:T(8,128)(2,1)} %copy.53), channel_id=1, source_target_pairs={{0,1},{1,0},{2,3},{3,2},{4,5},{5,4},{6,7},{7,6},{8,9},{9,8},{10,11... | collective-permute-start | bytes 3686408 | tf_op jit(solution)/shard_map/ppermute | solution.py:86
  101.2 30.6 %collective-permute-start.10 = (bf16[320,1920]{1,0:T(8,128)(2,1)}, bf16[320,1920]{1,0:T(8,128)(2,1)S(1)}, u32[]{:S(2)}, u32[]{:S(2)}) collective-permute-start(bf16[320,1920]{1,0:T(8,128)(2,1)} %copy.53), channel_id=1, source_target_pairs={{0,2},{1,3},{2,4},{3,5},{4,6},{5,7},{6,0},{7,1},{8,10},{9,11},{10,... | collective-permute-start | bytes 3686408 | tf_op jit(solution)/shard_map/ppermute | solution.py:86
  102.7 29.2 %collective-permute-start.11 = (bf16[320,1920]{1,0:T(8,128)(2,1)}, bf16[320,1920]{1,0:T(8,128)(2,1)S(1)}, u32[]{:S(2)}, u32[]{:S(2)}) collective-permute-start(bf16[320,1920]{1,0:T(8,128)(2,1)} %copy.53), channel_id=1, source_target_pairs={{0,6},{1,7},{2,0},{3,1},{4,2},{5,3},{6,4},{7,5},{8,14},{9,15},{10,... | collective-permute-start | bytes 3686408 | tf_op jit(solution)/shard_map/ppermute | solution.py:86
  128.5 40.9 %collective-permute-start.16 = (bf16[320,1920]{1,0:T(8,128)(2,1)S(1)}, bf16[320,1920]{1,0:T(8,128)(2,1)S(1)}, u32[]{:S(2)}, u32[]{:S(2)}) collective-permute-start(bf16[320,1920]{1,0:T(8,128)(2,1)S(1)} %collective-permute-done.12), channel_id=1, source_target_pairs={{0,2},{1,3},{2,4},{3,5},{4,6},{5,7},{6,0},{7,1},{8,10},{9,11},{10,... | collective-permute-start | bytes 3686408 | tf_op jit(solution)/shard_map/ppermute | solution.py:86
  128.9 40.5 %collective-permute-start.17 = (bf16[320,1920]{1,0:T(8,128)(2,1)S(1)}, bf16[320,1920]{1,0:T(8,128)(2,1)S(1)}, u32[]{:S(2)}, u32[]{:S(2)}) collective-permute-start(bf16[320,1920]{1,0:T(8,128)(2,1)S(1)} %collective-permute-done.12), channel_id=1, source_target_pairs={{0,6},{1,7},{2,0},{3,1},{4,2},{5,3},{6,4},{7,5},{8,14},{9,15},{10,... | collective-permute-start | bytes 3686408 | tf_op jit(solution)/shard_map/ppermute | solution.py:86
  131.8 37.4 %collective-permute-start.14 = (bf16[160,1920]{1,0:T(8,128)(2,1)S(1)}, bf16[160,1920]{1,0:T(8,128)(2,1)S(1)}, u32[]{:S(2)}, u32[]{:S(2)}) collective-permute-start(bf16[160,1920]{1,0:T(8,128)(2,1)S(1)} %slice.381), channel_id=1, source_target_pairs={{0,2},{1,3},{2,4},{3,5},{4,6},{5,7},{6,0},{7,1},{8,10},{9,11},{10,... | collective-permute-start | bytes 1843208 | tf_op jit(solution)/shard_map/ppermute | solution.py:86
  132.0 37.5 %collective-permute-start.15 = (bf16[160,1920]{1,0:T(8,128)(2,1)S(1)}, bf16[160,1920]{1,0:T(8,128)(2,1)S(1)}, u32[]{:S(2)}, u32[]{:S(2)}) collective-permute-start(bf16[160,1920]{1,0:T(8,128)(2,1)S(1)} %slice.382), channel_id=1, source_target_pairs={{0,6},{1,7},{2,0},{3,1},{4,2},{5,3},{6,4},{7,5},{8,14},{9,15},{10,... | collective-permute-start | bytes 1843208 | tf_op jit(solution)/shard_map/ppermute | solution.py:86
  141.7 77.3 %collective-permute-start.13 = (bf16[960,1920]{1,0:T(8,128)(2,1)}, bf16[960,1920]{1,0:T(8,128)(2,1)}, u32[]{:S(2)}, u32[]{:S(2)}) collective-permute-start(bf16[960,1920]{1,0:T(8,128)(2,1)} %pad_maximum_fusion), channel_id=1, source_target_pairs={{0,32},{32,0},{64,96},{96,64},{1,33},{33,1},{65,97},{97,65},{2,34}... | collective-permute-start | bytes 11059208 | tf_op jit(solution)/shard_map/ppermute | solution.py:89
  176.5 46.7 %collective-permute-start.18 = (bf16[960,1920]{1,0:T(8,128)(2,1)}, bf16[960,1920]{1,0:T(8,128)(2,1)}, u32[]{:S(2)}, u32[]{:S(2)}) collective-permute-start(bf16[960,1920]{1,0:T(8,128)(2,1)} %pad_maximum_fusion.1), channel_id=1, source_target_pairs={{0,32},{32,0},{64,96},{96,64},{1,33},{33,1},{65,97},{97,65},{2,34}... | collective-permute-start | bytes 11059208 | tf_op jit(solution)/shard_map/ppermute | solution.py:89
  186.1 16.7 %collective-permute-start.19 = (bf16[160,1920]{1,0:T(8,128)(2,1)S(1)}, bf16[160,1920]{1,0:T(8,128)(2,1)S(1)}, u32[]{:S(2)}, u32[]{:S(2)}) collective-permute-start(bf16[160,1920]{1,0:T(8,128)(2,1)S(1)} %collective-permute-done.14), channel_id=1, source_target_pairs={{0,1},{1,0},{2,3},{3,2},{4,5},{5,4},{6,7},{7,6},{8,9},{9,8},{10,11... | collective-permute-start | bytes 1843208 | tf_op jit(solution)/shard_map/ppermute | solution.py:86
  187.7 27.7 %collective-permute-start.20 = (bf16[160,1920]{1,0:T(8,128)(2,1)S(1)}, bf16[160,1920]{1,0:T(8,128)(2,1)S(1)}, u32[]{:S(2)}, u32[]{:S(2)}) collective-permute-start(bf16[160,1920]{1,0:T(8,128)(2,1)S(1)} %copy-done.13), channel_id=1, source_target_pairs={{0,1},{1,0},{2,3},{3,2},{4,5},{5,4},{6,7},{7,6},{8,9},{9,8},{10,11... | collective-permute-start | bytes 1843208 | tf_op jit(solution)/shard_map/ppermute | solution.py:86
  216.6 49.7 %collective-permute-start.21 = (bf16[320,1920]{1,0:T(8,128)(2,1)}, bf16[320,1920]{1,0:T(8,128)(2,1)}, u32[]{:S(2)}, u32[]{:S(2)}) collective-permute-start(bf16[320,1920]{1,0:T(8,128)(2,1)} %pad_maximum_fusion.4), channel_id=1, source_target_pairs={{0,32},{32,0},{64,96},{96,64},{1,33},{33,1},{65,97},{97,65},{2,34}... | collective-permute-start | bytes 3686408 | tf_op jit(solution)/shard_map/ppermute | solution.py:89
  277.0 17.1 %collective-permute-start.22 = (bf16[512,3,128]{2,0,1:T(8,128)(2,1)}, bf16[512,3,128]{2,0,1:T(8,128)(2,1)}, u32[]{:S(2)}, u32[]{:S(2)}) collective-permute-start(bf16[512,3,128]{2,0,1:T(8,128)(2,1)} %bitcast.48), channel_id=1, source_target_pairs={{0,1},{1,2},{2,3},{3,4},{7,0},{8,9},{9,10},{10,11},{11,12},{15,8},... | collective-permute-start | bytes 1179656 | tf_op jit(solution)/shard_map/ppermute | solution.py:208
  283.6 34.5 %collective-permute-start.23 = (bf16[512,3,128]{2,0,1:T(8,128)(2,1)}, bf16[512,3,128]{2,0,1:T(8,128)(2,1)}, u32[]{:S(2)}, u32[]{:S(2)}) collective-permute-start(bf16[512,3,128]{2,0,1:T(8,128)(2,1)} %bitcast.50), channel_id=1, source_target_pairs={{0,2},{1,3},{2,4},{6,0},{7,1},{8,10},{9,11},{10,12},{14,8},{15,9},... | collective-permute-start | bytes 1179656 | tf_op jit(solution)/shard_map/ppermute | solution.py:208
  287.3 33.1 %collective-permute-start.24 = (bf16[512,3,128]{2,0,1:T(8,128)(2,1)}, bf16[512,3,128]{2,0,1:T(8,128)(2,1)}, u32[]{:S(2)}, u32[]{:S(2)}) collective-permute-start(bf16[512,3,128]{2,0,1:T(8,128)(2,1)} %bitcast.52), channel_id=1, source_target_pairs={{0,3},{1,4},{5,0},{6,1},{7,2},{8,11},{9,12},{13,8},{14,9},{15,10},... | collective-permute-start | bytes 1179656 | tf_op jit(solution)/shard_map/ppermute | solution.py:208
  290.2 31.3 %collective-permute-start.25 = (bf16[512,3,128]{2,0,1:T(8,128)(2,1)}, bf16[512,3,128]{2,0,1:T(8,128)(2,1)}, u32[]{:S(2)}, u32[]{:S(2)}) collective-permute-start(bf16[512,3,128]{2,0,1:T(8,128)(2,1)} %bitcast.54), channel_id=1, source_target_pairs={{0,4},{4,0},{5,1},{6,2},{7,3},{8,12},{12,8},{13,9},{14,10},{15,11}... | collective-permute-start | bytes 1179656 | tf_op jit(solution)/shard_map/ppermute | solution.py:208
  292.3 30.2 %collective-permute-start.26 = (bf16[512,3,128]{2,0,1:T(8,128)(2,1)S(1)}, bf16[512,3,128]{2,0,1:T(8,128)(2,1)S(1)}, u32[]{:S(2)}, u32[]{:S(2)}) collective-permute-start(bf16[512,3,128]{2,0,1:T(8,128)(2,1)S(1)} %bitcast.187), channel_id=1, source_target_pairs={{3,0},{4,1},{5,2},{6,3},{7,4},{11,8},{12,9},{13,10},{14,11},{15,12... | collective-permute-start | bytes 1179656 | tf_op jit(solution)/shard_map/ppermute | solution.py:208
  294.1 28.5 %collective-permute-start.27 = (bf16[512,3,128]{2,0,1:T(8,128)(2,1)S(1)}, bf16[512,3,128]{2,0,1:T(8,128)(2,1)S(1)}, u32[]{:S(2)}, u32[]{:S(2)}) collective-permute-start(bf16[512,3,128]{2,0,1:T(8,128)(2,1)S(1)} %bitcast.186), channel_id=1, source_target_pairs={{2,0},{3,1},{4,2},{5,3},{6,4},{10,8},{11,9},{12,10},{13,11},{14,12... | collective-permute-start | bytes 1179656 | tf_op jit(solution)/shard_map/ppermute | solution.py:208
  318.1 17.7 %collective-permute-start.28 = (bf16[512,3,128]{2,0,1:T(8,128)(2,1)S(1)}, bf16[512,3,128]{2,0,1:T(8,128)(2,1)S(1)}, u32[]{:S(2)}, u32[]{:S(2)}) collective-permute-start(bf16[512,3,128]{2,0,1:T(8,128)(2,1)S(1)} %bitcast.185), channel_id=1, source_target_pairs={{1,0},{2,1},{3,2},{4,3},{5,4},{9,8},{10,9},{11,10},{12,11},{13,12}... | collective-permute-start | bytes 1179656 | tf_op jit(solution)/shard_map/ppermute | solution.py:208
  374.5 14.9 %collective-permute-start.30 = (bf16[512,128]{1,0:T(8,128)(2,1)S(1)}, bf16[512,128]{1,0:T(8,128)(2,1)S(1)}, u32[]{:S(2)}, u32[]{:S(2)}) collective-permute-start(bf16[512,128]{1,0:T(8,128)(2,1)S(1)} %get-tuple-element.79), channel_id=1, source_target_pairs={{0,6},{1,7},{2,0},{3,1},{4,2},{8,14},{9,15},{10,8},{11,9},{12,10},... | collective-permute-start | bytes 393224 | tf_op jit(solution)/shard_map/ppermute | solution.py:231
  376.4 16.1 %collective-permute-start.31 = (bf16[512,128]{1,0:T(8,128)(2,1)S(1)}, bf16[512,128]{1,0:T(8,128)(2,1)S(1)}, u32[]{:S(2)}, u32[]{:S(2)}) collective-permute-start(bf16[512,128]{1,0:T(8,128)(2,1)S(1)} %get-tuple-element.78), channel_id=1, source_target_pairs={{0,5},{1,6},{2,7},{3,0},{4,1},{8,13},{9,14},{10,15},{11,8},{12,9},... | collective-permute-start | bytes 393224 | tf_op jit(solution)/shard_map/ppermute | solution.py:231
  378.3 15.5 %collective-permute-start.32 = (bf16[512,128]{1,0:T(8,128)(2,1)S(1)}, bf16[512,128]{1,0:T(8,128)(2,1)S(1)}, u32[]{:S(2)}, u32[]{:S(2)}) collective-permute-start(bf16[512,128]{1,0:T(8,128)(2,1)S(1)} %get-tuple-element.77), channel_id=1, source_target_pairs={{0,4},{1,5},{2,6},{3,7},{4,0},{8,12},{9,13},{10,14},{11,15},{12,8}... | collective-permute-start | bytes 393224 | tf_op jit(solution)/shard_map/ppermute | solution.py:231
  (55 other events, 450.3 us)
Sparse Core Ops, SparseCore 0:
  17.5 59.8 all-gather.2
  93.1 55.8 all-gather.4

commit v2 on v1

--- a/solution.py
+++ b/solution.py
@@ -201,17 +201,11 @@
         qkv = part if qkv is None else qkv + part
     qkv = qkv.astype(jnp.bfloat16).reshape(group_rows, heads_here, 3, HDIM)
     active = min(heads_here, n_ctx)
-    received = [lax.dynamic_index_in_dim(qkv, jnp.minimum(c_idx, active - 1), 1, keepdims=False)]
-    for s in range(1, n_ctx):
-        target = jnp.minimum((c_idx + s) % n_ctx, active - 1)
-        received.append(
-            lax.ppermute(
-                lax.dynamic_index_in_dim(qkv, target, 1, keepdims=False),
-                "ctx",
-                [(b, (b + s) % n_ctx) for b in range(n_ctx) if (b + s) % n_ctx < active],
-            )
-        )
-    triple = jnp.stack(received)
+    spare = n_ctx - active
+    outgoing = jnp.concatenate(
+        [qkv.transpose(1, 0, 2, 3), jnp.zeros((spare,) + qkv.shape[:1] + qkv.shape[2:], qkv.dtype)], 0
+    )
+    triple = lax.all_to_all(outgoing, "ctx", 0, 0, tiled=True)
     keys = triple[:, :, 1].reshape(-1, HDIM)
     values = triple[:, :, 2].reshape(-1, HDIM)
     inv_root = 1.0 / jnp.sqrt(jnp.float32(HDIM))
@@ -225,12 +219,7 @@
         return (accum / denom[:, None]).astype(jnp.bfloat16)
 
     attended = lax.map(one_block, triple[:, :, 0])
-    returned = [attended[0]]
-    for s in range(1, n_ctx):
-        returned.append(
-            lax.ppermute(attended[s], "ctx", [(d, (d - s) % n_ctx) for d in range(active)])
-        )
-    by_head = jnp.take(jnp.stack(returned), (jnp.arange(heads_here) - c_idx) % n_ctx, axis=0)
+    by_head = lax.all_to_all(attended, "ctx", 0, 0, tiled=True)[:heads_here]
     return by_head.transpose(1, 0, 2).reshape(group_rows, heads_here * HDIM)
 
 

time: 411 us -> 405 us (0.985)
  starting transfers between devices: 67.8 us -> 40.5 us
  blocking collectives: 0 us -> 19.3 us
  matrix products: 59 us -> 66.3 us
    ppermute x14 -> x0, waiting for transfers between devices: 39.6 us -> none  [the longest x7 34.7 us: shards(): lax.ppermute(lax.dynamic_index_in_dim(qkv, target, 1, keepdims=False), 'c...]
    all_to_all x0 -> x1, waiting for transfers between devices: none -> 38.9 us  [shards(): triple = lax.all_to_all(outgoing, 'ctx', 0, 0, tiled=True)]
    ppermute x14 -> x0, starting transfers between devices: 32.9 us -> none  [the longest x7 19 us: shards(): lax.ppermute(attended[s], 'ctx', [(d, (d - s) % n_ctx) for d in range(act...]
    all_to_all x0 -> x1, blocking collectives: none -> 19.3 us  [shards(): by_head = lax.all_to_all(attended, 'ctx', 0, 0, tiled=True)[:heads_here]]
    dynamic_slice x9 -> x0, local copies, waits for them, and re-layouts: 8.93 us -> none  [the longest x8 7.72 us: shards(): lax.dynamic_index_in_dim(qkv, target, 1, keepdims=False)]
    dot_general x8, matrix products: 10.7 us -> 18.2 us  [one_block(): jnp.dot(query, keys.T, preferred_element_type=jnp.float32) * inv_root]
    dynamic_update_slice x0 -> x16, local copies, waits for them, and re-layouts: none -> 6.27 us  [shards(): attended = lax.map(one_block, triple[:, :, 0])]
    all_to_all x0 -> x1, starting transfers between devices: none -> 5.75 us  [shards(): triple = lax.all_to_all(outgoing, 'ctx', 0, 0, tiled=True)]
  transfers between devices with their start and end apart: 38 -> 25, of which waited for: 16 -> 12; matrix products, arithmetic and copies ran while one was open for 30% -> 28% of each run, Pallas kernels for 0% -> 0%
where the time goes in v2:
time: 405 us; the launch traced here: 400 us
  waiting for transfers between devices  141 us (35%)
  local copies, waits for them, and re-layouts  82.5 us (20%)
  matrix products  66.3 us (16%)
  starting transfers between devices  40.5 us (10%)
  other arithmetic  35.7 us (9%)
  blocking collectives  19.3 us (5%)
  between operations  15.2 us (4%)
    ppermute x9, waiting for transfers between devices, send(): return lax.ppermute(cells, 'ctx', [(i, step(i)) for i in range(n_ctx)])  76.1 us
    all_to_all x1, waiting for transfers between devices, shards(): triple = lax.all_to_all(outgoing, 'ctx', 0, 0, tiled=True)  38.9 us
    dot_general x3, matrix products, shards(): jnp.dot(jnp.concatenate(columns, 1), jnp.concatenate(weights, 0), preferr...  22.6 us
    all_to_all x1, blocking collectives, shards(): by_head = lax.all_to_all(attended, 'ctx', 0, 0, tiled=True)[:heads_here]  19.3 us
    dot_general x8, matrix products, one_block(): jnp.dot(query, keys.T, preferred_element_type=jnp.float32) * inv_root  18.2 us
    unnamed x74, local copies, waits for them, and re-layouts  17.8 us
    concatenate x3, other arithmetic, shards(): jnp.concatenate([cells for cells, _, _ in s], 0)  14.7 us
    all_gather x1, waiting for transfers between devices, shards(): lax.all_gather(jnp.concatenate([patch_weight, share_parts], 0), 'ctx', ax...  14.3 us
  transfers between devices with their start and end apart: 25, of which 12 were waited for; matrix products, arithmetic and copies ran while one was open for 28% of the time, Pallas kernels for 0%

profile of v2, /device:TPU:0, one launch (start us, length us, event | category | flops | bytes accessed | tf_op | source)
XLA Modules:
  0.0 400.5 jit_solution(8599806529541993874)
XLA Ops:
  10.0 4.1 %collective-permute-start = (bf16[6,1,32,96]{3,2,1,0:T(8,128)(2,1)}, bf16[6,1,32,96]{3,2,1,0:T(8,128)(2,1)}, u32[]{:S(2)}, u32[]{:S(2)}) collective-permute-start(bf16[6,1,32,96]{3,2,1,0:T(8,128)(2,1)} %get-tuple-element.109), channel_id=1, source_target_pairs={{0,8},{8,16},{16,24},{1,9},{9,17},{17,25},{2,10},{10,18},{18,26},{... | collective-permute-start | bytes 110600 | tf_op jit(solution)/shard_map/ppermute | solution.py:19
  22.5 3.5 collective-permute-start.2
  63.0 14.3 %all-gather.3.cloned.1.call-done = bf16[774,1280]{0,1:T(8,128)(2,1)} async-done(((bf16[774,160]{0,1:T(8,128)(2,1)}), bf16[774,1280]{0,1:T(8,128)(2,1)}) %all-gather.3.cloned.1.call-update) | async-done | bytes 1981456 | tf_op jit(solution)/shard_map/all_gather | solution.py:157
  92.9 3.9 copy.42
  104.3 24.1 %collective-permute-done.12 = bf16[320,1920]{1,0:T(8,128)(2,1)S(1)} collective-permute-done((bf16[320,1920]{1,0:T(8,128)(2,1)}, bf16[320,1920]{1,0:T(8,128)(2,1)S(1)}, u32[]{:S(2)}, u32[]{:S(2)}) %collective-permute-start.12) | collective-permute-done | bytes 1228832 | tf_op jit(solution)/shard_map/ppermute | solution.py:86
  135.2 6.4 %pad_maximum_fusion = bf16[960,1920]{1,0:T(8,128)(2,1)} fusion(bf16[320,1920]{1,0:T(8,128)(2,1)S(1)} %collective-permute-done.12, bf16[320,1920]{1,0:T(8,128)(2,1)S(1)} %collective-permute-done.11, bf16[320,1920]{1,0:T(8,128)(2,1)S(1)} %collective-permute-done.10), kind=kLoop, calls=%fused_computation.34 | loop fusion | flops 11059200 | bytes 7372800 | tf_op jit(solution)/shard_map/concatenate | solution.py:114
  141.7 27.5 %collective-permute-done.14 = bf16[160,1920]{1,0:T(8,128)(2,1)S(1)} collective-permute-done((bf16[160,1920]{1,0:T(8,128)(2,1)S(1)}, bf16[160,1920]{1,0:T(8,128)(2,1)S(1)}, u32[]{:S(2)}, u32[]{:S(2)}) %collective-permute-start.14) | collective-permute-done | bytes 614432 | tf_op jit(solution)/shard_map/ppermute | solution.py:86
  169.3 7.1 %pad_maximum_fusion.1 = bf16[960,1920]{1,0:T(8,128)(2,1)} fusion(bf16[320,1920]{1,0:T(8,128)(2,1)S(1)} %collective-permute-done.17, bf16[320,1920]{1,0:T(8,128)(2,1)S(1)} %collective-permute-done.16, bf16[160,1920]{1,0:T(8,128)(2,1)S(1)} %collective-permute-done.15, bf16[160,1920]{1,0:T(8,128)(2,1)S(1)} %collective-permute-done.14), kind=kLoop, calls=%fused_computation.35 | loop fusion | flops 14745600 | bytes 7372800 | tf_op jit(solution)/shard_map/concatenate | solution.py:114
  179.6 3.4 constant_dynamic-update-slice_fusion.14
  190.8 11.8 %collective-permute-done.19 = bf16[160,1920]{1,0:T(8,128)(2,1)S(1)} collective-permute-done((bf16[160,1920]{1,0:T(8,128)(2,1)S(1)}, bf16[160,1920]{1,0:T(8,128)(2,1)S(1)}, u32[]{:S(2)}, u32[]{:S(2)}) %collective-permute-start.19) | collective-permute-done | bytes 614432 | tf_op jit(solution)/shard_map/ppermute | solution.py:86
  202.6 12.6 %collective-permute-done.20 = bf16[160,1920]{1,0:T(8,128)(2,1)S(1)} collective-permute-done((bf16[160,1920]{1,0:T(8,128)(2,1)S(1)}, bf16[160,1920]{1,0:T(8,128)(2,1)S(1)}, u32[]{:S(2)}, u32[]{:S(2)}) %collective-permute-start.20) | collective-permute-done | bytes 614432 | tf_op jit(solution)/shard_map/ppermute | solution.py:86
  218.7 4.2 %constant_dynamic-update-slice_fusion.10 = bf16[2560,1920]{1,0:T(8,128)(2,1)} fusion(bf16[2560,1920]{1,0:T(8,128)(2,1)} %constant_dynamic-update-slice_fusion.11, bf16[960,1920]{1,0:T(8,128)(2,1)} %collective-permute-done.13), kind=kLoop, calls=%fused_computation.177 | loop fusion | bytes 7372800 | tf_op jit(solution)/shard_map/concatenate | solution.py:198
  223.0 4.1 %constant_dynamic-update-slice_fusion.15 = bf16[1920,1920]{1,0:T(8,128)(2,1)} fusion(bf16[1920,1920]{1,0:T(8,128)(2,1)} %constant_dynamic-update-slice_fusion.16, bf16[960,1920]{1,0:T(8,128)(2,1)} %collective-permute-done.18), kind=kLoop, calls=%fused_computation.182 | loop fusion | bytes 7372800 | tf_op jit(solution)/shard_map/concatenate | solution.py:198
  227.1 4.3 %constant_dynamic-slice_fusion.3 = (bf16[512,160]{1,0:T(8,128)(2,1)}, bf16[512,160]{1,0:T(8,128)(2,1)}, bf16[512,160]{1,0:T(8,128)(2,1)}, bf16[512,160]{1,0:T(8,...) fusion(bf16[512,5120]{1,0:T(8,128)(2,1)} %all-gather.5.cloned.1, ...), kind=kLoop, calls=%fused_computation.200 | loop fusion | bytes 2621472 | tf_op jit(solution)/shard_map/dynamic_slice | solution.py:192
  231.3 6.5 %constant_dynamic-slice_fusion.4 = (bf16[512,320]{1,0:T(8,128)(2,1)S(1)}, bf16[512,320]{1,0:T(8,128)(2,1)S(1)}, bf16[512,320]{1,0:T(8,128)(2,1)S(1)}, bf16[512,3...) fusion(bf16[512,5120]{1,0:T(8,128)(2,1)} %all-gather.5.cloned.1, ...), kind=kLoop, calls=%fused_computation.201 | loop fusion | bytes 6553640 | tf_op jit(solution)/shard_map/dynamic_slice | solution.py:192
  237.8 4.2 %concatenate.131 = bf16[512,1920]{1,0:T(8,128)(2,1)S(1)} concatenate(bf16[512,160]{1,0:T(8,128)(2,1)} %get-tuple-element.67, bf16[512,160]{1,0:T(8,128)(2,1)} %get-tuple-element.66, bf16[512,320]{1,0:T(8,128)(2,1)} %get-tuple-element.71, bf16[512,320]{1,0:T(8,128)(2,1)S(1)} %get-tuple-element.70, bf16[512,160]{1,0:T(8,128)(2,1)} %get-tuple-element.65, ...), dimensions={1} | concatenate | bytes 3932160 | tf_op jit(solution)/shard_map/concatenate | solution.py:197
  242.1 9.5 %fusion.149 = f32[512,1920]{1,0:T(8,128)} fusion(bf16[512,1920]{1,0:T(8,128)(2,1)S(1)} %concatenate.131, bf16[1920,1920]{1,0:T(8,128)(2,1)} %constant_dynamic-update-slice_fusion.15), kind=kOutput, calls=%fused_computation.260 | convolution fusion | flops 3774873600 | bytes 13271040 | tf_op jit(solution)/shard_map/dot_general | solution.py:196
  253.6 4.1 %concatenate.128 = bf16[512,2560]{1,0:T(8,128)(2,1)S(1)} concatenate(bf16[512,640]{1,0:T(8,128)(2,1)} %constant_dynamic-slice_fusion.19, bf16[512,320]{1,0:T(8,128)(2,1)} %get-tuple-element.77, bf16[512,320]{1,0:T(8,128)(2,1)} %get-tuple-element.76, bf16[512,320]{1,0:T(8,128)(2,1)} %get-tuple-element.75, bf16[512,320]{1,0:T(8,128)(2,1)} %get-tuple-element.74, ...), dimensions={1} | concatenate | bytes 5242880 | tf_op jit(solution)/shard_map/concatenate | solution.py:197
  257.8 8.5 %fusion.148 = f32[512,1920]{1,0:T(8,128)S(1)} fusion(bf16[512,2560]{1,0:T(8,128)(2,1)S(1)} %concatenate.128, bf16[2560,1920]{1,0:T(8,128)(2,1)} %constant_dynamic-update-slice_fusion.10), kind=kOutput, calls=%fused_computation.259 | convolution fusion | flops 5033164800 | bytes 16384000 | tf_op jit(solution)/shard_map/dot_general | solution.py:196
  266.4 4.6 %add_convert_fusion = bf16[512,1920]{1,0:T(8,128)(2,1)} fusion(f32[512,1920]{1,0:T(8,128)S(1)} %fusion.148, f32[512,1920]{1,0:T(8,128)S(1)} %copy-done.30, bf16[320,1920]{1,0:T(8,128)(2,1)} %collective-permute-done.21, bf16[160,1920]{1,0:T(8,128)(2,1)S(1)} %copy-done.20, bf16[160,1920]{1,0:T(8,128)(2,1)S(1)} %copy-done.18, ...), kind=kOutput, calls=%fused_computation.17 | convolution fusion | flops 1271234560 | bytes 12943360 | tf_op jit(solution)/shard_map/dot_general | solution.py:196
  275.5 5.8 %all-to-all-start = ((bf16[8,512,3,128]{1,3,2,0:T(8,128)(2,1)}), bf16[8,512,3,128]{1,3,2,0:T(8,128)(2,1)S(1)}, u32[]{:S(2)}, u32[]{:S(2)}) async-start(bf16[8,512,3,128]{1,3,2,0:T(8,128)(2,1)} %concatenate.137), calls=%async_computation | async-start | bytes 6291456 | tf_op jit(solution)/shard_map/all_to_all | solution.py:208
  281.3 38.9 %all-to-all-done = bf16[8,512,3,128]{1,3,2,0:T(8,128)(2,1)S(1)} async-done(((bf16[8,512,3,128]{1,3,2,0:T(8,128)(2,1)}), bf16[8,512,3,128]{1,3,2,0:T(8,128)(2,1)S(1)}, u32[]{:S(2)}, u32[]{:S(2)}) %all-to-all-start) | async-done | bytes 3145760 | tf_op jit(solution)/shard_map/all_to_all | solution.py:208
  324.3 48.6 %while.10 = (s32[]{:T(128)}, bf16[8,512,128]{1,2,0:T(8,128)(2,1)}, bf16[8,512,128]{1,2,0:T(8,128)(2,1)}, bf16[4096,128]{1,0:T(8,128)(2,1)S(1)}, bf16[4096,128]{1,0:T(8,128)(2,1)S(1)}, /*index=5*/s32[]{:T(128)}) while((s32[]{:T(128)}, bf16[8,512,128]{1,2,0:T(8,128)(2,1)}, bf16[8,512,128]{1,2,0:T(8,128)(2,1)}, bf16[4096,128]{1,0:T(8,128)(2,1)S(1)}, ...), condition=%wide.region_5.6_spmd, body=%wide.region_2.5_spmd.sunk | while | flops 1090649600 | bytes 28064836 | solution.py:221
  373.0 19.3 %all_to_all.10 = bf16[8,512,128]{1,2,0:T(8,128)(2,1)S(1)} all-to-all(bf16[8,512,128]{1,2,0:T(8,128)(2,1)} %get-tuple-element.32), channel_id=1, replica_groups=mesh['dp'=4,'head'=4,'ctx'=8] {'ctx'}, dimensions={0} | all-to-all | bytes 2097152 | tf_op jit(solution)/shard_map/all_to_all | solution.py:222
  (244 shorter events, 152.6 us)
Async XLA Ops:
  6.5 70.8 %all-gather.3.cloned.1.call-start = ((), (), s32[]{:S(2)}) async-start(), calls=%async_computation.2 | async-start | bytes 2580480 | tf_op jit(solution)/shard_map/all_gather | solution.py:157
  10.0 10.3 %collective-permute-start = (bf16[6,1,32,96]{3,2,1,0:T(8,128)(2,1)}, bf16[6,1,32,96]{3,2,1,0:T(8,128)(2,1)}, u32[]{:S(2)}, u32[]{:S(2)}) collective-permute-start(bf16[6,1,32,96]{3,2,1,0:T(8,128)(2,1)} %get-tuple-element.109), channel_id=1, source_target_pairs={{0,8},{8,16},{16,24},{1,9},{9,17},{17,25},{2,10},{10,18},{18,26},{... | collective-permute-start | bytes 110600 | tf_op jit(solution)/shard_map/ppermute | solution.py:19
  14.1 7.5 %collective-permute-start.1 = (bf16[6,1,32,96]{3,2,1,0:T(8,128)(2,1)S(1)}, bf16[6,1,32,96]{3,2,1,0:T(8,128)(2,1)}, u32[]{:S(2)}, u32[]{:S(2)}) collective-permute-start(bf16[6,1,32,96]{3,2,1,0:T(8,128)(2,1)S(1)} %get-tuple-element.108), channel_id=1, source_target_pairs={{8,0},{16,8},{24,16},{9,1},{17,9},{25,17},{10,2},{18,10},{26,18},{... | collective-permute-start | bytes 110600 | tf_op jit(solution)/shard_map/ppermute | solution.py:21
  17.4 209.7 %all-gather.5.cloned.1.call-start = ((), (), s32[]{:S(2)}) async-start(), calls=%async_computation.3 | async-start | bytes 6553600 | tf_op jit(solution)/shard_map/all_gather | solution.py:180
  22.5 5.8 %collective-permute-start.2 = (bf16[6,18,1,96]{3,2,1,0:T(2,128)(2,1)S(1)}, bf16[6,18,1,96]{3,2,1,0:T(2,128)(2,1)S(1)}, u32[]{:S(2)}, u32[]{:S(2)}) collective-permute-start(bf16[6,18,1,96]{3,2,1,0:T(2,128)(2,1)S(1)} %get-tuple-element.97), channel_id=1, source_target_pairs={{0,1},{1,2},{2,3},{3,4},{4,5},{5,6},{6,7},{8,9},{9,10},{10,11},{11... | collective-permute-start | bytes 62216 | tf_op jit(solution)/shard_map/ppermute | solution.py:19
  26.0 7.0 %collective-permute-start.3 = (bf16[6,18,1,96]{3,2,1,0:T(2,128)(2,1)S(1)}, bf16[6,18,1,96]{3,2,1,0:T(2,128)(2,1)S(1)}, u32[]{:S(2)}, u32[]{:S(2)}) collective-permute-start(bf16[6,18,1,96]{3,2,1,0:T(2,128)(2,1)S(1)} %get-tuple-element.98), channel_id=1, source_target_pairs={{1,0},{2,1},{3,2},{4,3},{5,4},{6,5},{7,6},{9,8},{10,9},{11,10},{12... | collective-permute-start | bytes 62216 | tf_op jit(solution)/shard_map/ppermute | solution.py:21
  48.6 9.7 %collective-permute-start.4 = (bf16[128,768]{1,0:T(8,128)(2,1)S(1)}, bf16[128,768]{1,0:T(8,128)(2,1)S(1)}, u32[]{:S(2)}, u32[]{:S(2)}) collective-permute-start(bf16[128,768]{1,0:T(8,128)(2,1)S(1)} %reshape.127), channel_id=1, source_target_pairs={{0,8},{8,16},{16,24},{24,0},{1,9},{9,17},{17,25},{25,1},{2,10},{10... | collective-permute-start | bytes 589832 | tf_op jit(solution)/shard_map/ppermute | solution.py:32
  51.3 9.8 %collective-permute-start.5 = (bf16[128,768]{1,0:T(8,128)(2,1)S(1)}, bf16[128,768]{1,0:T(8,128)(2,1)S(1)}, u32[]{:S(2)}, u32[]{:S(2)}) collective-permute-start(bf16[128,768]{1,0:T(8,128)(2,1)S(1)} %reshape.127), channel_id=1, source_target_pairs={{0,16},{8,24},{16,0},{24,8},{1,17},{9,25},{17,1},{25,9},{2,18},{10... | collective-permute-start | bytes 589832 | tf_op jit(solution)/shard_map/ppermute | solution.py:32
  54.1 7.0 %collective-permute-start.6 = (bf16[128,768]{1,0:T(8,128)(2,1)S(1)}, bf16[128,768]{1,0:T(8,128)(2,1)S(1)}, u32[]{:S(2)}, u32[]{:S(2)}) collective-permute-start(bf16[128,768]{1,0:T(8,128)(2,1)S(1)} %reshape.127), channel_id=1, source_target_pairs={{0,24},{8,0},{16,8},{24,16},{1,25},{9,1},{17,9},{25,17},{2,26},{10... | collective-permute-start | bytes 589832 | tf_op jit(solution)/shard_map/ppermute | solution.py:32
  81.9 6.0 %collective-permute-start.7 = (f32[3072]{0:T(1024)S(1)}, f32[3072]{0:T(1024)S(1)}, u32[]{:S(2)}, u32[]{:S(2)}) collective-permute-start(f32[3072]{0:T(1024)S(1)} %pad_maximum_fusion.8), channel_id=1, source_target_pairs={{0,8},{8,16},{16,24},{24,0},{1,9},{9,17},{17,25},{25,1},{2,10},{10... | collective-permute-start | bytes 36872 | tf_op jit(solution)/shard_map/ppermute | solution.py:32
  84.0 5.2 %collective-permute-start.8 = (f32[3072]{0:T(1024)S(1)}, f32[3072]{0:T(1024)S(1)}, u32[]{:S(2)}, u32[]{:S(2)}) collective-permute-start(f32[3072]{0:T(1024)S(1)} %pad_maximum_fusion.8), channel_id=1, source_target_pairs={{0,16},{8,24},{16,0},{24,8},{1,17},{9,25},{17,1},{25,9},{2,18},{10... | collective-permute-start | bytes 36872 | tf_op jit(solution)/shard_map/ppermute | solution.py:32
  101.1 27.4 %collective-permute-start.12 = (bf16[320,1920]{1,0:T(8,128)(2,1)}, bf16[320,1920]{1,0:T(8,128)(2,1)S(1)}, u32[]{:S(2)}, u32[]{:S(2)}) collective-permute-start(bf16[320,1920]{1,0:T(8,128)(2,1)} %copy.43), channel_id=1, source_target_pairs={{0,1},{1,0},{2,3},{3,2},{4,5},{5,4},{6,7},{7,6},{8,9},{9,8},{10,11... | collective-permute-start | bytes 3686408 | tf_op jit(solution)/shard_map/ppermute | solution.py:86
  101.1 30.6 %collective-permute-start.10 = (bf16[320,1920]{1,0:T(8,128)(2,1)}, bf16[320,1920]{1,0:T(8,128)(2,1)S(1)}, u32[]{:S(2)}, u32[]{:S(2)}) collective-permute-start(bf16[320,1920]{1,0:T(8,128)(2,1)} %copy.43), channel_id=1, source_target_pairs={{0,2},{1,3},{2,4},{3,5},{4,6},{5,7},{6,0},{7,1},{8,10},{9,11},{10,... | collective-permute-start | bytes 3686408 | tf_op jit(solution)/shard_map/ppermute | solution.py:86
  102.6 29.3 %collective-permute-start.11 = (bf16[320,1920]{1,0:T(8,128)(2,1)}, bf16[320,1920]{1,0:T(8,128)(2,1)S(1)}, u32[]{:S(2)}, u32[]{:S(2)}) collective-permute-start(bf16[320,1920]{1,0:T(8,128)(2,1)} %copy.43), channel_id=1, source_target_pairs={{0,6},{1,7},{2,0},{3,1},{4,2},{5,3},{6,4},{7,5},{8,14},{9,15},{10,... | collective-permute-start | bytes 3686408 | tf_op jit(solution)/shard_map/ppermute | solution.py:86
  128.5 40.8 %collective-permute-start.16 = (bf16[320,1920]{1,0:T(8,128)(2,1)S(1)}, bf16[320,1920]{1,0:T(8,128)(2,1)S(1)}, u32[]{:S(2)}, u32[]{:S(2)}) collective-permute-start(bf16[320,1920]{1,0:T(8,128)(2,1)S(1)} %collective-permute-done.12), channel_id=1, source_target_pairs={{0,2},{1,3},{2,4},{3,5},{4,6},{5,7},{6,0},{7,1},{8,10},{9,11},{10,... | collective-permute-start | bytes 3686408 | tf_op jit(solution)/shard_map/ppermute | solution.py:86
  128.8 40.5 %collective-permute-start.17 = (bf16[320,1920]{1,0:T(8,128)(2,1)S(1)}, bf16[320,1920]{1,0:T(8,128)(2,1)S(1)}, u32[]{:S(2)}, u32[]{:S(2)}) collective-permute-start(bf16[320,1920]{1,0:T(8,128)(2,1)S(1)} %collective-permute-done.12), channel_id=1, source_target_pairs={{0,6},{1,7},{2,0},{3,1},{4,2},{5,3},{6,4},{7,5},{8,14},{9,15},{10,... | collective-permute-start | bytes 3686408 | tf_op jit(solution)/shard_map/ppermute | solution.py:86
  131.7 37.4 %collective-permute-start.14 = (bf16[160,1920]{1,0:T(8,128)(2,1)S(1)}, bf16[160,1920]{1,0:T(8,128)(2,1)S(1)}, u32[]{:S(2)}, u32[]{:S(2)}) collective-permute-start(bf16[160,1920]{1,0:T(8,128)(2,1)S(1)} %slice.351), channel_id=1, source_target_pairs={{0,2},{1,3},{2,4},{3,5},{4,6},{5,7},{6,0},{7,1},{8,10},{9,11},{10,... | collective-permute-start | bytes 1843208 | tf_op jit(solution)/shard_map/ppermute | solution.py:86
  131.9 37.4 %collective-permute-start.15 = (bf16[160,1920]{1,0:T(8,128)(2,1)S(1)}, bf16[160,1920]{1,0:T(8,128)(2,1)S(1)}, u32[]{:S(2)}, u32[]{:S(2)}) collective-permute-start(bf16[160,1920]{1,0:T(8,128)(2,1)S(1)} %slice.352), channel_id=1, source_target_pairs={{0,6},{1,7},{2,0},{3,1},{4,2},{5,3},{6,4},{7,5},{8,14},{9,15},{10,... | collective-permute-start | bytes 1843208 | tf_op jit(solution)/shard_map/ppermute | solution.py:86
  141.6 77.2 %collective-permute-start.13 = (bf16[960,1920]{1,0:T(8,128)(2,1)}, bf16[960,1920]{1,0:T(8,128)(2,1)}, u32[]{:S(2)}, u32[]{:S(2)}) collective-permute-start(bf16[960,1920]{1,0:T(8,128)(2,1)} %pad_maximum_fusion), channel_id=1, source_target_pairs={{0,32},{32,0},{64,96},{96,64},{1,33},{33,1},{65,97},{97,65},{2,34}... | collective-permute-start | bytes 11059208 | tf_op jit(solution)/shard_map/ppermute | solution.py:89
  176.4 46.6 %collective-permute-start.18 = (bf16[960,1920]{1,0:T(8,128)(2,1)}, bf16[960,1920]{1,0:T(8,128)(2,1)}, u32[]{:S(2)}, u32[]{:S(2)}) collective-permute-start(bf16[960,1920]{1,0:T(8,128)(2,1)} %pad_maximum_fusion.1), channel_id=1, source_target_pairs={{0,32},{32,0},{64,96},{96,64},{1,33},{33,1},{65,97},{97,65},{2,34}... | collective-permute-start | bytes 11059208 | tf_op jit(solution)/shard_map/ppermute | solution.py:89
  185.9 16.7 %collective-permute-start.19 = (bf16[160,1920]{1,0:T(8,128)(2,1)S(1)}, bf16[160,1920]{1,0:T(8,128)(2,1)S(1)}, u32[]{:S(2)}, u32[]{:S(2)}) collective-permute-start(bf16[160,1920]{1,0:T(8,128)(2,1)S(1)} %collective-permute-done.14), channel_id=1, source_target_pairs={{0,1},{1,0},{2,3},{3,2},{4,5},{5,4},{6,7},{7,6},{8,9},{9,8},{10,11... | collective-permute-start | bytes 1843208 | tf_op jit(solution)/shard_map/ppermute | solution.py:86
  187.6 27.6 %collective-permute-start.20 = (bf16[160,1920]{1,0:T(8,128)(2,1)S(1)}, bf16[160,1920]{1,0:T(8,128)(2,1)S(1)}, u32[]{:S(2)}, u32[]{:S(2)}) collective-permute-start(bf16[160,1920]{1,0:T(8,128)(2,1)S(1)} %copy-done.14), channel_id=1, source_target_pairs={{0,1},{1,0},{2,3},{3,2},{4,5},{5,4},{6,7},{7,6},{8,9},{9,8},{10,11... | collective-permute-start | bytes 1843208 | tf_op jit(solution)/shard_map/ppermute | solution.py:86
  216.4 49.9 %collective-permute-start.21 = (bf16[320,1920]{1,0:T(8,128)(2,1)}, bf16[320,1920]{1,0:T(8,128)(2,1)}, u32[]{:S(2)}, u32[]{:S(2)}) collective-permute-start(bf16[320,1920]{1,0:T(8,128)(2,1)} %pad_maximum_fusion.4), channel_id=1, source_target_pairs={{0,32},{32,0},{64,96},{96,64},{1,33},{33,1},{65,97},{97,65},{2,34}... | collective-permute-start | bytes 3686408 | tf_op jit(solution)/shard_map/ppermute | solution.py:89
  275.5 44.6 %all-to-all-start = ((bf16[8,512,3,128]{1,3,2,0:T(8,128)(2,1)}), bf16[8,512,3,128]{1,3,2,0:T(8,128)(2,1)S(1)}, u32[]{:S(2)}, u32[]{:S(2)}) async-start(bf16[8,512,3,128]{1,3,2,0:T(8,128)(2,1)} %concatenate.137), calls=%async_computation | async-start | bytes 6291456 | tf_op jit(solution)/shard_map/all_to_all | solution.py:208
  (32 other events, 321.3 us)
Sparse Core Ops, SparseCore 0:
  17.5 59.8 all-gather.2
  93.0 55.8 all-gather.4

commit v3 on v2

--- a/solution.py
+++ b/solution.py
@@ -202,12 +202,11 @@
     qkv = qkv.astype(jnp.bfloat16).reshape(group_rows, heads_here, 3, HDIM)
     active = min(heads_here, n_ctx)
     spare = n_ctx - active
-    outgoing = jnp.concatenate(
-        [qkv.transpose(1, 0, 2, 3), jnp.zeros((spare,) + qkv.shape[:1] + qkv.shape[2:], qkv.dtype)], 0
-    )
+    by_part = qkv.transpose(1, 2, 0, 3)
+    outgoing = jnp.concatenate([by_part, jnp.zeros((spare,) + by_part.shape[1:], qkv.dtype)], 0)
     triple = lax.all_to_all(outgoing, "ctx", 0, 0, tiled=True)
-    keys = triple[:, :, 1].reshape(-1, HDIM)
-    values = triple[:, :, 2].reshape(-1, HDIM)
+    keys = triple[:, 1].reshape(-1, HDIM)
+    values = triple[:, 2].reshape(-1, HDIM)
     inv_root = 1.0 / jnp.sqrt(jnp.float32(HDIM))
 
     def one_block(query):
@@ -218,7 +217,7 @@
         accum = jnp.dot(probs.astype(jnp.bfloat16), values, preferred_element_type=jnp.float32)
         return (accum / denom[:, None]).astype(jnp.bfloat16)
 
-    attended = lax.map(one_block, triple[:, :, 0])
+    attended = lax.map(one_block, triple[:, 0])
     by_head = lax.all_to_all(attended, "ctx", 0, 0, tiled=True)[:heads_here]
     return by_head.transpose(1, 0, 2).reshape(group_rows, heads_here * HDIM)
 

time: 405 us -> 405 us (level)
  no operation moved by 1% of the time
where the time goes in v3:
time: 405 us; the launch traced here: 400 us
  waiting for transfers between devices  141 us (35%)
  local copies, waits for them, and re-layouts  82.5 us (20%)
  matrix products  66.3 us (16%)
  starting transfers between devices  40.5 us (10%)
  other arithmetic  35.7 us (9%)
  blocking collectives  19.3 us (5%)
  between operations  15.2 us (4%)
    ppermute x9, waiting for transfers between devices, send(): return lax.ppermute(cells, 'ctx', [(i, step(i)) for i in range(n_ctx)])  76.1 us
    all_to_all x1, waiting for transfers between devices, shards(): triple = lax.all_to_all(outgoing, 'ctx', 0, 0, tiled=True)  38.9 us
    dot_general x3, matrix products, shards(): jnp.dot(jnp.concatenate(columns, 1), jnp.concatenate(weights, 0), preferr...  22.6 us
    all_to_all x1, blocking collectives, shards(): by_head = lax.all_to_all(attended, 'ctx', 0, 0, tiled=True)[:heads_here]  19.3 us
    dot_general x8, matrix products, one_block(): jnp.dot(query, keys.T, preferred_element_type=jnp.float32) * inv_root  18.2 us
    unnamed x74, local copies, waits for them, and re-layouts  17.8 us
    concatenate x3, other arithmetic, shards(): jnp.concatenate([cells for cells, _, _ in s], 0)  14.7 us
    all_gather x1, waiting for transfers between devices, shards(): lax.all_gather(jnp.concatenate([patch_weight, share_parts], 0), 'ctx', ax...  14.3 us
  transfers between devices with their start and end apart: 25, of which 12 were waited for; matrix products, arithmetic and copies ran while one was open for 28% of the time, Pallas kernels for 0%

profile of v3, /device:TPU:0, one launch (start us, length us, event | category | flops | bytes accessed | tf_op | source)
XLA Modules:
  0.0 400.5 jit_solution(8599806529541993874)
XLA Ops:
  10.0 4.1 %collective-permute-start = (bf16[6,1,32,96]{3,2,1,0:T(8,128)(2,1)}, bf16[6,1,32,96]{3,2,1,0:T(8,128)(2,1)}, u32[]{:S(2)}, u32[]{:S(2)}) collective-permute-start(bf16[6,1,32,96]{3,2,1,0:T(8,128)(2,1)} %get-tuple-element.109), channel_id=1, source_target_pairs={{0,8},{8,16},{16,24},{1,9},{9,17},{17,25},{2,10},{10,18},{18,26},{... | collective-permute-start | bytes 110600 | tf_op jit(solution)/shard_map/ppermute | solution.py:19
  22.5 3.5 collective-permute-start.2
  63.0 14.3 %all-gather.3.cloned.1.call-done = bf16[774,1280]{0,1:T(8,128)(2,1)} async-done(((bf16[774,160]{0,1:T(8,128)(2,1)}), bf16[774,1280]{0,1:T(8,128)(2,1)}) %all-gather.3.cloned.1.call-update) | async-done | bytes 1981456 | tf_op jit(solution)/shard_map/all_gather | solution.py:157
  92.9 3.9 copy.42
  104.3 24.1 %collective-permute-done.12 = bf16[320,1920]{1,0:T(8,128)(2,1)S(1)} collective-permute-done((bf16[320,1920]{1,0:T(8,128)(2,1)}, bf16[320,1920]{1,0:T(8,128)(2,1)S(1)}, u32[]{:S(2)}, u32[]{:S(2)}) %collective-permute-start.12) | collective-permute-done | bytes 1228832 | tf_op jit(solution)/shard_map/ppermute | solution.py:86
  135.2 6.4 %pad_maximum_fusion = bf16[960,1920]{1,0:T(8,128)(2,1)} fusion(bf16[320,1920]{1,0:T(8,128)(2,1)S(1)} %collective-permute-done.12, bf16[320,1920]{1,0:T(8,128)(2,1)S(1)} %collective-permute-done.11, bf16[320,1920]{1,0:T(8,128)(2,1)S(1)} %collective-permute-done.10), kind=kLoop, calls=%fused_computation.34 | loop fusion | flops 11059200 | bytes 7372800 | tf_op jit(solution)/shard_map/concatenate | solution.py:114
  141.7 27.5 %collective-permute-done.14 = bf16[160,1920]{1,0:T(8,128)(2,1)S(1)} collective-permute-done((bf16[160,1920]{1,0:T(8,128)(2,1)S(1)}, bf16[160,1920]{1,0:T(8,128)(2,1)S(1)}, u32[]{:S(2)}, u32[]{:S(2)}) %collective-permute-start.14) | collective-permute-done | bytes 614432 | tf_op jit(solution)/shard_map/ppermute | solution.py:86
  169.3 7.1 %pad_maximum_fusion.1 = bf16[960,1920]{1,0:T(8,128)(2,1)} fusion(bf16[320,1920]{1,0:T(8,128)(2,1)S(1)} %collective-permute-done.17, bf16[320,1920]{1,0:T(8,128)(2,1)S(1)} %collective-permute-done.16, bf16[160,1920]{1,0:T(8,128)(2,1)S(1)} %collective-permute-done.15, bf16[160,1920]{1,0:T(8,128)(2,1)S(1)} %collective-permute-done.14), kind=kLoop, calls=%fused_computation.35 | loop fusion | flops 14745600 | bytes 7372800 | tf_op jit(solution)/shard_map/concatenate | solution.py:114
  179.6 3.4 constant_dynamic-update-slice_fusion.14
  190.8 11.8 %collective-permute-done.19 = bf16[160,1920]{1,0:T(8,128)(2,1)S(1)} collective-permute-done((bf16[160,1920]{1,0:T(8,128)(2,1)S(1)}, bf16[160,1920]{1,0:T(8,128)(2,1)S(1)}, u32[]{:S(2)}, u32[]{:S(2)}) %collective-permute-start.19) | collective-permute-done | bytes 614432 | tf_op jit(solution)/shard_map/ppermute | solution.py:86
  202.6 12.6 %collective-permute-done.20 = bf16[160,1920]{1,0:T(8,128)(2,1)S(1)} collective-permute-done((bf16[160,1920]{1,0:T(8,128)(2,1)S(1)}, bf16[160,1920]{1,0:T(8,128)(2,1)S(1)}, u32[]{:S(2)}, u32[]{:S(2)}) %collective-permute-start.20) | collective-permute-done | bytes 614432 | tf_op jit(solution)/shard_map/ppermute | solution.py:86
  218.7 4.2 %constant_dynamic-update-slice_fusion.10 = bf16[2560,1920]{1,0:T(8,128)(2,1)} fusion(bf16[2560,1920]{1,0:T(8,128)(2,1)} %constant_dynamic-update-slice_fusion.11, bf16[960,1920]{1,0:T(8,128)(2,1)} %collective-permute-done.13), kind=kLoop, calls=%fused_computation.177 | loop fusion | bytes 7372800 | tf_op jit(solution)/shard_map/concatenate | solution.py:198
  223.0 4.1 %constant_dynamic-update-slice_fusion.15 = bf16[1920,1920]{1,0:T(8,128)(2,1)} fusion(bf16[1920,1920]{1,0:T(8,128)(2,1)} %constant_dynamic-update-slice_fusion.16, bf16[960,1920]{1,0:T(8,128)(2,1)} %collective-permute-done.18), kind=kLoop, calls=%fused_computation.182 | loop fusion | bytes 7372800 | tf_op jit(solution)/shard_map/concatenate | solution.py:198
  227.1 4.3 %constant_dynamic-slice_fusion.3 = (bf16[512,160]{1,0:T(8,128)(2,1)}, bf16[512,160]{1,0:T(8,128)(2,1)}, bf16[512,160]{1,0:T(8,128)(2,1)}, bf16[512,160]{1,0:T(8,...) fusion(bf16[512,5120]{1,0:T(8,128)(2,1)} %all-gather.5.cloned.1, ...), kind=kLoop, calls=%fused_computation.200 | loop fusion | bytes 2621472 | tf_op jit(solution)/shard_map/dynamic_slice | solution.py:192
  231.3 6.5 %constant_dynamic-slice_fusion.4 = (bf16[512,320]{1,0:T(8,128)(2,1)S(1)}, bf16[512,320]{1,0:T(8,128)(2,1)S(1)}, bf16[512,320]{1,0:T(8,128)(2,1)S(1)}, bf16[512,3...) fusion(bf16[512,5120]{1,0:T(8,128)(2,1)} %all-gather.5.cloned.1, ...), kind=kLoop, calls=%fused_computation.201 | loop fusion | bytes 6553640 | tf_op jit(solution)/shard_map/dynamic_slice | solution.py:192
  237.8 4.2 %concatenate.131 = bf16[512,1920]{1,0:T(8,128)(2,1)S(1)} concatenate(bf16[512,160]{1,0:T(8,128)(2,1)} %get-tuple-element.67, bf16[512,160]{1,0:T(8,128)(2,1)} %get-tuple-element.66, bf16[512,320]{1,0:T(8,128)(2,1)} %get-tuple-element.71, bf16[512,320]{1,0:T(8,128)(2,1)S(1)} %get-tuple-element.70, bf16[512,160]{1,0:T(8,128)(2,1)} %get-tuple-element.65, ...), dimensions={1} | concatenate | bytes 3932160 | tf_op jit(solution)/shard_map/concatenate | solution.py:197
  242.1 9.5 %fusion.149 = f32[512,1920]{1,0:T(8,128)} fusion(bf16[512,1920]{1,0:T(8,128)(2,1)S(1)} %concatenate.131, bf16[1920,1920]{1,0:T(8,128)(2,1)} %constant_dynamic-update-slice_fusion.15), kind=kOutput, calls=%fused_computation.260 | convolution fusion | flops 3774873600 | bytes 13271040 | tf_op jit(solution)/shard_map/dot_general | solution.py:196
  253.6 4.1 %concatenate.128 = bf16[512,2560]{1,0:T(8,128)(2,1)S(1)} concatenate(bf16[512,640]{1,0:T(8,128)(2,1)} %constant_dynamic-slice_fusion.19, bf16[512,320]{1,0:T(8,128)(2,1)} %get-tuple-element.77, bf16[512,320]{1,0:T(8,128)(2,1)} %get-tuple-element.76, bf16[512,320]{1,0:T(8,128)(2,1)} %get-tuple-element.75, bf16[512,320]{1,0:T(8,128)(2,1)} %get-tuple-element.74, ...), dimensions={1} | concatenate | bytes 5242880 | tf_op jit(solution)/shard_map/concatenate | solution.py:197
  257.8 8.5 %fusion.148 = f32[512,1920]{1,0:T(8,128)S(1)} fusion(bf16[512,2560]{1,0:T(8,128)(2,1)S(1)} %concatenate.128, bf16[2560,1920]{1,0:T(8,128)(2,1)} %constant_dynamic-update-slice_fusion.10), kind=kOutput, calls=%fused_computation.259 | convolution fusion | flops 5033164800 | bytes 16384000 | tf_op jit(solution)/shard_map/dot_general | solution.py:196
  266.4 4.6 %add_convert_fusion = bf16[512,1920]{1,0:T(8,128)(2,1)} fusion(f32[512,1920]{1,0:T(8,128)S(1)} %fusion.148, f32[512,1920]{1,0:T(8,128)S(1)} %copy-done.30, bf16[320,1920]{1,0:T(8,128)(2,1)} %collective-permute-done.21, bf16[160,1920]{1,0:T(8,128)(2,1)S(1)} %copy-done.20, bf16[160,1920]{1,0:T(8,128)(2,1)S(1)} %copy-done.18, ...), kind=kOutput, calls=%fused_computation.17 | convolution fusion | flops 1271234560 | bytes 12943360 | tf_op jit(solution)/shard_map/dot_general | solution.py:196
  275.5 5.8 %all-to-all-start = ((bf16[8,3,512,128]{2,3,1,0:T(8,128)(2,1)}), bf16[8,3,512,128]{2,3,1,0:T(8,128)(2,1)S(1)}, u32[]{:S(2)}, u32[]{:S(2)}) async-start(bf16[8,3,512,128]{2,3,1,0:T(8,128)(2,1)} %concatenate.137), calls=%async_computation | async-start | bytes 6291456 | tf_op jit(solution)/shard_map/all_to_all | solution.py:207
  281.3 38.9 %all-to-all-done = bf16[8,3,512,128]{2,3,1,0:T(8,128)(2,1)S(1)} async-done(((bf16[8,3,512,128]{2,3,1,0:T(8,128)(2,1)}), bf16[8,3,512,128]{2,3,1,0:T(8,128)(2,1)S(1)}, u32[]{:S(2)}, u32[]{:S(2)}) %all-to-all-start) | async-done | bytes 3145760 | tf_op jit(solution)/shard_map/all_to_all | solution.py:207
  324.3 48.6 %while.10 = (s32[]{:T(128)}, bf16[8,512,128]{1,2,0:T(8,128)(2,1)}, bf16[8,512,128]{1,2,0:T(8,128)(2,1)}, bf16[4096,128]{1,0:T(8,128)(2,1)S(1)}, bf16[4096,128]{1,0:T(8,128)(2,1)S(1)}, /*index=5*/s32[]{:T(128)}) while((s32[]{:T(128)}, bf16[8,512,128]{1,2,0:T(8,128)(2,1)}, bf16[8,512,128]{1,2,0:T(8,128)(2,1)}, bf16[4096,128]{1,0:T(8,128)(2,1)S(1)}, ...), condition=%wide.region_5.6_spmd, body=%wide.region_2.5_spmd.sunk | while | flops 1090649600 | bytes 28064836 | solution.py:220
  373.0 19.3 %all_to_all.10 = bf16[8,512,128]{1,2,0:T(8,128)(2,1)S(1)} all-to-all(bf16[8,512,128]{1,2,0:T(8,128)(2,1)} %get-tuple-element.32), channel_id=1, replica_groups=mesh['dp'=4,'head'=4,'ctx'=8] {'ctx'}, dimensions={0} | all-to-all | bytes 2097152 | tf_op jit(solution)/shard_map/all_to_all | solution.py:221
  (244 shorter events, 152.6 us)
Async XLA Ops:
  6.5 70.8 %all-gather.3.cloned.1.call-start = ((), (), s32[]{:S(2)}) async-start(), calls=%async_computation.2 | async-start | bytes 2580480 | tf_op jit(solution)/shard_map/all_gather | solution.py:157
  10.0 10.3 %collective-permute-start = (bf16[6,1,32,96]{3,2,1,0:T(8,128)(2,1)}, bf16[6,1,32,96]{3,2,1,0:T(8,128)(2,1)}, u32[]{:S(2)}, u32[]{:S(2)}) collective-permute-start(bf16[6,1,32,96]{3,2,1,0:T(8,128)(2,1)} %get-tuple-element.109), channel_id=1, source_target_pairs={{0,8},{8,16},{16,24},{1,9},{9,17},{17,25},{2,10},{10,18},{18,26},{... | collective-permute-start | bytes 110600 | tf_op jit(solution)/shard_map/ppermute | solution.py:19
  14.1 7.5 %collective-permute-start.1 = (bf16[6,1,32,96]{3,2,1,0:T(8,128)(2,1)S(1)}, bf16[6,1,32,96]{3,2,1,0:T(8,128)(2,1)}, u32[]{:S(2)}, u32[]{:S(2)}) collective-permute-start(bf16[6,1,32,96]{3,2,1,0:T(8,128)(2,1)S(1)} %get-tuple-element.108), channel_id=1, source_target_pairs={{8,0},{16,8},{24,16},{9,1},{17,9},{25,17},{10,2},{18,10},{26,18},{... | collective-permute-start | bytes 110600 | tf_op jit(solution)/shard_map/ppermute | solution.py:21
  17.4 209.7 %all-gather.5.cloned.1.call-start = ((), (), s32[]{:S(2)}) async-start(), calls=%async_computation.3 | async-start | bytes 6553600 | tf_op jit(solution)/shard_map/all_gather | solution.py:180
  22.5 5.8 %collective-permute-start.2 = (bf16[6,18,1,96]{3,2,1,0:T(2,128)(2,1)S(1)}, bf16[6,18,1,96]{3,2,1,0:T(2,128)(2,1)S(1)}, u32[]{:S(2)}, u32[]{:S(2)}) collective-permute-start(bf16[6,18,1,96]{3,2,1,0:T(2,128)(2,1)S(1)} %get-tuple-element.97), channel_id=1, source_target_pairs={{0,1},{1,2},{2,3},{3,4},{4,5},{5,6},{6,7},{8,9},{9,10},{10,11},{11... | collective-permute-start | bytes 62216 | tf_op jit(solution)/shard_map/ppermute | solution.py:19
  26.0 7.0 %collective-permute-start.3 = (bf16[6,18,1,96]{3,2,1,0:T(2,128)(2,1)S(1)}, bf16[6,18,1,96]{3,2,1,0:T(2,128)(2,1)S(1)}, u32[]{:S(2)}, u32[]{:S(2)}) collective-permute-start(bf16[6,18,1,96]{3,2,1,0:T(2,128)(2,1)S(1)} %get-tuple-element.98), channel_id=1, source_target_pairs={{1,0},{2,1},{3,2},{4,3},{5,4},{6,5},{7,6},{9,8},{10,9},{11,10},{12... | collective-permute-start | bytes 62216 | tf_op jit(solution)/shard_map/ppermute | solution.py:21
  48.6 9.7 %collective-permute-start.4 = (bf16[128,768]{1,0:T(8,128)(2,1)S(1)}, bf16[128,768]{1,0:T(8,128)(2,1)S(1)}, u32[]{:S(2)}, u32[]{:S(2)}) collective-permute-start(bf16[128,768]{1,0:T(8,128)(2,1)S(1)} %reshape.127), channel_id=1, source_target_pairs={{0,8},{8,16},{16,24},{24,0},{1,9},{9,17},{17,25},{25,1},{2,10},{10... | collective-permute-start | bytes 589832 | tf_op jit(solution)/shard_map/ppermute | solution.py:32
  51.3 9.8 %collective-permute-start.5 = (bf16[128,768]{1,0:T(8,128)(2,1)S(1)}, bf16[128,768]{1,0:T(8,128)(2,1)S(1)}, u32[]{:S(2)}, u32[]{:S(2)}) collective-permute-start(bf16[128,768]{1,0:T(8,128)(2,1)S(1)} %reshape.127), channel_id=1, source_target_pairs={{0,16},{8,24},{16,0},{24,8},{1,17},{9,25},{17,1},{25,9},{2,18},{10... | collective-permute-start | bytes 589832 | tf_op jit(solution)/shard_map/ppermute | solution.py:32
  54.1 7.0 %collective-permute-start.6 = (bf16[128,768]{1,0:T(8,128)(2,1)S(1)}, bf16[128,768]{1,0:T(8,128)(2,1)S(1)}, u32[]{:S(2)}, u32[]{:S(2)}) collective-permute-start(bf16[128,768]{1,0:T(8,128)(2,1)S(1)} %reshape.127), channel_id=1, source_target_pairs={{0,24},{8,0},{16,8},{24,16},{1,25},{9,1},{17,9},{25,17},{2,26},{10... | collective-permute-start | bytes 589832 | tf_op jit(solution)/shard_map/ppermute | solution.py:32
  81.9 6.0 %collective-permute-start.7 = (f32[3072]{0:T(1024)S(1)}, f32[3072]{0:T(1024)S(1)}, u32[]{:S(2)}, u32[]{:S(2)}) collective-permute-start(f32[3072]{0:T(1024)S(1)} %pad_maximum_fusion.8), channel_id=1, source_target_pairs={{0,8},{8,16},{16,24},{24,0},{1,9},{9,17},{17,25},{25,1},{2,10},{10... | collective-permute-start | bytes 36872 | tf_op jit(solution)/shard_map/ppermute | solution.py:32
  84.0 5.2 %collective-permute-start.8 = (f32[3072]{0:T(1024)S(1)}, f32[3072]{0:T(1024)S(1)}, u32[]{:S(2)}, u32[]{:S(2)}) collective-permute-start(f32[3072]{0:T(1024)S(1)} %pad_maximum_fusion.8), channel_id=1, source_target_pairs={{0,16},{8,24},{16,0},{24,8},{1,17},{9,25},{17,1},{25,9},{2,18},{10... | collective-permute-start | bytes 36872 | tf_op jit(solution)/shard_map/ppermute | solution.py:32
  101.1 27.4 %collective-permute-start.12 = (bf16[320,1920]{1,0:T(8,128)(2,1)}, bf16[320,1920]{1,0:T(8,128)(2,1)S(1)}, u32[]{:S(2)}, u32[]{:S(2)}) collective-permute-start(bf16[320,1920]{1,0:T(8,128)(2,1)} %copy.43), channel_id=1, source_target_pairs={{0,1},{1,0},{2,3},{3,2},{4,5},{5,4},{6,7},{7,6},{8,9},{9,8},{10,11... | collective-permute-start | bytes 3686408 | tf_op jit(solution)/shard_map/ppermute | solution.py:86
  101.1 30.6 %collective-permute-start.10 = (bf16[320,1920]{1,0:T(8,128)(2,1)}, bf16[320,1920]{1,0:T(8,128)(2,1)S(1)}, u32[]{:S(2)}, u32[]{:S(2)}) collective-permute-start(bf16[320,1920]{1,0:T(8,128)(2,1)} %copy.43), channel_id=1, source_target_pairs={{0,2},{1,3},{2,4},{3,5},{4,6},{5,7},{6,0},{7,1},{8,10},{9,11},{10,... | collective-permute-start | bytes 3686408 | tf_op jit(solution)/shard_map/ppermute | solution.py:86
  102.6 29.3 %collective-permute-start.11 = (bf16[320,1920]{1,0:T(8,128)(2,1)}, bf16[320,1920]{1,0:T(8,128)(2,1)S(1)}, u32[]{:S(2)}, u32[]{:S(2)}) collective-permute-start(bf16[320,1920]{1,0:T(8,128)(2,1)} %copy.43), channel_id=1, source_target_pairs={{0,6},{1,7},{2,0},{3,1},{4,2},{5,3},{6,4},{7,5},{8,14},{9,15},{10,... | collective-permute-start | bytes 3686408 | tf_op jit(solution)/shard_map/ppermute | solution.py:86
  128.5 40.8 %collective-permute-start.16 = (bf16[320,1920]{1,0:T(8,128)(2,1)S(1)}, bf16[320,1920]{1,0:T(8,128)(2,1)S(1)}, u32[]{:S(2)}, u32[]{:S(2)}) collective-permute-start(bf16[320,1920]{1,0:T(8,128)(2,1)S(1)} %collective-permute-done.12), channel_id=1, source_target_pairs={{0,2},{1,3},{2,4},{3,5},{4,6},{5,7},{6,0},{7,1},{8,10},{9,11},{10,... | collective-permute-start | bytes 3686408 | tf_op jit(solution)/shard_map/ppermute | solution.py:86
  128.8 40.5 %collective-permute-start.17 = (bf16[320,1920]{1,0:T(8,128)(2,1)S(1)}, bf16[320,1920]{1,0:T(8,128)(2,1)S(1)}, u32[]{:S(2)}, u32[]{:S(2)}) collective-permute-start(bf16[320,1920]{1,0:T(8,128)(2,1)S(1)} %collective-permute-done.12), channel_id=1, source_target_pairs={{0,6},{1,7},{2,0},{3,1},{4,2},{5,3},{6,4},{7,5},{8,14},{9,15},{10,... | collective-permute-start | bytes 3686408 | tf_op jit(solution)/shard_map/ppermute | solution.py:86
  131.7 37.4 %collective-permute-start.14 = (bf16[160,1920]{1,0:T(8,128)(2,1)S(1)}, bf16[160,1920]{1,0:T(8,128)(2,1)S(1)}, u32[]{:S(2)}, u32[]{:S(2)}) collective-permute-start(bf16[160,1920]{1,0:T(8,128)(2,1)S(1)} %slice.351), channel_id=1, source_target_pairs={{0,2},{1,3},{2,4},{3,5},{4,6},{5,7},{6,0},{7,1},{8,10},{9,11},{10,... | collective-permute-start | bytes 1843208 | tf_op jit(solution)/shard_map/ppermute | solution.py:86
  131.9 37.4 %collective-permute-start.15 = (bf16[160,1920]{1,0:T(8,128)(2,1)S(1)}, bf16[160,1920]{1,0:T(8,128)(2,1)S(1)}, u32[]{:S(2)}, u32[]{:S(2)}) collective-permute-start(bf16[160,1920]{1,0:T(8,128)(2,1)S(1)} %slice.352), channel_id=1, source_target_pairs={{0,6},{1,7},{2,0},{3,1},{4,2},{5,3},{6,4},{7,5},{8,14},{9,15},{10,... | collective-permute-start | bytes 1843208 | tf_op jit(solution)/shard_map/ppermute | solution.py:86
  141.6 77.2 %collective-permute-start.13 = (bf16[960,1920]{1,0:T(8,128)(2,1)}, bf16[960,1920]{1,0:T(8,128)(2,1)}, u32[]{:S(2)}, u32[]{:S(2)}) collective-permute-start(bf16[960,1920]{1,0:T(8,128)(2,1)} %pad_maximum_fusion), channel_id=1, source_target_pairs={{0,32},{32,0},{64,96},{96,64},{1,33},{33,1},{65,97},{97,65},{2,34}... | collective-permute-start | bytes 11059208 | tf_op jit(solution)/shard_map/ppermute | solution.py:89
  176.4 46.6 %collective-permute-start.18 = (bf16[960,1920]{1,0:T(8,128)(2,1)}, bf16[960,1920]{1,0:T(8,128)(2,1)}, u32[]{:S(2)}, u32[]{:S(2)}) collective-permute-start(bf16[960,1920]{1,0:T(8,128)(2,1)} %pad_maximum_fusion.1), channel_id=1, source_target_pairs={{0,32},{32,0},{64,96},{96,64},{1,33},{33,1},{65,97},{97,65},{2,34}... | collective-permute-start | bytes 11059208 | tf_op jit(solution)/shard_map/ppermute | solution.py:89
  185.9 16.7 %collective-permute-start.19 = (bf16[160,1920]{1,0:T(8,128)(2,1)S(1)}, bf16[160,1920]{1,0:T(8,128)(2,1)S(1)}, u32[]{:S(2)}, u32[]{:S(2)}) collective-permute-start(bf16[160,1920]{1,0:T(8,128)(2,1)S(1)} %collective-permute-done.14), channel_id=1, source_target_pairs={{0,1},{1,0},{2,3},{3,2},{4,5},{5,4},{6,7},{7,6},{8,9},{9,8},{10,11... | collective-permute-start | bytes 1843208 | tf_op jit(solution)/shard_map/ppermute | solution.py:86
  187.6 27.6 %collective-permute-start.20 = (bf16[160,1920]{1,0:T(8,128)(2,1)S(1)}, bf16[160,1920]{1,0:T(8,128)(2,1)S(1)}, u32[]{:S(2)}, u32[]{:S(2)}) collective-permute-start(bf16[160,1920]{1,0:T(8,128)(2,1)S(1)} %copy-done.14), channel_id=1, source_target_pairs={{0,1},{1,0},{2,3},{3,2},{4,5},{5,4},{6,7},{7,6},{8,9},{9,8},{10,11... | collective-permute-start | bytes 1843208 | tf_op jit(solution)/shard_map/ppermute | solution.py:86
  216.4 49.9 %collective-permute-start.21 = (bf16[320,1920]{1,0:T(8,128)(2,1)}, bf16[320,1920]{1,0:T(8,128)(2,1)}, u32[]{:S(2)}, u32[]{:S(2)}) collective-permute-start(bf16[320,1920]{1,0:T(8,128)(2,1)} %pad_maximum_fusion.4), channel_id=1, source_target_pairs={{0,32},{32,0},{64,96},{96,64},{1,33},{33,1},{65,97},{97,65},{2,34}... | collective-permute-start | bytes 3686408 | tf_op jit(solution)/shard_map/ppermute | solution.py:89
  275.5 44.6 %all-to-all-start = ((bf16[8,3,512,128]{2,3,1,0:T(8,128)(2,1)}), bf16[8,3,512,128]{2,3,1,0:T(8,128)(2,1)S(1)}, u32[]{:S(2)}, u32[]{:S(2)}) async-start(bf16[8,3,512,128]{2,3,1,0:T(8,128)(2,1)} %concatenate.137), calls=%async_computation | async-start | bytes 6291456 | tf_op jit(solution)/shard_map/all_to_all | solution.py:207
  (32 other events, 321.3 us)
Sparse Core Ops, SparseCore 0:
  17.5 59.8 all-gather.2
  93.0 55.8 all-gather.4

commit v4 on v3

--- a/solution.py
+++ b/solution.py
@@ -217,7 +217,9 @@
         accum = jnp.dot(probs.astype(jnp.bfloat16), values, preferred_element_type=jnp.float32)
         return (accum / denom[:, None]).astype(jnp.bfloat16)
 
-    attended = lax.map(one_block, triple[:, 0])
+    queries = triple[:, 0]
+    chunks = 4
+    attended = lax.map(one_block, queries.reshape(chunks, -1, HDIM)).reshape(queries.shape)
     by_head = lax.all_to_all(attended, "ctx", 0, 0, tiled=True)[:heads_here]
     return by_head.transpose(1, 0, 2).reshape(group_rows, heads_here * HDIM)
 

time: 405 us -> 463 us (1.14)
  matrix products: 66.3 us -> 105 us
  other arithmetic: 35.7 us -> 58.5 us
    dot_general x8 -> x4, matrix products: 12 us -> 36.7 us  [one_block(): jnp.dot(probs.astype(jnp.bfloat16), values, preferred_element_type=jnp.fl...]
    reduce_sum x8 -> x4, other arithmetic: 12.1 us -> 34.8 us  [one_block(): denom = jnp.sum(probs, -1)]
    dot_general x8 -> x4, matrix products: 18.2 us -> 32.6 us  [one_block(): jnp.dot(query, keys.T, preferred_element_type=jnp.float32) * inv_root]
    dynamic_update_slice x16 -> x0, local copies, waits for them, and re-layouts: 6.27 us -> none  [shards(): attended = lax.map(one_block, triple[:, 0])]
  transfers between devices with their start and end apart: 25 -> 25, of which waited for: 12 -> 12; matrix products, arithmetic and copies ran while one was open for 28% -> 24% of each run, Pallas kernels for 0% -> 0%
where the time goes in v4:
time: 463 us; the launch traced here: 458 us
  waiting for transfers between devices  141 us (30%)
  matrix products  105 us (23%)
  local copies, waits for them, and re-layouts  78.9 us (17%)
  other arithmetic  58.5 us (13%)
  starting transfers between devices  40.3 us (9%)
  blocking collectives  19.3 us (4%)
  between operations  15.2 us (3%)
    ppermute x9, waiting for transfers between devices, send(): return lax.ppermute(cells, 'ctx', [(i, step(i)) for i in range(n_ctx)])  76.1 us
    all_to_all x1, waiting for transfers between devices, shards(): triple = lax.all_to_all(outgoing, 'ctx', 0, 0, tiled=True)  38.8 us
    dot_general x4, matrix products, one_block(): jnp.dot(probs.astype(jnp.bfloat16), values, preferred_element_type=jnp.fl...  36.7 us
    reduce_sum x4, other arithmetic, one_block(): denom = jnp.sum(probs, -1)  34.8 us
    dot_general x4, matrix products, one_block(): jnp.dot(query, keys.T, preferred_element_type=jnp.float32) * inv_root  32.6 us
    dot_general x3, matrix products, shards(): jnp.dot(jnp.concatenate(columns, 1), jnp.concatenate(weights, 0), preferr...  22.6 us
    all_to_all x1, blocking collectives, shards(): by_head = lax.all_to_all(attended, 'ctx', 0, 0, tiled=True)[:heads_here]  19.3 us
    unnamed x74, local copies, waits for them, and re-layouts  17.8 us
  transfers between devices with their start and end apart: 25, of which 12 were waited for; matrix products, arithmetic and copies ran while one was open for 24% of the time, Pallas kernels for 0%

profile of v4, /device:TPU:0, one launch (start us, length us, event | category | flops | bytes accessed | tf_op | source)
XLA Modules:
  0.0 458.3 jit_solution(10106550866489987910)
XLA Ops:
  63.6 13.8 %all-gather.3.cloned.1.call-done = bf16[774,1280]{0,1:T(8,128)(2,1)} async-done(((bf16[774,160]{0,1:T(8,128)(2,1)}), bf16[774,1280]{0,1:T(8,128)(2,1)}) %all-gather.3.cloned.1.call-update) | async-done | bytes 1981456 | tf_op jit(solution)/shard_map/all_gather | solution.py:157
  104.3 24.1 %collective-permute-done.12 = bf16[320,1920]{1,0:T(8,128)(2,1)S(1)} collective-permute-done((bf16[320,1920]{1,0:T(8,128)(2,1)}, bf16[320,1920]{1,0:T(8,128)(2,1)S(1)}, u32[]{:S(2)}, u32[]{:S(2)}) %collective-permute-start.12) | collective-permute-done | bytes 1228832 | tf_op jit(solution)/shard_map/ppermute | solution.py:86
  135.1 6.4 %pad_maximum_fusion = bf16[960,1920]{1,0:T(8,128)(2,1)} fusion(bf16[320,1920]{1,0:T(8,128)(2,1)S(1)} %collective-permute-done.12, bf16[320,1920]{1,0:T(8,128)(2,1)S(1)} %collective-permute-done.11, bf16[320,1920]{1,0:T(8,128)(2,1)S(1)} %collective-permute-done.10), kind=kLoop, calls=%fused_computation.34 | loop fusion | flops 11059200 | bytes 7372800 | tf_op jit(solution)/shard_map/concatenate | solution.py:114
  141.7 27.5 %collective-permute-done.14 = bf16[160,1920]{1,0:T(8,128)(2,1)S(1)} collective-permute-done((bf16[160,1920]{1,0:T(8,128)(2,1)S(1)}, bf16[160,1920]{1,0:T(8,128)(2,1)S(1)}, u32[]{:S(2)}, u32[]{:S(2)}) %collective-permute-start.14) | collective-permute-done | bytes 614432 | tf_op jit(solution)/shard_map/ppermute | solution.py:86
  169.4 7.1 %pad_maximum_fusion.1 = bf16[960,1920]{1,0:T(8,128)(2,1)} fusion(bf16[320,1920]{1,0:T(8,128)(2,1)S(1)} %collective-permute-done.17, bf16[320,1920]{1,0:T(8,128)(2,1)S(1)} %collective-permute-done.16, bf16[160,1920]{1,0:T(8,128)(2,1)S(1)} %collective-permute-done.15, bf16[160,1920]{1,0:T(8,128)(2,1)S(1)} %collective-permute-done.14), kind=kLoop, calls=%fused_computation.35 | loop fusion | flops 14745600 | bytes 7372800 | tf_op jit(solution)/shard_map/concatenate | solution.py:114
  190.9 11.7 %collective-permute-done.19 = bf16[160,1920]{1,0:T(8,128)(2,1)S(1)} collective-permute-done((bf16[160,1920]{1,0:T(8,128)(2,1)S(1)}, bf16[160,1920]{1,0:T(8,128)(2,1)S(1)}, u32[]{:S(2)}, u32[]{:S(2)}) %collective-permute-start.19) | collective-permute-done | bytes 614432 | tf_op jit(solution)/shard_map/ppermute | solution.py:86
  202.7 12.6 %collective-permute-done.20 = bf16[160,1920]{1,0:T(8,128)(2,1)S(1)} collective-permute-done((bf16[160,1920]{1,0:T(8,128)(2,1)S(1)}, bf16[160,1920]{1,0:T(8,128)(2,1)S(1)}, u32[]{:S(2)}, u32[]{:S(2)}) %collective-permute-start.20) | collective-permute-done | bytes 614432 | tf_op jit(solution)/shard_map/ppermute | solution.py:86
  242.2 9.5 %fusion.152 = f32[512,1920]{1,0:T(8,128)} fusion(bf16[512,1920]{1,0:T(8,128)(2,1)S(1)} %concatenate.131, bf16[1920,1920]{1,0:T(8,128)(2,1)} %constant_dynamic-update-slice_fusion.14), kind=kOutput, calls=%fused_computation.260 | convolution fusion | flops 3774873600 | bytes 13271040 | tf_op jit(solution)/shard_map/dot_general | solution.py:196
  257.9 8.5 %fusion.151 = f32[512,1920]{1,0:T(8,128)S(1)} fusion(bf16[512,2560]{1,0:T(8,128)(2,1)S(1)} %concatenate.128, bf16[2560,1920]{1,0:T(8,128)(2,1)} %constant_dynamic-update-slice_fusion.9), kind=kOutput, calls=%fused_computation.259 | convolution fusion | flops 5033164800 | bytes 16384000 | tf_op jit(solution)/shard_map/dot_general | solution.py:196
  281.1 38.8 %all-to-all-done = bf16[8,3,512,128]{2,3,1,0:T(8,128)(2,1)S(1)} async-done(((bf16[8,3,512,128]{2,3,1,0:T(8,128)(2,1)}), bf16[8,3,512,128]{2,3,1,0:T(8,128)(2,1)S(1)}, u32[]{:S(2)}, u32[]{:S(2)}) %all-to-all-start) | async-done | bytes 3145760 | tf_op jit(solution)/shard_map/all_to_all | solution.py:207
  326.4 104.2 %while.10 = (s32[]{:T(128)}, bf16[4,1024,128]{2,1,0:T(8,128)(2,1)}, bf16[4,1024,128]{2,1,0:T(8,128)(2,1)S(1)}, bf16[4096,128]{1,0:T(8,128)(2,1)S(1)}, bf16[4096,128]{1,0:T(8,128)(2,1)}, /*index=5*/s32[]{:T(128)}) while((s32[]{:T(128)}, bf16[4,1024,128]{2,1,0:T(8,128)(2,1)}, bf16[4,1024,128]{2,1,0:T(8,128)(2,1)S(1)}, ...), condition=%wide.region_5.6_spmd, body=%wide.region_2.5_spmd.sunk | while | flops 2181299200 | bytes 57176676 | solution.py:222
  326.4 8.1 %multiply_reduce_fusion.3 = (f32[1024]{0:T(1024)S(1)}, f32[1024,4096]{1,0:T(8,128)}) fusion(bf16[4096,128]{1,0:T(8,128)(2,1)S(1)} %get-tuple-element.160, bf16[4,1024,128]{2,1,0:T(8,128)(2,1)S(1)} %get-tuple-element.159, s32[]{:T(128)} %get-tuple-element.151), kind=kOutput, calls=%fused_computation.3.clone.1 | convolution fusion | flops 1082129408 | bytes 18092036 | tf_op jit(solution)/shard_map/while/body/eval_jaxpr/dot_general | solution.py:213
  334.5 8.7 %fusion.172 = f32[1024]{0:T(1024)S(1)} fusion(f32[1024,4096]{1,0:T(8,128)} %get-tuple-element.143, f32[1024]{0:T(1024)S(1)} %broadcast_maximum_fusion.2), kind=kLoop, calls=%fused_computation.4.clone.1 | loop fusion | flops 12581888 | bytes 16785408 | tf_op jit(solution)/shard_map/while/body/eval_jaxpr/reduce_sum | solution.py:216
  343.3 9.2 %fusion.173 = bf16[4,1024,128]{2,1,0:T(8,128)(2,1)} fusion(bf16[4,1024,128]{2,1,0:T(8,128)(2,1)} %get-tuple-element.152, s32[]{:T(128)} %get-tuple-element.151, bf16[4096,128]{1,0:T(8,128)(2,1)S(1)} %copy-done.17, f32[1024,4096]{1,0:T(8,128)} %get-tuple-element.143, f32[1024]{0:T(1024)S(1)} %broadcast_maximum_fusion.2, f32[1024]{0:T(1024)S(1)} %fusion.172), kind=kOutput, calls=%fused_computation.10.clone.1 | convolution fusion | flops 1086586880 | bytes 18096640 | tf_op jit(solution)/shard_map/while/body/eval_jaxpr/dot_general | solution.py:217
  352.4 8.1 %multiply_reduce_fusion.3 = (f32[1024]{0:T(1024)S(1)}, f32[1024,4096]{1,0:T(8,128)}) fusion(bf16[4096,128]{1,0:T(8,128)(2,1)S(1)} %get-tuple-element.160, bf16[4,1024,128]{2,1,0:T(8,128)(2,1)S(1)} %get-tuple-element.159, s32[]{:T(128)} %get-tuple-element.151), kind=kOutput, calls=%fused_computation.3.clone.1 | convolution fusion | flops 1082129408 | bytes 18092036 | tf_op jit(solution)/shard_map/while/body/eval_jaxpr/dot_general | solution.py:213
  360.6 8.7 %fusion.172 = f32[1024]{0:T(1024)S(1)} fusion(f32[1024,4096]{1,0:T(8,128)} %get-tuple-element.143, f32[1024]{0:T(1024)S(1)} %broadcast_maximum_fusion.2), kind=kLoop, calls=%fused_computation.4.clone.1 | loop fusion | flops 12581888 | bytes 16785408 | tf_op jit(solution)/shard_map/while/body/eval_jaxpr/reduce_sum | solution.py:216
  369.3 9.2 %fusion.173 = bf16[4,1024,128]{2,1,0:T(8,128)(2,1)} fusion(bf16[4,1024,128]{2,1,0:T(8,128)(2,1)} %get-tuple-element.152, s32[]{:T(128)} %get-tuple-element.151, bf16[4096,128]{1,0:T(8,128)(2,1)S(1)} %copy-done.17, f32[1024,4096]{1,0:T(8,128)} %get-tuple-element.143, f32[1024]{0:T(1024)S(1)} %broadcast_maximum_fusion.2, f32[1024]{0:T(1024)S(1)} %fusion.172), kind=kOutput, calls=%fused_computation.10.clone.1 | convolution fusion | flops 1086586880 | bytes 18096640 | tf_op jit(solution)/shard_map/while/body/eval_jaxpr/dot_general | solution.py:217
  378.5 8.2 %multiply_reduce_fusion.3 = (f32[1024]{0:T(1024)S(1)}, f32[1024,4096]{1,0:T(8,128)}) fusion(bf16[4096,128]{1,0:T(8,128)(2,1)S(1)} %get-tuple-element.160, bf16[4,1024,128]{2,1,0:T(8,128)(2,1)S(1)} %get-tuple-element.159, s32[]{:T(128)} %get-tuple-element.151), kind=kOutput, calls=%fused_computation.3.clone.1 | convolution fusion | flops 1082129408 | bytes 18092036 | tf_op jit(solution)/shard_map/while/body/eval_jaxpr/dot_general | solution.py:213
  386.6 8.7 %fusion.172 = f32[1024]{0:T(1024)S(1)} fusion(f32[1024,4096]{1,0:T(8,128)} %get-tuple-element.143, f32[1024]{0:T(1024)S(1)} %broadcast_maximum_fusion.2), kind=kLoop, calls=%fused_computation.4.clone.1 | loop fusion | flops 12581888 | bytes 16785408 | tf_op jit(solution)/shard_map/while/body/eval_jaxpr/reduce_sum | solution.py:216
  395.4 9.2 %fusion.173 = bf16[4,1024,128]{2,1,0:T(8,128)(2,1)} fusion(bf16[4,1024,128]{2,1,0:T(8,128)(2,1)} %get-tuple-element.152, s32[]{:T(128)} %get-tuple-element.151, bf16[4096,128]{1,0:T(8,128)(2,1)S(1)} %copy-done.17, f32[1024,4096]{1,0:T(8,128)} %get-tuple-element.143, f32[1024]{0:T(1024)S(1)} %broadcast_maximum_fusion.2, f32[1024]{0:T(1024)S(1)} %fusion.172), kind=kOutput, calls=%fused_computation.10.clone.1 | convolution fusion | flops 1086586880 | bytes 18096640 | tf_op jit(solution)/shard_map/while/body/eval_jaxpr/dot_general | solution.py:217
  404.5 8.2 %multiply_reduce_fusion.3 = (f32[1024]{0:T(1024)S(1)}, f32[1024,4096]{1,0:T(8,128)}) fusion(bf16[4096,128]{1,0:T(8,128)(2,1)S(1)} %get-tuple-element.160, bf16[4,1024,128]{2,1,0:T(8,128)(2,1)S(1)} %get-tuple-element.159, s32[]{:T(128)} %get-tuple-element.151), kind=kOutput, calls=%fused_computation.3.clone.1 | convolution fusion | flops 1082129408 | bytes 18092036 | tf_op jit(solution)/shard_map/while/body/eval_jaxpr/dot_general | solution.py:213
  412.7 8.7 %fusion.172 = f32[1024]{0:T(1024)S(1)} fusion(f32[1024,4096]{1,0:T(8,128)} %get-tuple-element.143, f32[1024]{0:T(1024)S(1)} %broadcast_maximum_fusion.2), kind=kLoop, calls=%fused_computation.4.clone.1 | loop fusion | flops 12581888 | bytes 16785408 | tf_op jit(solution)/shard_map/while/body/eval_jaxpr/reduce_sum | solution.py:216
  421.4 9.2 %fusion.173 = bf16[4,1024,128]{2,1,0:T(8,128)(2,1)} fusion(bf16[4,1024,128]{2,1,0:T(8,128)(2,1)} %get-tuple-element.152, s32[]{:T(128)} %get-tuple-element.151, bf16[4096,128]{1,0:T(8,128)(2,1)S(1)} %copy-done.17, f32[1024,4096]{1,0:T(8,128)} %get-tuple-element.143, f32[1024]{0:T(1024)S(1)} %broadcast_maximum_fusion.2, f32[1024]{0:T(1024)S(1)} %fusion.172), kind=kOutput, calls=%fused_computation.10.clone.1 | convolution fusion | flops 1086586880 | bytes 18096640 | tf_op jit(solution)/shard_map/while/body/eval_jaxpr/dot_general | solution.py:217
  430.6 19.3 %all_to_all.10 = bf16[8,512,128]{2,1,0:T(8,128)(2,1)S(1)} all-to-all(bf16[8,512,128]{2,1,0:T(8,128)(2,1)} %bitcast.51), channel_id=1, replica_groups=mesh['dp'=4,'head'=4,'ctx'=8] {'ctx'}, dimensions={0} | all-to-all | bytes 2097152 | tf_op jit(solution)/shard_map/all_to_all | solution.py:223
  (222 shorter events, 159.6 us)
Async XLA Ops:
  6.5 70.9 %all-gather.3.cloned.1.call-start = ((), (), s32[]{:S(2)}) async-start(), calls=%async_computation.2 | async-start | bytes 2580480 | tf_op jit(solution)/shard_map/all_gather | solution.py:157
  10.0 10.3 %collective-permute-start = (bf16[6,1,32,96]{3,2,1,0:T(8,128)(2,1)}, bf16[6,1,32,96]{3,2,1,0:T(8,128)(2,1)}, u32[]{:S(2)}, u32[]{:S(2)}) collective-permute-start(bf16[6,1,32,96]{3,2,1,0:T(8,128)(2,1)} %get-tuple-element.94), channel_id=1, source_target_pairs={{0,8},{8,16},{16,24},{1,9},{9,17},{17,25},{2,10},{10,18},{18,26},{... | collective-permute-start | bytes 110600 | tf_op jit(solution)/shard_map/ppermute | solution.py:19
  14.1 7.6 %collective-permute-start.1 = (bf16[6,1,32,96]{3,2,1,0:T(8,128)(2,1)S(1)}, bf16[6,1,32,96]{3,2,1,0:T(8,128)(2,1)}, u32[]{:S(2)}, u32[]{:S(2)}) collective-permute-start(bf16[6,1,32,96]{3,2,1,0:T(8,128)(2,1)S(1)} %get-tuple-element.93), channel_id=1, source_target_pairs={{8,0},{16,8},{24,16},{9,1},{17,9},{25,17},{10,2},{18,10},{26,18},{... | collective-permute-start | bytes 110600 | tf_op jit(solution)/shard_map/ppermute | solution.py:21
  17.4 209.8 %all-gather.5.cloned.1.call-start = ((), (), s32[]{:S(2)}) async-start(), calls=%async_computation.3 | async-start | bytes 6553600 | tf_op jit(solution)/shard_map/all_gather | solution.py:180
  22.6 5.8 %collective-permute-start.2 = (bf16[6,18,1,96]{3,2,1,0:T(2,128)(2,1)S(1)}, bf16[6,18,1,96]{3,2,1,0:T(2,128)(2,1)S(1)}, u32[]{:S(2)}, u32[]{:S(2)}) collective-permute-start(bf16[6,18,1,96]{3,2,1,0:T(2,128)(2,1)S(1)} %get-tuple-element.82), channel_id=1, source_target_pairs={{0,1},{1,2},{2,3},{3,4},{4,5},{5,6},{6,7},{8,9},{9,10},{10,11},{11... | collective-permute-start | bytes 62216 | tf_op jit(solution)/shard_map/ppermute | solution.py:19
  26.1 7.0 %collective-permute-start.3 = (bf16[6,18,1,96]{3,2,1,0:T(2,128)(2,1)S(1)}, bf16[6,18,1,96]{3,2,1,0:T(2,128)(2,1)S(1)}, u32[]{:S(2)}, u32[]{:S(2)}) collective-permute-start(bf16[6,18,1,96]{3,2,1,0:T(2,128)(2,1)S(1)} %get-tuple-element.83), channel_id=1, source_target_pairs={{1,0},{2,1},{3,2},{4,3},{5,4},{6,5},{7,6},{9,8},{10,9},{11,10},{12... | collective-permute-start | bytes 62216 | tf_op jit(solution)/shard_map/ppermute | solution.py:21
  48.7 9.1 %collective-permute-start.4 = (bf16[128,768]{1,0:T(8,128)(2,1)S(1)}, bf16[128,768]{1,0:T(8,128)(2,1)S(1)}, u32[]{:S(2)}, u32[]{:S(2)}) collective-permute-start(bf16[128,768]{1,0:T(8,128)(2,1)S(1)} %reshape.130), channel_id=1, source_target_pairs={{0,8},{8,16},{16,24},{24,0},{1,9},{9,17},{17,25},{25,1},{2,10},{10... | collective-permute-start | bytes 589832 | tf_op jit(solution)/shard_map/ppermute | solution.py:32
  51.4 10.3 %collective-permute-start.5 = (bf16[128,768]{1,0:T(8,128)(2,1)S(1)}, bf16[128,768]{1,0:T(8,128)(2,1)S(1)}, u32[]{:S(2)}, u32[]{:S(2)}) collective-permute-start(bf16[128,768]{1,0:T(8,128)(2,1)S(1)} %reshape.130), channel_id=1, source_target_pairs={{0,16},{8,24},{16,0},{24,8},{1,17},{9,25},{17,1},{25,9},{2,18},{10... | collective-permute-start | bytes 589832 | tf_op jit(solution)/shard_map/ppermute | solution.py:32
  54.2 7.5 %collective-permute-start.6 = (bf16[128,768]{1,0:T(8,128)(2,1)S(1)}, bf16[128,768]{1,0:T(8,128)(2,1)S(1)}, u32[]{:S(2)}, u32[]{:S(2)}) collective-permute-start(bf16[128,768]{1,0:T(8,128)(2,1)S(1)} %reshape.130), channel_id=1, source_target_pairs={{0,24},{8,0},{16,8},{24,16},{1,25},{9,1},{17,9},{25,17},{2,26},{10... | collective-permute-start | bytes 589832 | tf_op jit(solution)/shard_map/ppermute | solution.py:32
  82.0 6.0 %collective-permute-start.7 = (f32[3072]{0:T(1024)S(1)}, f32[3072]{0:T(1024)S(1)}, u32[]{:S(2)}, u32[]{:S(2)}) collective-permute-start(f32[3072]{0:T(1024)S(1)} %pad_maximum_fusion.8), channel_id=1, source_target_pairs={{0,8},{8,16},{16,24},{24,0},{1,9},{9,17},{17,25},{25,1},{2,10},{10... | collective-permute-start | bytes 36872 | tf_op jit(solution)/shard_map/ppermute | solution.py:32
  84.0 5.2 %collective-permute-start.8 = (f32[3072]{0:T(1024)S(1)}, f32[3072]{0:T(1024)S(1)}, u32[]{:S(2)}, u32[]{:S(2)}) collective-permute-start(f32[3072]{0:T(1024)S(1)} %pad_maximum_fusion.8), channel_id=1, source_target_pairs={{0,16},{8,24},{16,0},{24,8},{1,17},{9,25},{17,1},{25,9},{2,18},{10... | collective-permute-start | bytes 36872 | tf_op jit(solution)/shard_map/ppermute | solution.py:32
  101.1 27.4 %collective-permute-start.12 = (bf16[320,1920]{1,0:T(8,128)(2,1)}, bf16[320,1920]{1,0:T(8,128)(2,1)S(1)}, u32[]{:S(2)}, u32[]{:S(2)}) collective-permute-start(bf16[320,1920]{1,0:T(8,128)(2,1)} %copy.43), channel_id=1, source_target_pairs={{0,1},{1,0},{2,3},{3,2},{4,5},{5,4},{6,7},{7,6},{8,9},{9,8},{10,11... | collective-permute-start | bytes 3686408 | tf_op jit(solution)/shard_map/ppermute | solution.py:86
  101.1 30.6 %collective-permute-start.10 = (bf16[320,1920]{1,0:T(8,128)(2,1)}, bf16[320,1920]{1,0:T(8,128)(2,1)S(1)}, u32[]{:S(2)}, u32[]{:S(2)}) collective-permute-start(bf16[320,1920]{1,0:T(8,128)(2,1)} %copy.43), channel_id=1, source_target_pairs={{0,2},{1,3},{2,4},{3,5},{4,6},{5,7},{6,0},{7,1},{8,10},{9,11},{10,... | collective-permute-start | bytes 3686408 | tf_op jit(solution)/shard_map/ppermute | solution.py:86
  102.6 29.2 %collective-permute-start.11 = (bf16[320,1920]{1,0:T(8,128)(2,1)}, bf16[320,1920]{1,0:T(8,128)(2,1)S(1)}, u32[]{:S(2)}, u32[]{:S(2)}) collective-permute-start(bf16[320,1920]{1,0:T(8,128)(2,1)} %copy.43), channel_id=1, source_target_pairs={{0,6},{1,7},{2,0},{3,1},{4,2},{5,3},{6,4},{7,5},{8,14},{9,15},{10,... | collective-permute-start | bytes 3686408 | tf_op jit(solution)/shard_map/ppermute | solution.py:86
  128.4 40.9 %collective-permute-start.16 = (bf16[320,1920]{1,0:T(8,128)(2,1)S(1)}, bf16[320,1920]{1,0:T(8,128)(2,1)S(1)}, u32[]{:S(2)}, u32[]{:S(2)}) collective-permute-start(bf16[320,1920]{1,0:T(8,128)(2,1)S(1)} %collective-permute-done.12), channel_id=1, source_target_pairs={{0,2},{1,3},{2,4},{3,5},{4,6},{5,7},{6,0},{7,1},{8,10},{9,11},{10,... | collective-permute-start | bytes 3686408 | tf_op jit(solution)/shard_map/ppermute | solution.py:86
  128.8 40.5 %collective-permute-start.17 = (bf16[320,1920]{1,0:T(8,128)(2,1)S(1)}, bf16[320,1920]{1,0:T(8,128)(2,1)S(1)}, u32[]{:S(2)}, u32[]{:S(2)}) collective-permute-start(bf16[320,1920]{1,0:T(8,128)(2,1)S(1)} %collective-permute-done.12), channel_id=1, source_target_pairs={{0,6},{1,7},{2,0},{3,1},{4,2},{5,3},{6,4},{7,5},{8,14},{9,15},{10,... | collective-permute-start | bytes 3686408 | tf_op jit(solution)/shard_map/ppermute | solution.py:86
  131.7 37.4 %collective-permute-start.14 = (bf16[160,1920]{1,0:T(8,128)(2,1)S(1)}, bf16[160,1920]{1,0:T(8,128)(2,1)S(1)}, u32[]{:S(2)}, u32[]{:S(2)}) collective-permute-start(bf16[160,1920]{1,0:T(8,128)(2,1)S(1)} %slice.351), channel_id=1, source_target_pairs={{0,2},{1,3},{2,4},{3,5},{4,6},{5,7},{6,0},{7,1},{8,10},{9,11},{10,... | collective-permute-start | bytes 1843208 | tf_op jit(solution)/shard_map/ppermute | solution.py:86
  131.9 37.5 %collective-permute-start.15 = (bf16[160,1920]{1,0:T(8,128)(2,1)S(1)}, bf16[160,1920]{1,0:T(8,128)(2,1)S(1)}, u32[]{:S(2)}, u32[]{:S(2)}) collective-permute-start(bf16[160,1920]{1,0:T(8,128)(2,1)S(1)} %slice.352), channel_id=1, source_target_pairs={{0,6},{1,7},{2,0},{3,1},{4,2},{5,3},{6,4},{7,5},{8,14},{9,15},{10,... | collective-permute-start | bytes 1843208 | tf_op jit(solution)/shard_map/ppermute | solution.py:86
  141.6 77.2 %collective-permute-start.13 = (bf16[960,1920]{1,0:T(8,128)(2,1)}, bf16[960,1920]{1,0:T(8,128)(2,1)}, u32[]{:S(2)}, u32[]{:S(2)}) collective-permute-start(bf16[960,1920]{1,0:T(8,128)(2,1)} %pad_maximum_fusion), channel_id=1, source_target_pairs={{0,32},{32,0},{64,96},{96,64},{1,33},{33,1},{65,97},{97,65},{2,34}... | collective-permute-start | bytes 11059208 | tf_op jit(solution)/shard_map/ppermute | solution.py:89
  176.4 46.6 %collective-permute-start.18 = (bf16[960,1920]{1,0:T(8,128)(2,1)}, bf16[960,1920]{1,0:T(8,128)(2,1)}, u32[]{:S(2)}, u32[]{:S(2)}) collective-permute-start(bf16[960,1920]{1,0:T(8,128)(2,1)} %pad_maximum_fusion.1), channel_id=1, source_target_pairs={{0,32},{32,0},{64,96},{96,64},{1,33},{33,1},{65,97},{97,65},{2,34}... | collective-permute-start | bytes 11059208 | tf_op jit(solution)/shard_map/ppermute | solution.py:89
  186.0 16.7 %collective-permute-start.19 = (bf16[160,1920]{1,0:T(8,128)(2,1)S(1)}, bf16[160,1920]{1,0:T(8,128)(2,1)S(1)}, u32[]{:S(2)}, u32[]{:S(2)}) collective-permute-start(bf16[160,1920]{1,0:T(8,128)(2,1)S(1)} %collective-permute-done.14), channel_id=1, source_target_pairs={{0,1},{1,0},{2,3},{3,2},{4,5},{5,4},{6,7},{7,6},{8,9},{9,8},{10,11... | collective-permute-start | bytes 1843208 | tf_op jit(solution)/shard_map/ppermute | solution.py:86
  187.5 27.7 %collective-permute-start.20 = (bf16[160,1920]{1,0:T(8,128)(2,1)S(1)}, bf16[160,1920]{1,0:T(8,128)(2,1)S(1)}, u32[]{:S(2)}, u32[]{:S(2)}) collective-permute-start(bf16[160,1920]{1,0:T(8,128)(2,1)S(1)} %copy-done.14), channel_id=1, source_target_pairs={{0,1},{1,0},{2,3},{3,2},{4,5},{5,4},{6,7},{7,6},{8,9},{9,8},{10,11... | collective-permute-start | bytes 1843208 | tf_op jit(solution)/shard_map/ppermute | solution.py:86
  216.5 50.0 %collective-permute-start.21 = (bf16[320,1920]{1,0:T(8,128)(2,1)}, bf16[320,1920]{1,0:T(8,128)(2,1)}, u32[]{:S(2)}, u32[]{:S(2)}) collective-permute-start(bf16[320,1920]{1,0:T(8,128)(2,1)} %pad_maximum_fusion.4), channel_id=1, source_target_pairs={{0,32},{32,0},{64,96},{96,64},{1,33},{33,1},{65,97},{97,65},{2,34}... | collective-permute-start | bytes 3686408 | tf_op jit(solution)/shard_map/ppermute | solution.py:89
  275.7 44.3 %all-to-all-start = ((bf16[8,3,512,128]{2,3,1,0:T(8,128)(2,1)}), bf16[8,3,512,128]{2,3,1,0:T(8,128)(2,1)S(1)}, u32[]{:S(2)}, u32[]{:S(2)}) async-start(bf16[8,3,512,128]{2,3,1,0:T(8,128)(2,1)} %concatenate.137), calls=%async_computation | async-start | bytes 6291456 | tf_op jit(solution)/shard_map/all_to_all | solution.py:207
  (36 other events, 358.0 us)
Sparse Core Ops, SparseCore 0:
  17.5 59.8 all-gather.2
  93.0 55.8 all-gather.4

commit v5 on v4

--- a/solution.py
+++ b/solution.py
@@ -218,7 +218,7 @@
         return (accum / denom[:, None]).astype(jnp.bfloat16)
 
     queries = triple[:, 0]
-    chunks = 4
+    chunks = 16
     attended = lax.map(one_block, queries.reshape(chunks, -1, HDIM)).reshape(queries.shape)
     by_head = lax.all_to_all(attended, "ctx", 0, 0, tiled=True)[:heads_here]
     return by_head.transpose(1, 0, 2).reshape(group_rows, heads_here * HDIM)

time: 463 us -> 420 us (0.907)
  other arithmetic: 58.5 us -> 35.2 us
  matrix products: 105 us -> 86.3 us
    reduce_sum x4 -> x16, other arithmetic: 34.8 us -> 11.5 us  [one_block(): denom = jnp.sum(probs, -1)]
    dot_general x4 -> x16, matrix products: 36.7 us -> 24.1 us  [one_block(): jnp.dot(probs.astype(jnp.bfloat16), values, preferred_element_type=jnp.fl...]
    dot_general x4 -> x16, matrix products: 32.6 us -> 26 us  [one_block(): jnp.dot(query, keys.T, preferred_element_type=jnp.float32) * inv_root]
    unnamed x74 -> x76, local copies, waits for them, and re-layouts: 17.8 us -> 17.8 us
  transfers between devices with their start and end apart: 25 -> 25, of which waited for: 12 -> 12; matrix products, arithmetic and copies ran while one was open for 24% -> 27% of each run, Pallas kernels for 0% -> 0%
where the time goes in v5:
time: 420 us; the launch traced here: 415 us
  waiting for transfers between devices  141 us (34%)
  matrix products  86.3 us (21%)
  local copies, waits for them, and re-layouts  77.8 us (19%)
  starting transfers between devices  40 us (10%)
  other arithmetic  35.2 us (8%)
  blocking collectives  19.3 us (5%)
  between operations  15.4 us (4%)
    ppermute x9, waiting for transfers between devices, send(): return lax.ppermute(cells, 'ctx', [(i, step(i)) for i in range(n_ctx)])  76.1 us
    all_to_all x1, waiting for transfers between devices, shards(): triple = lax.all_to_all(outgoing, 'ctx', 0, 0, tiled=True)  38.9 us
    dot_general x16, matrix products, one_block(): jnp.dot(query, keys.T, preferred_element_type=jnp.float32) * inv_root  26 us
    dot_general x16, matrix products, one_block(): jnp.dot(probs.astype(jnp.bfloat16), values, preferred_element_type=jnp.fl...  24.1 us
    dot_general x3, matrix products, shards(): jnp.dot(jnp.concatenate(columns, 1), jnp.concatenate(weights, 0), preferr...  22.6 us
    all_to_all x1, blocking collectives, shards(): by_head = lax.all_to_all(attended, 'ctx', 0, 0, tiled=True)[:heads_here]  19.3 us
    unnamed x76, local copies, waits for them, and re-layouts  17.8 us
    concatenate x3, other arithmetic, shards(): jnp.concatenate([cells for cells, _, _ in s], 0)  14.7 us
  transfers between devices with their start and end apart: 25, of which 12 were waited for; matrix products, arithmetic and copies ran while one was open for 27% of the time, Pallas kernels for 0%

profile of v5, /device:TPU:0, one launch (start us, length us, event | category | flops | bytes accessed | tf_op | source)
XLA Modules:
  0.0 414.9 jit_solution(10599854205339496787)
XLA Ops:
  10.0 4.1 collective-permute-start
  22.6 3.5 collective-permute-start.2
  57.8 3.9 collective-permute-done.5
  63.6 13.8 %all-gather.3.cloned.1.call-done = bf16[774,1280]{0,1:T(8,128)(2,1)} async-done(((bf16[774,160]{0,1:T(8,128)(2,1)}), bf16[774,1280]{0,1:T(8,128)(2,1)}) %all-gather.3.cloned.1.call-update) | async-done | bytes 1981456 | tf_op jit(solution)/shard_map/all_gather | solution.py:157
  92.9 3.9 copy.42
  104.3 24.1 %collective-permute-done.12 = bf16[320,1920]{1,0:T(8,128)(2,1)S(1)} collective-permute-done((bf16[320,1920]{1,0:T(8,128)(2,1)}, bf16[320,1920]{1,0:T(8,128)(2,1)S(1)}, u32[]{:S(2)}, u32[]{:S(2)}) %collective-permute-start.12) | collective-permute-done | bytes 1228832 | tf_op jit(solution)/shard_map/ppermute | solution.py:86
  135.1 6.4 %pad_maximum_fusion = bf16[960,1920]{1,0:T(8,128)(2,1)} fusion(bf16[320,1920]{1,0:T(8,128)(2,1)S(1)} %collective-permute-done.12, bf16[320,1920]{1,0:T(8,128)(2,1)S(1)} %collective-permute-done.11, bf16[320,1920]{1,0:T(8,128)(2,1)S(1)} %collective-permute-done.10), kind=kLoop, calls=%fused_computation.33 | loop fusion | flops 11059200 | bytes 7372800 | tf_op jit(solution)/shard_map/concatenate | solution.py:114
  141.6 27.5 %collective-permute-done.14 = bf16[160,1920]{1,0:T(8,128)(2,1)S(1)} collective-permute-done((bf16[160,1920]{1,0:T(8,128)(2,1)S(1)}, bf16[160,1920]{1,0:T(8,128)(2,1)S(1)}, u32[]{:S(2)}, u32[]{:S(2)}) %collective-permute-start.14) | collective-permute-done | bytes 614432 | tf_op jit(solution)/shard_map/ppermute | solution.py:86
  169.4 7.1 %pad_maximum_fusion.1 = bf16[960,1920]{1,0:T(8,128)(2,1)} fusion(bf16[320,1920]{1,0:T(8,128)(2,1)S(1)} %collective-permute-done.17, bf16[320,1920]{1,0:T(8,128)(2,1)S(1)} %collective-permute-done.16, bf16[160,1920]{1,0:T(8,128)(2,1)S(1)} %collective-permute-done.15, bf16[160,1920]{1,0:T(8,128)(2,1)S(1)} %collective-permute-done.14), kind=kLoop, calls=%fused_computation.34 | loop fusion | flops 14745600 | bytes 7372800 | tf_op jit(solution)/shard_map/concatenate | solution.py:114
  190.9 11.7 %collective-permute-done.19 = bf16[160,1920]{1,0:T(8,128)(2,1)S(1)} collective-permute-done((bf16[160,1920]{1,0:T(8,128)(2,1)S(1)}, bf16[160,1920]{1,0:T(8,128)(2,1)S(1)}, u32[]{:S(2)}, u32[]{:S(2)}) %collective-permute-start.19) | collective-permute-done | bytes 614432 | tf_op jit(solution)/shard_map/ppermute | solution.py:86
  202.7 12.6 %collective-permute-done.20 = bf16[160,1920]{1,0:T(8,128)(2,1)S(1)} collective-permute-done((bf16[160,1920]{1,0:T(8,128)(2,1)S(1)}, bf16[160,1920]{1,0:T(8,128)(2,1)S(1)}, u32[]{:S(2)}, u32[]{:S(2)}) %collective-permute-start.20) | collective-permute-done | bytes 614432 | tf_op jit(solution)/shard_map/ppermute | solution.py:86
  218.8 4.2 %constant_dynamic-update-slice_fusion.9 = bf16[2560,1920]{1,0:T(8,128)(2,1)} fusion(bf16[2560,1920]{1,0:T(8,128)(2,1)} %constant_dynamic-update-slice_fusion.10, bf16[960,1920]{1,0:T(8,128)(2,1)} %collective-permute-done.13), kind=kLoop, calls=%fused_computation.176 | loop fusion | bytes 7372800 | tf_op jit(solution)/shard_map/concatenate | solution.py:198
  223.0 4.1 constant_dynamic-update-slice_fusion.14
  227.1 4.5 %constant_dynamic-slice_fusion.3 = (bf16[512,160]{1,0:T(8,128)(2,1)}, bf16[512,160]{1,0:T(8,128)(2,1)}, bf16[512,160]{1,0:T(8,128)(2,1)}, bf16[512,160]{1,0:T(8,...) fusion(bf16[512,5120]{1,0:T(8,128)(2,1)} %all-gather.5.cloned.1, ...), kind=kLoop, calls=%fused_computation.199 | loop fusion | bytes 2621472 | tf_op jit(solution)/shard_map/dynamic_slice | solution.py:192
  231.6 6.4 %constant_dynamic-slice_fusion.4 = (bf16[512,320]{1,0:T(8,128)(2,1)S(1)}, bf16[512,320]{1,0:T(8,128)(2,1)S(1)}, bf16[512,320]{1,0:T(8,128)(2,1)S(1)}, bf16[512,3...) fusion(bf16[512,5120]{1,0:T(8,128)(2,1)} %all-gather.5.cloned.1, ...), kind=kLoop, calls=%fused_computation.200 | loop fusion | bytes 6553640 | tf_op jit(solution)/shard_map/dynamic_slice | solution.py:192
  238.0 4.1 concatenate.131
  242.1 9.5 %fusion.152 = f32[512,1920]{1,0:T(8,128)} fusion(bf16[512,1920]{1,0:T(8,128)(2,1)S(1)} %concatenate.131, bf16[1920,1920]{1,0:T(8,128)(2,1)} %constant_dynamic-update-slice_fusion.14), kind=kOutput, calls=%fused_computation.260 | convolution fusion | flops 3774873600 | bytes 13271040 | tf_op jit(solution)/shard_map/dot_general | solution.py:196
  253.6 4.1 concatenate.128
  257.8 8.5 %fusion.151 = f32[512,1920]{1,0:T(8,128)S(1)} fusion(bf16[512,2560]{1,0:T(8,128)(2,1)S(1)} %concatenate.128, bf16[2560,1920]{1,0:T(8,128)(2,1)} %constant_dynamic-update-slice_fusion.9), kind=kOutput, calls=%fused_computation.259 | convolution fusion | flops 5033164800 | bytes 16384000 | tf_op jit(solution)/shard_map/dot_general | solution.py:196
  266.4 4.6 %add_convert_fusion = bf16[512,1920]{1,0:T(8,128)(2,1)} fusion(f32[512,1920]{1,0:T(8,128)S(1)} %fusion.151, f32[512,1920]{1,0:T(8,128)S(1)} %copy-done.31, bf16[320,1920]{1,0:T(8,128)(2,1)} %collective-permute-done.21, bf16[160,1920]{1,0:T(8,128)(2,1)S(1)} %copy-done.21, bf16[160,1920]{1,0:T(8,128)(2,1)S(1)} %copy-done.19, ...), kind=kOutput, calls=%fused_computation.16 | convolution fusion | flops 1271234560 | bytes 12943360 | tf_op jit(solution)/shard_map/dot_general | solution.py:196
  275.5 5.2 %all-to-all-start = ((bf16[8,3,512,128]{2,3,1,0:T(8,128)(2,1)}), bf16[8,3,512,128]{2,3,1,0:T(8,128)(2,1)S(1)}, u32[]{:S(2)}, u32[]{:S(2)}) async-start(bf16[8,3,512,128]{2,3,1,0:T(8,128)(2,1)} %concatenate.137), calls=%async_computation | async-start | bytes 6291456 | tf_op jit(solution)/shard_map/all_to_all | solution.py:207
  280.8 38.9 %all-to-all-done = bf16[8,3,512,128]{2,3,1,0:T(8,128)(2,1)S(1)} async-done(((bf16[8,3,512,128]{2,3,1,0:T(8,128)(2,1)}), bf16[8,3,512,128]{2,3,1,0:T(8,128)(2,1)S(1)}, u32[]{:S(2)}, u32[]{:S(2)}) %all-to-all-start) | async-done | bytes 3145760 | tf_op jit(solution)/shard_map/all_to_all | solution.py:207
  325.2 61.7 %while.10 = (s32[]{:T(128)}, bf16[16,256,128]{2,1,0:T(8,128)(2,1)}, bf16[16,256,128]{2,1,0:T(8,128)(2,1)}, bf16[4096,128]{1,0:T(8,128)(2,1)S(1)}, bf16[4096,128]{1,0:T(8,128)(2,1)S(1)}, /*index=5*/s32[]{:T(128)}) while((s32[]{:T(128)}, bf16[16,256,128]{2,1,0:T(8,128)(2,1)}, bf16[16,256,128]{2,1,0:T(8,128)(2,1)}, ...), condition=%wide.region_5.6_spmd, body=%wide.region_2.5_spmd.sunk | while | flops 543227648 | bytes 14819397 | solution.py:222
  386.9 19.3 %all_to_all.10 = bf16[8,512,128]{2,1,0:T(8,128)(2,1)S(1)} all-to-all(bf16[8,512,128]{2,1,0:T(8,128)(2,1)} %bitcast.134), channel_id=1, replica_groups=mesh['dp'=4,'head'=4,'ctx'=8] {'ctx'}, dimensions={0} | all-to-all | bytes 2097152 | tf_op jit(solution)/shard_map/all_to_all | solution.py:223
  (264 shorter events, 167.5 us)
Async XLA Ops:
  6.5 70.9 %all-gather.3.cloned.1.call-start = ((), (), s32[]{:S(2)}) async-start(), calls=%async_computation.2 | async-start | bytes 2580480 | tf_op jit(solution)/shard_map/all_gather | solution.py:157
  10.0 10.3 %collective-permute-start = (bf16[6,1,32,96]{3,2,1,0:T(8,128)(2,1)}, bf16[6,1,32,96]{3,2,1,0:T(8,128)(2,1)}, u32[]{:S(2)}, u32[]{:S(2)}) collective-permute-start(bf16[6,1,32,96]{3,2,1,0:T(8,128)(2,1)} %get-tuple-element.94), channel_id=1, source_target_pairs={{0,8},{8,16},{16,24},{1,9},{9,17},{17,25},{2,10},{10,18},{18,26},{... | collective-permute-start | bytes 110600 | tf_op jit(solution)/shard_map/ppermute | solution.py:19
  14.1 7.6 %collective-permute-start.1 = (bf16[6,1,32,96]{3,2,1,0:T(8,128)(2,1)S(1)}, bf16[6,1,32,96]{3,2,1,0:T(8,128)(2,1)}, u32[]{:S(2)}, u32[]{:S(2)}) collective-permute-start(bf16[6,1,32,96]{3,2,1,0:T(8,128)(2,1)S(1)} %get-tuple-element.93), channel_id=1, source_target_pairs={{8,0},{16,8},{24,16},{9,1},{17,9},{25,17},{10,2},{18,10},{26,18},{... | collective-permute-start | bytes 110600 | tf_op jit(solution)/shard_map/ppermute | solution.py:21
  17.4 209.8 %all-gather.5.cloned.1.call-start = ((), (), s32[]{:S(2)}) async-start(), calls=%async_computation.3 | async-start | bytes 6553600 | tf_op jit(solution)/shard_map/all_gather | solution.py:180
  22.6 5.8 %collective-permute-start.2 = (bf16[6,18,1,96]{3,2,1,0:T(2,128)(2,1)S(1)}, bf16[6,18,1,96]{3,2,1,0:T(2,128)(2,1)S(1)}, u32[]{:S(2)}, u32[]{:S(2)}) collective-permute-start(bf16[6,18,1,96]{3,2,1,0:T(2,128)(2,1)S(1)} %get-tuple-element.82), channel_id=1, source_target_pairs={{0,1},{1,2},{2,3},{3,4},{4,5},{5,6},{6,7},{8,9},{9,10},{10,11},{11... | collective-permute-start | bytes 62216 | tf_op jit(solution)/shard_map/ppermute | solution.py:19
  26.1 7.0 %collective-permute-start.3 = (bf16[6,18,1,96]{3,2,1,0:T(2,128)(2,1)S(1)}, bf16[6,18,1,96]{3,2,1,0:T(2,128)(2,1)S(1)}, u32[]{:S(2)}, u32[]{:S(2)}) collective-permute-start(bf16[6,18,1,96]{3,2,1,0:T(2,128)(2,1)S(1)} %get-tuple-element.83), channel_id=1, source_target_pairs={{1,0},{2,1},{3,2},{4,3},{5,4},{6,5},{7,6},{9,8},{10,9},{11,10},{12... | collective-permute-start | bytes 62216 | tf_op jit(solution)/shard_map/ppermute | solution.py:21
  48.7 9.1 %collective-permute-start.4 = (bf16[128,768]{1,0:T(8,128)(2,1)S(1)}, bf16[128,768]{1,0:T(8,128)(2,1)S(1)}, u32[]{:S(2)}, u32[]{:S(2)}) collective-permute-start(bf16[128,768]{1,0:T(8,128)(2,1)S(1)} %reshape.130), channel_id=1, source_target_pairs={{0,8},{8,16},{16,24},{24,0},{1,9},{9,17},{17,25},{25,1},{2,10},{10... | collective-permute-start | bytes 589832 | tf_op jit(solution)/shard_map/ppermute | solution.py:32
  51.4 10.3 %collective-permute-start.5 = (bf16[128,768]{1,0:T(8,128)(2,1)S(1)}, bf16[128,768]{1,0:T(8,128)(2,1)S(1)}, u32[]{:S(2)}, u32[]{:S(2)}) collective-permute-start(bf16[128,768]{1,0:T(8,128)(2,1)S(1)} %reshape.130), channel_id=1, source_target_pairs={{0,16},{8,24},{16,0},{24,8},{1,17},{9,25},{17,1},{25,9},{2,18},{10... | collective-permute-start | bytes 589832 | tf_op jit(solution)/shard_map/ppermute | solution.py:32
  54.2 7.5 %collective-permute-start.6 = (bf16[128,768]{1,0:T(8,128)(2,1)S(1)}, bf16[128,768]{1,0:T(8,128)(2,1)S(1)}, u32[]{:S(2)}, u32[]{:S(2)}) collective-permute-start(bf16[128,768]{1,0:T(8,128)(2,1)S(1)} %reshape.130), channel_id=1, source_target_pairs={{0,24},{8,0},{16,8},{24,16},{1,25},{9,1},{17,9},{25,17},{2,26},{10... | collective-permute-start | bytes 589832 | tf_op jit(solution)/shard_map/ppermute | solution.py:32
  82.0 6.0 %collective-permute-start.7 = (f32[3072]{0:T(1024)S(1)}, f32[3072]{0:T(1024)S(1)}, u32[]{:S(2)}, u32[]{:S(2)}) collective-permute-start(f32[3072]{0:T(1024)S(1)} %pad_maximum_fusion.8), channel_id=1, source_target_pairs={{0,8},{8,16},{16,24},{24,0},{1,9},{9,17},{17,25},{25,1},{2,10},{10... | collective-permute-start | bytes 36872 | tf_op jit(solution)/shard_map/ppermute | solution.py:32
  84.0 5.2 %collective-permute-start.8 = (f32[3072]{0:T(1024)S(1)}, f32[3072]{0:T(1024)S(1)}, u32[]{:S(2)}, u32[]{:S(2)}) collective-permute-start(f32[3072]{0:T(1024)S(1)} %pad_maximum_fusion.8), channel_id=1, source_target_pairs={{0,16},{8,24},{16,0},{24,8},{1,17},{9,25},{17,1},{25,9},{2,18},{10... | collective-permute-start | bytes 36872 | tf_op jit(solution)/shard_map/ppermute | solution.py:32
  101.1 27.4 %collective-permute-start.12 = (bf16[320,1920]{1,0:T(8,128)(2,1)}, bf16[320,1920]{1,0:T(8,128)(2,1)S(1)}, u32[]{:S(2)}, u32[]{:S(2)}) collective-permute-start(bf16[320,1920]{1,0:T(8,128)(2,1)} %copy.43), channel_id=1, source_target_pairs={{0,1},{1,0},{2,3},{3,2},{4,5},{5,4},{6,7},{7,6},{8,9},{9,8},{10,11... | collective-permute-start | bytes 3686408 | tf_op jit(solution)/shard_map/ppermute | solution.py:86
  101.1 30.6 %collective-permute-start.10 = (bf16[320,1920]{1,0:T(8,128)(2,1)}, bf16[320,1920]{1,0:T(8,128)(2,1)S(1)}, u32[]{:S(2)}, u32[]{:S(2)}) collective-permute-start(bf16[320,1920]{1,0:T(8,128)(2,1)} %copy.43), channel_id=1, source_target_pairs={{0,2},{1,3},{2,4},{3,5},{4,6},{5,7},{6,0},{7,1},{8,10},{9,11},{10,... | collective-permute-start | bytes 3686408 | tf_op jit(solution)/shard_map/ppermute | solution.py:86
  102.6 29.2 %collective-permute-start.11 = (bf16[320,1920]{1,0:T(8,128)(2,1)}, bf16[320,1920]{1,0:T(8,128)(2,1)S(1)}, u32[]{:S(2)}, u32[]{:S(2)}) collective-permute-start(bf16[320,1920]{1,0:T(8,128)(2,1)} %copy.43), channel_id=1, source_target_pairs={{0,6},{1,7},{2,0},{3,1},{4,2},{5,3},{6,4},{7,5},{8,14},{9,15},{10,... | collective-permute-start | bytes 3686408 | tf_op jit(solution)/shard_map/ppermute | solution.py:86
  128.4 40.9 %collective-permute-start.16 = (bf16[320,1920]{1,0:T(8,128)(2,1)S(1)}, bf16[320,1920]{1,0:T(8,128)(2,1)S(1)}, u32[]{:S(2)}, u32[]{:S(2)}) collective-permute-start(bf16[320,1920]{1,0:T(8,128)(2,1)S(1)} %collective-permute-done.12), channel_id=1, source_target_pairs={{0,2},{1,3},{2,4},{3,5},{4,6},{5,7},{6,0},{7,1},{8,10},{9,11},{10,... | collective-permute-start | bytes 3686408 | tf_op jit(solution)/shard_map/ppermute | solution.py:86
  128.8 40.5 %collective-permute-start.17 = (bf16[320,1920]{1,0:T(8,128)(2,1)S(1)}, bf16[320,1920]{1,0:T(8,128)(2,1)S(1)}, u32[]{:S(2)}, u32[]{:S(2)}) collective-permute-start(bf16[320,1920]{1,0:T(8,128)(2,1)S(1)} %collective-permute-done.12), channel_id=1, source_target_pairs={{0,6},{1,7},{2,0},{3,1},{4,2},{5,3},{6,4},{7,5},{8,14},{9,15},{10,... | collective-permute-start | bytes 3686408 | tf_op jit(solution)/shard_map/ppermute | solution.py:86
  131.7 37.4 %collective-permute-start.14 = (bf16[160,1920]{1,0:T(8,128)(2,1)S(1)}, bf16[160,1920]{1,0:T(8,128)(2,1)S(1)}, u32[]{:S(2)}, u32[]{:S(2)}) collective-permute-start(bf16[160,1920]{1,0:T(8,128)(2,1)S(1)} %slice.351), channel_id=1, source_target_pairs={{0,2},{1,3},{2,4},{3,5},{4,6},{5,7},{6,0},{7,1},{8,10},{9,11},{10,... | collective-permute-start | bytes 1843208 | tf_op jit(solution)/shard_map/ppermute | solution.py:86
  131.9 37.5 %collective-permute-start.15 = (bf16[160,1920]{1,0:T(8,128)(2,1)S(1)}, bf16[160,1920]{1,0:T(8,128)(2,1)S(1)}, u32[]{:S(2)}, u32[]{:S(2)}) collective-permute-start(bf16[160,1920]{1,0:T(8,128)(2,1)S(1)} %slice.352), channel_id=1, source_target_pairs={{0,6},{1,7},{2,0},{3,1},{4,2},{5,3},{6,4},{7,5},{8,14},{9,15},{10,... | collective-permute-start | bytes 1843208 | tf_op jit(solution)/shard_map/ppermute | solution.py:86
  141.6 77.2 %collective-permute-start.13 = (bf16[960,1920]{1,0:T(8,128)(2,1)}, bf16[960,1920]{1,0:T(8,128)(2,1)}, u32[]{:S(2)}, u32[]{:S(2)}) collective-permute-start(bf16[960,1920]{1,0:T(8,128)(2,1)} %pad_maximum_fusion), channel_id=1, source_target_pairs={{0,32},{32,0},{64,96},{96,64},{1,33},{33,1},{65,97},{97,65},{2,34}... | collective-permute-start | bytes 11059208 | tf_op jit(solution)/shard_map/ppermute | solution.py:89
  176.4 46.6 %collective-permute-start.18 = (bf16[960,1920]{1,0:T(8,128)(2,1)}, bf16[960,1920]{1,0:T(8,128)(2,1)}, u32[]{:S(2)}, u32[]{:S(2)}) collective-permute-start(bf16[960,1920]{1,0:T(8,128)(2,1)} %pad_maximum_fusion.1), channel_id=1, source_target_pairs={{0,32},{32,0},{64,96},{96,64},{1,33},{33,1},{65,97},{97,65},{2,34}... | collective-permute-start | bytes 11059208 | tf_op jit(solution)/shard_map/ppermute | solution.py:89
  186.0 16.7 %collective-permute-start.19 = (bf16[160,1920]{1,0:T(8,128)(2,1)S(1)}, bf16[160,1920]{1,0:T(8,128)(2,1)S(1)}, u32[]{:S(2)}, u32[]{:S(2)}) collective-permute-start(bf16[160,1920]{1,0:T(8,128)(2,1)S(1)} %collective-permute-done.14), channel_id=1, source_target_pairs={{0,1},{1,0},{2,3},{3,2},{4,5},{5,4},{6,7},{7,6},{8,9},{9,8},{10,11... | collective-permute-start | bytes 1843208 | tf_op jit(solution)/shard_map/ppermute | solution.py:86
  187.5 27.7 %collective-permute-start.20 = (bf16[160,1920]{1,0:T(8,128)(2,1)S(1)}, bf16[160,1920]{1,0:T(8,128)(2,1)S(1)}, u32[]{:S(2)}, u32[]{:S(2)}) collective-permute-start(bf16[160,1920]{1,0:T(8,128)(2,1)S(1)} %copy-done.15), channel_id=1, source_target_pairs={{0,1},{1,0},{2,3},{3,2},{4,5},{5,4},{6,7},{7,6},{8,9},{9,8},{10,11... | collective-permute-start | bytes 1843208 | tf_op jit(solution)/shard_map/ppermute | solution.py:86
  216.5 49.8 %collective-permute-start.21 = (bf16[320,1920]{1,0:T(8,128)(2,1)}, bf16[320,1920]{1,0:T(8,128)(2,1)}, u32[]{:S(2)}, u32[]{:S(2)}) collective-permute-start(bf16[320,1920]{1,0:T(8,128)(2,1)} %pad_maximum_fusion.4), channel_id=1, source_target_pairs={{0,32},{32,0},{64,96},{96,64},{1,33},{33,1},{65,97},{97,65},{2,34}... | collective-permute-start | bytes 3686408 | tf_op jit(solution)/shard_map/ppermute | solution.py:89
  275.5 44.1 %all-to-all-start = ((bf16[8,3,512,128]{2,3,1,0:T(8,128)(2,1)}), bf16[8,3,512,128]{2,3,1,0:T(8,128)(2,1)S(1)}, u32[]{:S(2)}, u32[]{:S(2)}) async-start(bf16[8,3,512,128]{2,3,1,0:T(8,128)(2,1)} %concatenate.137), calls=%async_computation | async-start | bytes 6291456 | tf_op jit(solution)/shard_map/all_to_all | solution.py:207
  (33 other events, 324.5 us)
Sparse Core Ops, SparseCore 0:
  17.5 59.8 all-gather.2
  93.0 55.8 all-gather.4

commit v6 on v3

--- a/solution.py
+++ b/solution.py
@@ -217,7 +217,7 @@
         accum = jnp.dot(probs.astype(jnp.bfloat16), values, preferred_element_type=jnp.float32)
         return (accum / denom[:, None]).astype(jnp.bfloat16)
 
-    attended = lax.map(one_block, triple[:, 0])
+    attended = jnp.stack([one_block(triple[s, 0]) for s in range(triple.shape[0])])
     by_head = lax.all_to_all(attended, "ctx", 0, 0, tiled=True)[:heads_here]
     return by_head.transpose(1, 0, 2).reshape(group_rows, heads_here * HDIM)
 

time: 405 us -> 444 us (1.096)
  blocking collectives: 19.3 us -> 61.7 us
  waiting for transfers between devices: 141 us -> 104 us
  matrix products: 66.3 us -> 100 us
  other arithmetic: 35.7 us -> 51.5 us
  local copies, waits for them, and re-layouts: 82.5 us -> 72.7 us
  starting transfers between devices: 40.5 us -> 33.3 us
    all_to_all x0 -> x1, blocking collectives: none -> 43.7 us  [shards(): triple = lax.all_to_all(outgoing, 'ctx', 0, 0, tiled=True)]
    all_to_all x1 -> x0, waiting for transfers between devices: 38.9 us -> none  [shards(): triple = lax.all_to_all(outgoing, 'ctx', 0, 0, tiled=True)]
    dot_general x8, matrix products: 12 us -> 29.4 us  [one_block(): jnp.dot(probs.astype(jnp.bfloat16), values, preferred_element_type=jnp.fl...]
    reduce_sum x8, other arithmetic: 12.1 us -> 28.9 us  [one_block(): denom = jnp.sum(probs, -1)]
    dot_general x8, matrix products: 18.2 us -> 34 us  [one_block(): jnp.dot(query, keys.T, preferred_element_type=jnp.float32) * inv_root]
    dynamic_update_slice x16 -> x0, local copies, waits for them, and re-layouts: 6.27 us -> none  [shards(): attended = lax.map(one_block, triple[:, 0])]
    all_to_all x1 -> x0, starting transfers between devices: 5.75 us -> none  [shards(): triple = lax.all_to_all(outgoing, 'ctx', 0, 0, tiled=True)]
    unnamed x74 -> x72, local copies, waits for them, and re-layouts: 17.8 us -> 18.2 us
  transfers between devices with their start and end apart: 25 -> 24, of which waited for: 12 -> 11; matrix products, arithmetic and copies ran while one was open for 28% -> 25% of each run, Pallas kernels for 0% -> 0%
where the time goes in v6:
time: 444 us; the launch traced here: 439 us
  waiting for transfers between devices  104 us (23%)
  matrix products  100 us (23%)
  local copies, waits for them, and re-layouts  72.7 us (16%)
  blocking collectives  61.7 us (14%)
  other arithmetic  51.5 us (12%)
  starting transfers between devices  33.3 us (7%)
  between operations  15.4 us (3%)
    ppermute x9, waiting for transfers between devices, send(): return lax.ppermute(cells, 'ctx', [(i, step(i)) for i in range(n_ctx)])  76 us
    all_to_all x1, blocking collectives, shards(): triple = lax.all_to_all(outgoing, 'ctx', 0, 0, tiled=True)  43.7 us
    dot_general x8, matrix products, one_block(): jnp.dot(query, keys.T, preferred_element_type=jnp.float32) * inv_root  34 us
    dot_general x8, matrix products, one_block(): jnp.dot(probs.astype(jnp.bfloat16), values, preferred_element_type=jnp.fl...  29.4 us
    reduce_sum x8, other arithmetic, one_block(): denom = jnp.sum(probs, -1)  28.9 us
    dot_general x3, matrix products, shards(): jnp.dot(jnp.concatenate(columns, 1), jnp.concatenate(weights, 0), preferr...  22.6 us
    unnamed x72, local copies, waits for them, and re-layouts  18.2 us
    all_to_all x1, blocking collectives, shards(): by_head = lax.all_to_all(attended, 'ctx', 0, 0, tiled=True)[:heads_here]  18 us
  transfers between devices with their start and end apart: 24, of which 11 were waited for; matrix products, arithmetic and copies ran while one was open for 25% of the time, Pallas kernels for 0%

profile of v6, /device:TPU:0, one launch (start us, length us, event | category | flops | bytes accessed | tf_op | source)
XLA Modules:
  0.0 439.3 jit_solution(871707725037760021)
XLA Ops:
  22.2 5.0 %collective-permute-start.2 = (bf16[6,18,1,96]{3,2,1,0:T(2,128)(2,1)S(1)}, bf16[6,18,1,96]{3,2,1,0:T(2,128)(2,1)S(1)}, u32[]{:S(2)}, u32[]{:S(2)}) collective-permute-start(bf16[6,18,1,96]{3,2,1,0:T(2,128)(2,1)S(1)} %get-tuple-element.41), channel_id=1, source_target_pairs={{0,1},{1,2},{2,3},{3,4},{4,5},{5,6},{6,7},{8,9},{9,10},{10,11},{11... | collective-permute-start | bytes 62216 | tf_op jit(solution)/shard_map/ppermute | solution.py:19
  51.3 5.3 %collective-permute-done.6 = bf16[128,768]{1,0:T(8,128)(2,1)S(1)} collective-permute-done((bf16[128,768]{1,0:T(8,128)(2,1)S(1)}, bf16[128,768]{1,0:T(8,128)(2,1)S(1)}, u32[]{:S(2)}, u32[]{:S(2)}) %collective-permute-start.6) | collective-permute-done | bytes 196640 | tf_op jit(solution)/shard_map/ppermute | solution.py:32
  62.1 15.2 %all-gather.3.cloned.1.call-done = bf16[774,1280]{0,1:T(8,128)(2,1)} async-done(((bf16[774,160]{0,1:T(8,128)(2,1)}), bf16[774,1280]{0,1:T(8,128)(2,1)}) %all-gather.3.cloned.1.call-update) | async-done | bytes 1981456 | tf_op jit(solution)/shard_map/all_gather | solution.py:157
  104.2 23.8 %collective-permute-done.12 = bf16[320,1920]{1,0:T(8,128)(2,1)S(1)} collective-permute-done((bf16[320,1920]{1,0:T(8,128)(2,1)}, bf16[320,1920]{1,0:T(8,128)(2,1)S(1)}, u32[]{:S(2)}, u32[]{:S(2)}) %collective-permute-start.12) | collective-permute-done | bytes 1228832 | tf_op jit(solution)/shard_map/ppermute | solution.py:86
  134.7 6.4 %pad_maximum_fusion = bf16[960,1920]{1,0:T(8,128)(2,1)} fusion(bf16[320,1920]{1,0:T(8,128)(2,1)S(1)} %collective-permute-done.12, bf16[320,1920]{1,0:T(8,128)(2,1)S(1)} %collective-permute-done.11, bf16[320,1920]{1,0:T(8,128)(2,1)S(1)} %collective-permute-done.10), kind=kLoop, calls=%fused_computation.59 | loop fusion | flops 11059200 | bytes 7372800 | tf_op jit(solution)/shard_map/concatenate | solution.py:114
  141.2 27.5 %collective-permute-done.14 = bf16[160,1920]{1,0:T(8,128)(2,1)S(1)} collective-permute-done((bf16[160,1920]{1,0:T(8,128)(2,1)S(1)}, bf16[160,1920]{1,0:T(8,128)(2,1)S(1)}, u32[]{:S(2)}, u32[]{:S(2)}) %collective-permute-start.14) | collective-permute-done | bytes 614432 | tf_op jit(solution)/shard_map/ppermute | solution.py:86
  169.0 7.1 %pad_maximum_fusion.1 = bf16[960,1920]{1,0:T(8,128)(2,1)} fusion(bf16[320,1920]{1,0:T(8,128)(2,1)S(1)} %collective-permute-done.17, bf16[320,1920]{1,0:T(8,128)(2,1)S(1)} %collective-permute-done.16, bf16[160,1920]{1,0:T(8,128)(2,1)S(1)} %collective-permute-done.15, bf16[160,1920]{1,0:T(8,128)(2,1)S(1)} %collective-permute-done.14), kind=kLoop, calls=%fused_computation.60 | loop fusion | flops 14745600 | bytes 7372800 | tf_op jit(solution)/shard_map/concatenate | solution.py:114
  190.0 11.7 %collective-permute-done.20 = bf16[160,1920]{1,0:T(8,128)(2,1)S(1)} collective-permute-done((bf16[160,1920]{1,0:T(8,128)(2,1)S(1)}, bf16[160,1920]{1,0:T(8,128)(2,1)S(1)}, u32[]{:S(2)}, u32[]{:S(2)}) %collective-permute-start.20) | collective-permute-done | bytes 614432 | tf_op jit(solution)/shard_map/ppermute | solution.py:86
  201.7 12.7 %collective-permute-done.19 = bf16[160,1920]{1,0:T(8,128)(2,1)S(1)} collective-permute-done((bf16[160,1920]{1,0:T(8,128)(2,1)S(1)}, bf16[160,1920]{1,0:T(8,128)(2,1)S(1)}, u32[]{:S(2)}, u32[]{:S(2)}) %collective-permute-start.19) | collective-permute-done | bytes 614432 | tf_op jit(solution)/shard_map/ppermute | solution.py:86
  230.6 6.4 %constant_dynamic-slice_fusion.4 = (bf16[512,320]{1,0:T(8,128)(2,1)S(1)}, bf16[512,320]{1,0:T(8,128)(2,1)S(1)}, bf16[512,320]{1,0:T(8,128)(2,1)S(1)}, bf16[512,3...) fusion(bf16[512,5120]{1,0:T(8,128)(2,1)} %all-gather.5.cloned.1, ...), kind=kLoop, calls=%fused_computation.274 | loop fusion | bytes 6553640 | tf_op jit(solution)/shard_map/dynamic_slice | solution.py:192
  241.3 9.5 %fusion.275 = f32[512,1920]{1,0:T(8,128)} fusion(bf16[512,1920]{1,0:T(8,128)(2,1)S(1)} %concatenate.131, bf16[1920,1920]{1,0:T(8,128)(2,1)} %constant_dynamic-update-slice_fusion.14), kind=kOutput, calls=%fused_computation.349 | convolution fusion | flops 3774873600 | bytes 13271040 | tf_op jit(solution)/shard_map/dot_general | solution.py:196
  257.0 8.5 %fusion.274 = f32[512,1920]{1,0:T(8,128)S(1)} fusion(bf16[512,2560]{1,0:T(8,128)(2,1)S(1)} %concatenate.128, bf16[2560,1920]{1,0:T(8,128)(2,1)} %constant_dynamic-update-slice_fusion.9), kind=kOutput, calls=%fused_computation.348 | convolution fusion | flops 5033164800 | bytes 16384000 | tf_op jit(solution)/shard_map/dot_general | solution.py:196
  273.2 43.7 %all_to_all.10 = bf16[8,3,512,128]{2,3,1,0:T(8,128)(2,1)S(1)} all-to-all(bf16[8,3,512,128]{2,3,1,0:T(8,128)(2,1)S(1)} %concatenate.137), channel_id=1, replica_groups=mesh['dp'=4,'head'=4,'ctx'=8] {'ctx'}, dimensions={0} | all-to-all | bytes 6291456 | tf_op jit(solution)/shard_map/all_to_all | solution.py:207
  320.2 5.4 %multiply_reduce_fusion.7 = (f32[512]{0:T(512)S(1)}, f32[512,4096]{1,0:T(8,128)}) fusion(bf16[4096,128]{1,0:T(8,128)(2,1)S(1)} %bitcast.200, bf16[8,3,512,128]{2,3,1,0:T(8,128)(2,1)} %copy-done.2), kind=kOutput, calls=%fused_computation.17 | convolution fusion | flops 541064704 | bytes 9570304 | tf_op jit(solution)/shard_map/dot_general | solution.py:213
  325.7 5.4 %multiply_reduce_fusion.6 = (f32[512]{0:T(512)S(1)}, f32[512,4096]{1,0:T(8,128)}) fusion(bf16[4096,128]{1,0:T(8,128)(2,1)S(1)} %bitcast.201, bf16[8,3,512,128]{2,3,1,0:T(8,128)(2,1)} %copy-done.2), kind=kOutput, calls=%fused_computation.16 | convolution fusion | flops 541064704 | bytes 9570304 | tf_op jit(solution)/shard_map/dot_general | solution.py:213
  331.1 5.4 %multiply_reduce_fusion.5 = (f32[512]{0:T(512)S(1)}, f32[512,4096]{1,0:T(8,128)}) fusion(bf16[4096,128]{1,0:T(8,128)(2,1)S(1)} %bitcast.202, bf16[8,3,512,128]{2,3,1,0:T(8,128)(2,1)} %copy-done.2), kind=kOutput, calls=%fused_computation.15 | convolution fusion | flops 541064704 | bytes 9570304 | tf_op jit(solution)/shard_map/dot_general | solution.py:213
  336.6 5.4 %multiply_reduce_fusion.4 = (f32[512]{0:T(512)S(1)}, f32[512,4096]{1,0:T(8,128)}) fusion(bf16[4096,128]{1,0:T(8,128)(2,1)S(1)} %bitcast.203, bf16[8,3,512,128]{2,3,1,0:T(8,128)(2,1)} %copy-done.2), kind=kOutput, calls=%fused_computation.14 | convolution fusion | flops 541064704 | bytes 9570304 | tf_op jit(solution)/shard_map/dot_general | solution.py:213
  342.0 5.4 %multiply_reduce_fusion.3 = (f32[512]{0:T(512)S(1)}, f32[512,4096]{1,0:T(8,128)}) fusion(bf16[4096,128]{1,0:T(8,128)(2,1)S(1)} %bitcast.204, bf16[8,3,512,128]{2,3,1,0:T(8,128)(2,1)} %copy-done.2), kind=kOutput, calls=%fused_computation.13 | convolution fusion | flops 541064704 | bytes 9570304 | tf_op jit(solution)/shard_map/dot_general | solution.py:213
  354.3 4.9 %fusion = f32[512]{0:T(512)S(1)} fusion(f32[512,4096]{1,0:T(8,128)} %get-tuple-element.68, f32[512]{0:T(512)S(1)} %broadcast_maximum_fusion.7), kind=kLoop, calls=%fused_computation.18 | loop fusion | flops 6290944 | bytes 8392704 | tf_op jit(solution)/shard_map/reduce_sum | solution.py:216
  359.1 5.0 %fusion.106 = bf16[8,512,128]{2,1,0:T(8,128)(2,1)S(1)} fusion(bf16[4096,128]{1,0:T(8,128)(2,1)S(1)} %bitcast.214, f32[512,4096]{1,0:T(8,128)} %get-tuple-element.68, f32[512]{0:T(512)S(1)} %broadcast_maximum_fusion.7, f32[512]{0:T(512)S(1)} %fusion), kind=kOutput, calls=%fused_computation.132 | convolution fusion | flops 543293440 | bytes 9572352 | tf_op jit(solution)/shard_map/dot_general | solution.py:217
  373.9 4.9 %fusion.4 = f32[512]{0:T(512)S(1)} fusion(f32[512,4096]{1,0:T(8,128)} %get-tuple-element.72, f32[512]{0:T(512)S(1)} %broadcast_maximum_fusion.5), kind=kLoop, calls=%fused_computation.22 | loop fusion | flops 6290944 | bytes 8392704 | tf_op jit(solution)/shard_map/reduce_sum | solution.py:216
  383.7 4.9 %fusion.6 = f32[512]{0:T(512)S(1)} fusion(f32[512,4096]{1,0:T(8,128)} %get-tuple-element.74, f32[512]{0:T(512)S(1)} %broadcast_maximum_fusion.4), kind=kLoop, calls=%fused_computation.24 | loop fusion | flops 6290944 | bytes 8392704 | tf_op jit(solution)/shard_map/reduce_sum | solution.py:216
  398.3 5.1 %fusion.154 = bf16[8,512,128]{2,1,0:T(8,128)(2,1)S(1)} fusion(bf16[8,512,128]{2,1,0:T(8,128)(2,1)S(1)} %fusion.142, bf16[4096,128]{1,0:T(8,128)(2,1)S(1)} %bitcast.218, f32[512,4096]{1,0:T(8,128)} %get-tuple-element.76, f32[512]{0:T(512)S(1)} %broadcast_maximum_fusion.3, f32[512]{0:T(512)S(1)} %fusion.8), kind=kOutput, calls=%fused_computation.148 | convolution fusion | flops 543293440 | bytes 9572352 | tf_op jit(solution)/shard_map/dot_general | solution.py:217
  412.6 18.0 %all_to_all.11 = bf16[8,512,128]{2,1,0:T(8,128)(2,1)S(1)} all-to-all(bf16[8,512,128]{2,1,0:T(8,128)(2,1)S(1)} %fusion.190), channel_id=1, replica_groups=mesh['dp'=4,'head'=4,'ctx'=8] {'ctx'}, dimensions={0} | all-to-all | bytes 2097152 | tf_op jit(solution)/shard_map/all_to_all | solution.py:221
  (224 shorter events, 171.1 us)
Async XLA Ops:
  6.5 70.8 %all-gather.3.cloned.1.call-start = ((), (), s32[]{:S(2)}) async-start(), calls=%async_computation.2 | async-start | bytes 2580480 | tf_op jit(solution)/shard_map/all_gather | solution.py:157
  10.0 10.3 %collective-permute-start = (bf16[6,1,32,96]{3,2,1,0:T(8,128)(2,1)}, bf16[6,1,32,96]{3,2,1,0:T(8,128)(2,1)S(1)}, u32[]{:S(2)}, u32[]{:S(2)}) collective-permute-start(bf16[6,1,32,96]{3,2,1,0:T(8,128)(2,1)} %get-tuple-element.53), channel_id=1, source_target_pairs={{0,8},{8,16},{16,24},{1,9},{9,17},{17,25},{2,10},{10,18},{18,26},{... | collective-permute-start | bytes 110600 | tf_op jit(solution)/shard_map/ppermute | solution.py:19
  13.5 7.3 %collective-permute-start.1 = (bf16[6,1,32,96]{3,2,1,0:T(8,128)(2,1)S(1)}, bf16[6,1,32,96]{3,2,1,0:T(8,128)(2,1)S(1)}, u32[]{:S(2)}, u32[]{:S(2)}) collective-permute-start(bf16[6,1,32,96]{3,2,1,0:T(8,128)(2,1)S(1)} %get-tuple-element.52), channel_id=1, source_target_pairs={{8,0},{16,8},{24,16},{9,1},{17,9},{25,17},{10,2},{18,10},{26,18},{... | collective-permute-start | bytes 110600 | tf_op jit(solution)/shard_map/ppermute | solution.py:21
  17.7 208.5 %all-gather.5.cloned.1.call-start = ((), (), s32[]{:S(2)}) async-start(), calls=%async_computation.3 | async-start | bytes 6553600 | tf_op jit(solution)/shard_map/all_gather | solution.py:180
  20.9 6.8 %collective-permute-start.3 = (bf16[6,18,1,96]{3,2,1,0:T(2,128)(2,1)S(1)}, bf16[6,18,1,96]{3,2,1,0:T(2,128)(2,1)S(1)}, u32[]{:S(2)}, u32[]{:S(2)}) collective-permute-start(bf16[6,18,1,96]{3,2,1,0:T(2,128)(2,1)S(1)} %get-tuple-element.42), channel_id=1, source_target_pairs={{1,0},{2,1},{3,2},{4,3},{5,4},{6,5},{7,6},{9,8},{10,9},{11,10},{12... | collective-permute-start | bytes 62216 | tf_op jit(solution)/shard_map/ppermute | solution.py:21
  22.2 7.8 %collective-permute-start.2 = (bf16[6,18,1,96]{3,2,1,0:T(2,128)(2,1)S(1)}, bf16[6,18,1,96]{3,2,1,0:T(2,128)(2,1)S(1)}, u32[]{:S(2)}, u32[]{:S(2)}) collective-permute-start(bf16[6,18,1,96]{3,2,1,0:T(2,128)(2,1)S(1)} %get-tuple-element.41), channel_id=1, source_target_pairs={{0,1},{1,2},{2,3},{3,4},{4,5},{5,6},{6,7},{8,9},{9,10},{10,11},{11... | collective-permute-start | bytes 62216 | tf_op jit(solution)/shard_map/ppermute | solution.py:19
  45.4 11.2 %collective-permute-start.6 = (bf16[128,768]{1,0:T(8,128)(2,1)S(1)}, bf16[128,768]{1,0:T(8,128)(2,1)S(1)}, u32[]{:S(2)}, u32[]{:S(2)}) collective-permute-start(bf16[128,768]{1,0:T(8,128)(2,1)S(1)} %reshape.155), channel_id=1, source_target_pairs={{0,24},{8,0},{16,8},{24,16},{1,25},{9,1},{17,9},{25,17},{2,26},{10... | collective-permute-start | bytes 589832 | tf_op jit(solution)/shard_map/ppermute | solution.py:32
  49.4 8.9 %collective-permute-start.5 = (bf16[128,768]{1,0:T(8,128)(2,1)S(1)}, bf16[128,768]{1,0:T(8,128)(2,1)S(1)}, u32[]{:S(2)}, u32[]{:S(2)}) collective-permute-start(bf16[128,768]{1,0:T(8,128)(2,1)S(1)} %reshape.155), channel_id=1, source_target_pairs={{0,16},{8,24},{16,0},{24,8},{1,17},{9,25},{17,1},{25,9},{2,18},{10... | collective-permute-start | bytes 589832 | tf_op jit(solution)/shard_map/ppermute | solution.py:32
  50.2 10.2 %collective-permute-start.4 = (bf16[128,768]{1,0:T(8,128)(2,1)S(1)}, bf16[128,768]{1,0:T(8,128)(2,1)S(1)}, u32[]{:S(2)}, u32[]{:S(2)}) collective-permute-start(bf16[128,768]{1,0:T(8,128)(2,1)S(1)} %reshape.155), channel_id=1, source_target_pairs={{0,8},{8,16},{16,24},{24,0},{1,9},{9,17},{17,25},{25,1},{2,10},{10... | collective-permute-start | bytes 589832 | tf_op jit(solution)/shard_map/ppermute | solution.py:32
  81.9 4.5 %collective-permute-start.9 = (f32[3072]{0:T(1024)S(1)}, f32[3072]{0:T(1024)S(1)}, u32[]{:S(2)}, u32[]{:S(2)}) collective-permute-start(f32[3072]{0:T(1024)S(1)} %pad_maximum_fusion.8), channel_id=1, source_target_pairs={{0,24},{8,0},{16,8},{24,16},{1,25},{9,1},{17,9},{25,17},{2,26},{10... | collective-permute-start | bytes 36872 | tf_op jit(solution)/shard_map/ppermute | solution.py:32
  84.6 5.2 %collective-permute-start.8 = (f32[3072]{0:T(1024)S(1)}, f32[3072]{0:T(1024)S(1)}, u32[]{:S(2)}, u32[]{:S(2)}) collective-permute-start(f32[3072]{0:T(1024)S(1)} %pad_maximum_fusion.8), channel_id=1, source_target_pairs={{0,16},{8,24},{16,0},{24,8},{1,17},{9,25},{17,1},{25,9},{2,18},{10... | collective-permute-start | bytes 36872 | tf_op jit(solution)/shard_map/ppermute | solution.py:32
  85.5 4.9 %collective-permute-start.7 = (f32[3072]{0:T(1024)S(1)}, f32[3072]{0:T(1024)S(1)}, u32[]{:S(2)}, u32[]{:S(2)}) collective-permute-start(f32[3072]{0:T(1024)S(1)} %pad_maximum_fusion.8), channel_id=1, source_target_pairs={{0,8},{8,16},{16,24},{24,0},{1,9},{9,17},{17,25},{25,1},{2,10},{10... | collective-permute-start | bytes 36872 | tf_op jit(solution)/shard_map/ppermute | solution.py:32
  100.9 27.1 %collective-permute-start.12 = (bf16[320,1920]{1,0:T(8,128)(2,1)}, bf16[320,1920]{1,0:T(8,128)(2,1)S(1)}, u32[]{:S(2)}, u32[]{:S(2)}) collective-permute-start(bf16[320,1920]{1,0:T(8,128)(2,1)} %copy.37), channel_id=1, source_target_pairs={{0,1},{1,0},{2,3},{3,2},{4,5},{5,4},{6,7},{7,6},{8,9},{9,8},{10,11... | collective-permute-start | bytes 3686408 | tf_op jit(solution)/shard_map/ppermute | solution.py:86
  100.9 30.3 %collective-permute-start.10 = (bf16[320,1920]{1,0:T(8,128)(2,1)}, bf16[320,1920]{1,0:T(8,128)(2,1)S(1)}, u32[]{:S(2)}, u32[]{:S(2)}) collective-permute-start(bf16[320,1920]{1,0:T(8,128)(2,1)} %copy.37), channel_id=1, source_target_pairs={{0,2},{1,3},{2,4},{3,5},{4,6},{5,7},{6,0},{7,1},{8,10},{9,11},{10,... | collective-permute-start | bytes 3686408 | tf_op jit(solution)/shard_map/ppermute | solution.py:86
  102.6 28.8 %collective-permute-start.11 = (bf16[320,1920]{1,0:T(8,128)(2,1)}, bf16[320,1920]{1,0:T(8,128)(2,1)S(1)}, u32[]{:S(2)}, u32[]{:S(2)}) collective-permute-start(bf16[320,1920]{1,0:T(8,128)(2,1)} %copy.37), channel_id=1, source_target_pairs={{0,6},{1,7},{2,0},{3,1},{4,2},{5,3},{6,4},{7,5},{8,14},{9,15},{10,... | collective-permute-start | bytes 3686408 | tf_op jit(solution)/shard_map/ppermute | solution.py:86
  128.0 41.0 %collective-permute-start.16 = (bf16[320,1920]{1,0:T(8,128)(2,1)S(1)}, bf16[320,1920]{1,0:T(8,128)(2,1)S(1)}, u32[]{:S(2)}, u32[]{:S(2)}) collective-permute-start(bf16[320,1920]{1,0:T(8,128)(2,1)S(1)} %collective-permute-done.12), channel_id=1, source_target_pairs={{0,2},{1,3},{2,4},{3,5},{4,6},{5,7},{6,0},{7,1},{8,10},{9,11},{10,... | collective-permute-start | bytes 3686408 | tf_op jit(solution)/shard_map/ppermute | solution.py:86
  128.5 40.5 %collective-permute-start.17 = (bf16[320,1920]{1,0:T(8,128)(2,1)S(1)}, bf16[320,1920]{1,0:T(8,128)(2,1)S(1)}, u32[]{:S(2)}, u32[]{:S(2)}) collective-permute-start(bf16[320,1920]{1,0:T(8,128)(2,1)S(1)} %collective-permute-done.12), channel_id=1, source_target_pairs={{0,6},{1,7},{2,0},{3,1},{4,2},{5,3},{6,4},{7,5},{8,14},{9,15},{10,... | collective-permute-start | bytes 3686408 | tf_op jit(solution)/shard_map/ppermute | solution.py:86
  131.3 37.4 %collective-permute-start.14 = (bf16[160,1920]{1,0:T(8,128)(2,1)S(1)}, bf16[160,1920]{1,0:T(8,128)(2,1)S(1)}, u32[]{:S(2)}, u32[]{:S(2)}) collective-permute-start(bf16[160,1920]{1,0:T(8,128)(2,1)S(1)} %slice.379), channel_id=1, source_target_pairs={{0,2},{1,3},{2,4},{3,5},{4,6},{5,7},{6,0},{7,1},{8,10},{9,11},{10,... | collective-permute-start | bytes 1843208 | tf_op jit(solution)/shard_map/ppermute | solution.py:86
  131.4 37.6 %collective-permute-start.15 = (bf16[160,1920]{1,0:T(8,128)(2,1)S(1)}, bf16[160,1920]{1,0:T(8,128)(2,1)S(1)}, u32[]{:S(2)}, u32[]{:S(2)}) collective-permute-start(bf16[160,1920]{1,0:T(8,128)(2,1)S(1)} %slice.380), channel_id=1, source_target_pairs={{0,6},{1,7},{2,0},{3,1},{4,2},{5,3},{6,4},{7,5},{8,14},{9,15},{10,... | collective-permute-start | bytes 1843208 | tf_op jit(solution)/shard_map/ppermute | solution.py:86
  141.1 76.8 %collective-permute-start.13 = (bf16[960,1920]{1,0:T(8,128)(2,1)}, bf16[960,1920]{1,0:T(8,128)(2,1)}, u32[]{:S(2)}, u32[]{:S(2)}) collective-permute-start(bf16[960,1920]{1,0:T(8,128)(2,1)} %pad_maximum_fusion), channel_id=1, source_target_pairs={{0,32},{32,0},{64,96},{96,64},{1,33},{33,1},{65,97},{97,65},{2,34}... | collective-permute-start | bytes 11059208 | tf_op jit(solution)/shard_map/ppermute | solution.py:89
  176.1 46.0 %collective-permute-start.18 = (bf16[960,1920]{1,0:T(8,128)(2,1)}, bf16[960,1920]{1,0:T(8,128)(2,1)}, u32[]{:S(2)}, u32[]{:S(2)}) collective-permute-start(bf16[960,1920]{1,0:T(8,128)(2,1)} %pad_maximum_fusion.1), channel_id=1, source_target_pairs={{0,32},{32,0},{64,96},{96,64},{1,33},{33,1},{65,97},{97,65},{2,34}... | collective-permute-start | bytes 11059208 | tf_op jit(solution)/shard_map/ppermute | solution.py:89
  185.0 16.7 %collective-permute-start.20 = (bf16[160,1920]{1,0:T(8,128)(2,1)S(1)}, bf16[160,1920]{1,0:T(8,128)(2,1)S(1)}, u32[]{:S(2)}, u32[]{:S(2)}) collective-permute-start(bf16[160,1920]{1,0:T(8,128)(2,1)S(1)} %copy-done.14), channel_id=1, source_target_pairs={{0,1},{1,0},{2,3},{3,2},{4,5},{5,4},{6,7},{7,6},{8,9},{9,8},{10,11... | collective-permute-start | bytes 1843208 | tf_op jit(solution)/shard_map/ppermute | solution.py:86
  186.5 27.9 %collective-permute-start.19 = (bf16[160,1920]{1,0:T(8,128)(2,1)S(1)}, bf16[160,1920]{1,0:T(8,128)(2,1)S(1)}, u32[]{:S(2)}, u32[]{:S(2)}) collective-permute-start(bf16[160,1920]{1,0:T(8,128)(2,1)S(1)} %collective-permute-done.14), channel_id=1, source_target_pairs={{0,1},{1,0},{2,3},{3,2},{4,5},{5,4},{6,7},{7,6},{8,9},{9,8},{10,11... | collective-permute-start | bytes 1843208 | tf_op jit(solution)/shard_map/ppermute | solution.py:86
  215.6 49.9 %collective-permute-start.21 = (bf16[320,1920]{1,0:T(8,128)(2,1)}, bf16[320,1920]{1,0:T(8,128)(2,1)}, u32[]{:S(2)}, u32[]{:S(2)}) collective-permute-start(bf16[320,1920]{1,0:T(8,128)(2,1)} %pad_maximum_fusion.4), channel_id=1, source_target_pairs={{0,32},{32,0},{64,96},{96,64},{1,33},{33,1},{65,97},{97,65},{2,34}... | collective-permute-start | bytes 3686408 | tf_op jit(solution)/shard_map/ppermute | solution.py:89
  (30 other events, 305.0 us)
Sparse Core Ops, SparseCore 0:
  17.8 59.4 all-gather.2
  92.8 55.1 all-gather.4

commit v7 on v1

--- a/solution.py
+++ b/solution.py
@@ -225,12 +225,8 @@
         return (accum / denom[:, None]).astype(jnp.bfloat16)
 
     attended = lax.map(one_block, triple[:, :, 0])
-    returned = [attended[0]]
-    for s in range(1, n_ctx):
-        returned.append(
-            lax.ppermute(attended[s], "ctx", [(d, (d - s) % n_ctx) for d in range(active)])
-        )
-    by_head = jnp.take(jnp.stack(returned), (jnp.arange(heads_here) - c_idx) % n_ctx, axis=0)
+    attended = jnp.take(attended, (c_idx - jnp.arange(n_ctx)) % n_ctx, axis=0)
+    by_head = lax.all_to_all(attended, "ctx", 0, 0, tiled=True)[:heads_here]
     return by_head.transpose(1, 0, 2).reshape(group_rows, heads_here * HDIM)
 
 

time: 411 us -> 405 us (0.985)
  starting transfers between devices: 67.8 us -> 48.5 us
  blocking collectives: 0 us -> 18.3 us
  waiting for transfers between devices: 141 us -> 136 us
    ppermute x7 -> x0, starting transfers between devices: 19 us -> none  [shards(): lax.ppermute(attended[s], 'ctx', [(d, (d - s) % n_ctx) for d in range(act...]
    all_to_all x0 -> x1, blocking collectives: none -> 18.3 us  [shards(): by_head = lax.all_to_all(attended, 'ctx', 0, 0, tiled=True)[:heads_here]]
    ppermute x7 -> x0, waiting for transfers between devices: 4.91 us -> none  [shards(): lax.ppermute(attended[s], 'ctx', [(d, (d - s) % n_ctx) for d in range(act...]
    unnamed x91 -> x85, local copies, waits for them, and re-layouts: 22.3 us -> 22.2 us
  transfers between devices with their start and end apart: 38 -> 31, of which waited for: 16 -> 13; matrix products, arithmetic and copies ran while one was open for 30% -> 30% of each run, Pallas kernels for 0% -> 0%
where the time goes in v7:
time: 405 us; the launch traced here: 400 us
  waiting for transfers between devices  136 us (34%)
  local copies, waits for them, and re-layouts  86.2 us (21%)
  matrix products  58.9 us (15%)
  starting transfers between devices  48.5 us (12%)
  other arithmetic  35.9 us (9%)
  blocking collectives  18.3 us (5%)
  between operations  15.4 us (4%)
    ppermute x9, waiting for transfers between devices, send(): return lax.ppermute(cells, 'ctx', [(i, step(i)) for i in range(n_ctx)])  76.1 us
    ppermute x7, waiting for transfers between devices, shards(): lax.ppermute(lax.dynamic_index_in_dim(qkv, target, 1, keepdims=False), 'c...  34.7 us
    dot_general x3, matrix products, shards(): jnp.dot(jnp.concatenate(columns, 1), jnp.concatenate(weights, 0), preferr...  22.6 us
    unnamed x85, local copies, waits for them, and re-layouts  22.2 us
    all_to_all x1, blocking collectives, shards(): by_head = lax.all_to_all(attended, 'ctx', 0, 0, tiled=True)[:heads_here]  18.3 us
    concatenate x3, other arithmetic, shards(): jnp.concatenate([cells for cells, _, _ in s], 0)  14.7 us
    all_gather x1, waiting for transfers between devices, shards(): lax.all_gather(jnp.concatenate([patch_weight, share_parts], 0), 'ctx', ax...  14.3 us
    ppermute x7, starting transfers between devices, shards(): lax.ppermute(lax.dynamic_index_in_dim(qkv, target, 1, keepdims=False), 'c...  13.6 us
  transfers between devices with their start and end apart: 31, of which 13 were waited for; matrix products, arithmetic and copies ran while one was open for 30% of the time, Pallas kernels for 0%

profile of v7, /device:TPU:0, one launch (start us, length us, event | category | flops | bytes accessed | tf_op | source)
XLA Modules:
  0.0 400.0 jit_solution(2893303079807005197)
XLA Ops:
  10.1 4.1 %collective-permute-start = (bf16[6,1,32,96]{3,2,1,0:T(8,128)(2,1)}, bf16[6,1,32,96]{3,2,1,0:T(8,128)(2,1)}, u32[]{:S(2)}, u32[]{:S(2)}) collective-permute-start(bf16[6,1,32,96]{3,2,1,0:T(8,128)(2,1)} %get-tuple-element.102), channel_id=1, source_target_pairs={{0,8},{8,16},{16,24},{1,9},{9,17},{17,25},{2,10},{10,18},{18,26},{... | collective-permute-start | bytes 110600 | tf_op jit(solution)/shard_map/ppermute | solution.py:19
  22.6 3.5 collective-permute-start.2
  63.2 14.3 %all-gather.3.cloned.1.call-done = bf16[774,1280]{0,1:T(8,128)(2,1)} async-done(((bf16[774,160]{0,1:T(8,128)(2,1)}), bf16[774,1280]{0,1:T(8,128)(2,1)}) %all-gather.3.cloned.1.call-update) | async-done | bytes 1981456 | tf_op jit(solution)/shard_map/all_gather | solution.py:157
  93.0 3.9 copy.52
  104.4 24.1 %collective-permute-done.12 = bf16[320,1920]{1,0:T(8,128)(2,1)S(1)} collective-permute-done((bf16[320,1920]{1,0:T(8,128)(2,1)}, bf16[320,1920]{1,0:T(8,128)(2,1)S(1)}, u32[]{:S(2)}, u32[]{:S(2)}) %collective-permute-start.12) | collective-permute-done | bytes 1228832 | tf_op jit(solution)/shard_map/ppermute | solution.py:86
  135.2 6.4 %pad_maximum_fusion = bf16[960,1920]{1,0:T(8,128)(2,1)} fusion(bf16[320,1920]{1,0:T(8,128)(2,1)S(1)} %collective-permute-done.12, bf16[320,1920]{1,0:T(8,128)(2,1)S(1)} %collective-permute-done.11, bf16[320,1920]{1,0:T(8,128)(2,1)S(1)} %collective-permute-done.10), kind=kLoop, calls=%fused_computation.35 | loop fusion | flops 11059200 | bytes 7372800 | tf_op jit(solution)/shard_map/concatenate | solution.py:114
  141.7 27.5 %collective-permute-done.14 = bf16[160,1920]{1,0:T(8,128)(2,1)S(1)} collective-permute-done((bf16[160,1920]{1,0:T(8,128)(2,1)S(1)}, bf16[160,1920]{1,0:T(8,128)(2,1)S(1)}, u32[]{:S(2)}, u32[]{:S(2)}) %collective-permute-start.14) | collective-permute-done | bytes 614432 | tf_op jit(solution)/shard_map/ppermute | solution.py:86
  169.4 7.0 %pad_maximum_fusion.1 = bf16[960,1920]{1,0:T(8,128)(2,1)} fusion(bf16[320,1920]{1,0:T(8,128)(2,1)S(1)} %collective-permute-done.17, bf16[320,1920]{1,0:T(8,128)(2,1)S(1)} %collective-permute-done.16, bf16[160,1920]{1,0:T(8,128)(2,1)S(1)} %collective-permute-done.15, bf16[160,1920]{1,0:T(8,128)(2,1)S(1)} %collective-permute-done.14), kind=kLoop, calls=%fused_computation.36 | loop fusion | flops 14745600 | bytes 7372800 | tf_op jit(solution)/shard_map/concatenate | solution.py:114
  191.0 11.7 %collective-permute-done.19 = bf16[160,1920]{1,0:T(8,128)(2,1)S(1)} collective-permute-done((bf16[160,1920]{1,0:T(8,128)(2,1)S(1)}, bf16[160,1920]{1,0:T(8,128)(2,1)S(1)}, u32[]{:S(2)}, u32[]{:S(2)}) %collective-permute-start.19) | collective-permute-done | bytes 614432 | tf_op jit(solution)/shard_map/ppermute | solution.py:86
  202.7 12.6 %collective-permute-done.20 = bf16[160,1920]{1,0:T(8,128)(2,1)S(1)} collective-permute-done((bf16[160,1920]{1,0:T(8,128)(2,1)S(1)}, bf16[160,1920]{1,0:T(8,128)(2,1)S(1)}, u32[]{:S(2)}, u32[]{:S(2)}) %collective-permute-start.20) | collective-permute-done | bytes 614432 | tf_op jit(solution)/shard_map/ppermute | solution.py:86
  218.9 4.2 %constant_dynamic-update-slice_fusion.9 = bf16[2560,1920]{1,0:T(8,128)(2,1)} fusion(bf16[2560,1920]{1,0:T(8,128)(2,1)} %constant_dynamic-update-slice_fusion.10, bf16[960,1920]{1,0:T(8,128)(2,1)} %collective-permute-done.13), kind=kLoop, calls=%fused_computation.187 | loop fusion | bytes 7372800 | tf_op jit(solution)/shard_map/concatenate | solution.py:198
  223.1 4.1 %constant_dynamic-update-slice_fusion.14 = bf16[1920,1920]{1,0:T(8,128)(2,1)} fusion(bf16[1920,1920]{1,0:T(8,128)(2,1)} %constant_dynamic-update-slice_fusion.15, bf16[960,1920]{1,0:T(8,128)(2,1)} %collective-permute-done.18), kind=kLoop, calls=%fused_computation.192 | loop fusion | bytes 7372800 | tf_op jit(solution)/shard_map/concatenate | solution.py:198
  227.2 4.4 %constant_dynamic-slice_fusion.11 = (bf16[512,160]{1,0:T(8,128)(2,1)}, bf16[512,160]{1,0:T(8,128)(2,1)}, bf16[512,160]{1,0:T(8,128)(2,1)}, bf16[512,160]{1,0:T(8...) fusion(bf16[512,5120]{1,0:T(8,128)(2,1)} %all-gather.5.cloned.1, ...), kind=kLoop, calls=%fused_computation.219 | loop fusion | bytes 2621472 | tf_op jit(solution)/shard_map/dynamic_slice | solution.py:192
  231.7 6.4 %constant_dynamic-slice_fusion.12 = (bf16[512,320]{1,0:T(8,128)(2,1)S(1)}, bf16[512,320]{1,0:T(8,128)(2,1)S(1)}, bf16[512,320]{1,0:T(8,128)(2,1)S(1)}, bf16[512,...) fusion(bf16[512,5120]{1,0:T(8,128)(2,1)} %all-gather.5.cloned.1, ...), kind=kLoop, calls=%fused_computation.220 | loop fusion | bytes 6553640 | tf_op jit(solution)/shard_map/dynamic_slice | solution.py:192
  238.1 4.2 %concatenate.128 = bf16[512,1920]{1,0:T(8,128)(2,1)S(1)} concatenate(bf16[512,160]{1,0:T(8,128)(2,1)} %get-tuple-element.52, bf16[512,160]{1,0:T(8,128)(2,1)} %get-tuple-element.51, bf16[512,320]{1,0:T(8,128)(2,1)} %get-tuple-element.56, bf16[512,320]{1,0:T(8,128)(2,1)S(1)} %get-tuple-element.55, bf16[512,160]{1,0:T(8,128)(2,1)} %get-tuple-element.50, ...), dimensions={1} | concatenate | bytes 3932160 | tf_op jit(solution)/shard_map/concatenate | solution.py:197
  242.3 9.5 %fusion.155 = f32[512,1920]{1,0:T(8,128)} fusion(bf16[512,1920]{1,0:T(8,128)(2,1)S(1)} %concatenate.128, bf16[1920,1920]{1,0:T(8,128)(2,1)} %constant_dynamic-update-slice_fusion.14), kind=kOutput, calls=%fused_computation.292 | convolution fusion | flops 3774873600 | bytes 13271040 | tf_op jit(solution)/shard_map/dot_general | solution.py:196
  253.9 4.1 %concatenate.125 = bf16[512,2560]{1,0:T(8,128)(2,1)S(1)} concatenate(bf16[512,640]{1,0:T(8,128)(2,1)} %constant_dynamic-slice_fusion.27, bf16[512,320]{1,0:T(8,128)(2,1)} %get-tuple-element.62, bf16[512,320]{1,0:T(8,128)(2,1)} %get-tuple-element.61, bf16[512,320]{1,0:T(8,128)(2,1)} %get-tuple-element.60, bf16[512,320]{1,0:T(8,128)(2,1)} %get-tuple-element.59, ...), dimensions={1} | concatenate | bytes 5242880 | tf_op jit(solution)/shard_map/concatenate | solution.py:197
  258.1 8.5 %fusion.154 = f32[512,1920]{1,0:T(8,128)S(1)} fusion(bf16[512,2560]{1,0:T(8,128)(2,1)S(1)} %concatenate.125, bf16[2560,1920]{1,0:T(8,128)(2,1)} %constant_dynamic-update-slice_fusion.9), kind=kOutput, calls=%fused_computation.291 | convolution fusion | flops 5033164800 | bytes 16384000 | tf_op jit(solution)/shard_map/dot_general | solution.py:196
  266.6 4.6 %add_convert_fusion = bf16[512,1920]{1,0:T(8,128)(2,1)} fusion(f32[512,1920]{1,0:T(8,128)S(1)} %fusion.154, f32[512,1920]{1,0:T(8,128)S(1)} %copy-done.33, bf16[320,1920]{1,0:T(8,128)(2,1)} %collective-permute-done.21, bf16[160,1920]{1,0:T(8,128)(2,1)S(1)} %copy-done.23, bf16[160,1920]{1,0:T(8,128)(2,1)S(1)} %copy-done.21, ...), kind=kOutput, calls=%fused_computation.18 | convolution fusion | flops 1271234560 | bytes 12943360 | tf_op jit(solution)/shard_map/dot_general | solution.py:196
  277.2 3.4 collective-permute-start.22
  296.4 21.9 %collective-permute-done.23 = bf16[512,3,128]{2,0,1:T(8,128)(2,1)} collective-permute-done((bf16[512,3,128]{2,0,1:T(8,128)(2,1)}, bf16[512,3,128]{2,0,1:T(8,128)(2,1)}, u32[]{:S(2)}, u32[]{:S(2)}) %collective-permute-start.23) | collective-permute-done | bytes 393248 | tf_op jit(solution)/shard_map/ppermute | solution.py:208
  322.9 12.8 %collective-permute-done.28 = bf16[512,3,128]{2,0,1:T(8,128)(2,1)S(1)} collective-permute-done((bf16[512,3,128]{2,0,1:T(8,128)(2,1)S(1)}, bf16[512,3,128]{2,0,1:T(8,128)(2,1)S(1)}, u32[]{:S(2)}, u32[]{:S(2)}) %collective-permute-start.28) | collective-permute-done | bytes 393248 | tf_op jit(solution)/shard_map/ppermute | solution.py:208
  337.1 35.3 %while.10 = (s32[]{:T(128)}, bf16[8,512,128]{2,1,0:T(8,128)(2,1)S(1)}, bf16[8,512,128]{2,1,0:T(8,128)(2,1)S(1)}, bf16[4096,128]{1,0:T(8,128)(2,1)S(1)}, bf16[4096,128]{1,0:T(8,128)(2,1)}, /*index=5*/s32[]{:T(128)}) while((s32[]{:T(128)}, bf16[8,512,128]{2,1,0:T(8,128)(2,1)S(1)}, bf16[8,512,128]{2,1,0:T(8,128)(2,1)S(1)}, ...), condition=%wide.region_5.6_spmd, body=%wide.region_2.5_spmd.sunk | while | flops 1090649600 | bytes 31733864 | solution.py:227
  373.3 18.3 %all_to_all.5 = bf16[8,512,128]{2,1,0:T(8,128)(2,1)S(1)} all-to-all(bf16[8,512,128]{2,1,0:T(8,128)(2,1)S(1)} %broadcast_select_fusion), channel_id=1, replica_groups=mesh['dp'=4,'head'=4,'ctx'=8] {'ctx'}, dimensions={0} | all-to-all | bytes 2097152 | tf_op jit(solution)/shard_map/all_to_all | solution.py:229
  (280 shorter events, 162.7 us)
Async XLA Ops:
  6.5 70.9 %all-gather.3.cloned.1.call-start = ((), (), s32[]{:S(2)}) async-start(), calls=%async_computation.1 | async-start | bytes 2580480 | tf_op jit(solution)/shard_map/all_gather | solution.py:157
  10.1 10.3 %collective-permute-start = (bf16[6,1,32,96]{3,2,1,0:T(8,128)(2,1)}, bf16[6,1,32,96]{3,2,1,0:T(8,128)(2,1)}, u32[]{:S(2)}, u32[]{:S(2)}) collective-permute-start(bf16[6,1,32,96]{3,2,1,0:T(8,128)(2,1)} %get-tuple-element.102), channel_id=1, source_target_pairs={{0,8},{8,16},{16,24},{1,9},{9,17},{17,25},{2,10},{10,18},{18,26},{... | collective-permute-start | bytes 110600 | tf_op jit(solution)/shard_map/ppermute | solution.py:19
  17.4 209.8 %all-gather.5.cloned.1.call-start = ((), (), s32[]{:S(2)}) async-start(), calls=%async_computation.2 | async-start | bytes 6553600 | tf_op jit(solution)/shard_map/all_gather | solution.py:180
  48.7 9.8 %collective-permute-start.4 = (bf16[128,768]{1,0:T(8,128)(2,1)S(1)}, bf16[128,768]{1,0:T(8,128)(2,1)S(1)}, u32[]{:S(2)}, u32[]{:S(2)}) collective-permute-start(bf16[128,768]{1,0:T(8,128)(2,1)S(1)} %reshape.182), channel_id=1, source_target_pairs={{0,8},{8,16},{16,24},{24,0},{1,9},{9,17},{17,25},{25,1},{2,10},{10... | collective-permute-start | bytes 589832 | tf_op jit(solution)/shard_map/ppermute | solution.py:32
  51.4 9.9 %collective-permute-start.5 = (bf16[128,768]{1,0:T(8,128)(2,1)S(1)}, bf16[128,768]{1,0:T(8,128)(2,1)S(1)}, u32[]{:S(2)}, u32[]{:S(2)}) collective-permute-start(bf16[128,768]{1,0:T(8,128)(2,1)S(1)} %reshape.182), channel_id=1, source_target_pairs={{0,16},{8,24},{16,0},{24,8},{1,17},{9,25},{17,1},{25,9},{2,18},{10... | collective-permute-start | bytes 589832 | tf_op jit(solution)/shard_map/ppermute | solution.py:32
  101.1 27.4 %collective-permute-start.12 = (bf16[320,1920]{1,0:T(8,128)(2,1)}, bf16[320,1920]{1,0:T(8,128)(2,1)S(1)}, u32[]{:S(2)}, u32[]{:S(2)}) collective-permute-start(bf16[320,1920]{1,0:T(8,128)(2,1)} %copy.53), channel_id=1, source_target_pairs={{0,1},{1,0},{2,3},{3,2},{4,5},{5,4},{6,7},{7,6},{8,9},{9,8},{10,11... | collective-permute-start | bytes 3686408 | tf_op jit(solution)/shard_map/ppermute | solution.py:86
  101.1 30.6 %collective-permute-start.10 = (bf16[320,1920]{1,0:T(8,128)(2,1)}, bf16[320,1920]{1,0:T(8,128)(2,1)S(1)}, u32[]{:S(2)}, u32[]{:S(2)}) collective-permute-start(bf16[320,1920]{1,0:T(8,128)(2,1)} %copy.53), channel_id=1, source_target_pairs={{0,2},{1,3},{2,4},{3,5},{4,6},{5,7},{6,0},{7,1},{8,10},{9,11},{10,... | collective-permute-start | bytes 3686408 | tf_op jit(solution)/shard_map/ppermute | solution.py:86
  102.7 29.2 %collective-permute-start.11 = (bf16[320,1920]{1,0:T(8,128)(2,1)}, bf16[320,1920]{1,0:T(8,128)(2,1)S(1)}, u32[]{:S(2)}, u32[]{:S(2)}) collective-permute-start(bf16[320,1920]{1,0:T(8,128)(2,1)} %copy.53), channel_id=1, source_target_pairs={{0,6},{1,7},{2,0},{3,1},{4,2},{5,3},{6,4},{7,5},{8,14},{9,15},{10,... | collective-permute-start | bytes 3686408 | tf_op jit(solution)/shard_map/ppermute | solution.py:86
  128.5 40.9 %collective-permute-start.16 = (bf16[320,1920]{1,0:T(8,128)(2,1)S(1)}, bf16[320,1920]{1,0:T(8,128)(2,1)S(1)}, u32[]{:S(2)}, u32[]{:S(2)}) collective-permute-start(bf16[320,1920]{1,0:T(8,128)(2,1)S(1)} %collective-permute-done.12), channel_id=1, source_target_pairs={{0,2},{1,3},{2,4},{3,5},{4,6},{5,7},{6,0},{7,1},{8,10},{9,11},{10,... | collective-permute-start | bytes 3686408 | tf_op jit(solution)/shard_map/ppermute | solution.py:86
  128.9 40.5 %collective-permute-start.17 = (bf16[320,1920]{1,0:T(8,128)(2,1)S(1)}, bf16[320,1920]{1,0:T(8,128)(2,1)S(1)}, u32[]{:S(2)}, u32[]{:S(2)}) collective-permute-start(bf16[320,1920]{1,0:T(8,128)(2,1)S(1)} %collective-permute-done.12), channel_id=1, source_target_pairs={{0,6},{1,7},{2,0},{3,1},{4,2},{5,3},{6,4},{7,5},{8,14},{9,15},{10,... | collective-permute-start | bytes 3686408 | tf_op jit(solution)/shard_map/ppermute | solution.py:86
  131.8 37.4 %collective-permute-start.14 = (bf16[160,1920]{1,0:T(8,128)(2,1)S(1)}, bf16[160,1920]{1,0:T(8,128)(2,1)S(1)}, u32[]{:S(2)}, u32[]{:S(2)}) collective-permute-start(bf16[160,1920]{1,0:T(8,128)(2,1)S(1)} %slice.353), channel_id=1, source_target_pairs={{0,2},{1,3},{2,4},{3,5},{4,6},{5,7},{6,0},{7,1},{8,10},{9,11},{10,... | collective-permute-start | bytes 1843208 | tf_op jit(solution)/shard_map/ppermute | solution.py:86
  131.9 37.4 %collective-permute-start.15 = (bf16[160,1920]{1,0:T(8,128)(2,1)S(1)}, bf16[160,1920]{1,0:T(8,128)(2,1)S(1)}, u32[]{:S(2)}, u32[]{:S(2)}) collective-permute-start(bf16[160,1920]{1,0:T(8,128)(2,1)S(1)} %slice.354), channel_id=1, source_target_pairs={{0,6},{1,7},{2,0},{3,1},{4,2},{5,3},{6,4},{7,5},{8,14},{9,15},{10,... | collective-permute-start | bytes 1843208 | tf_op jit(solution)/shard_map/ppermute | solution.py:86
  141.6 77.3 %collective-permute-start.13 = (bf16[960,1920]{1,0:T(8,128)(2,1)}, bf16[960,1920]{1,0:T(8,128)(2,1)}, u32[]{:S(2)}, u32[]{:S(2)}) collective-permute-start(bf16[960,1920]{1,0:T(8,128)(2,1)} %pad_maximum_fusion), channel_id=1, source_target_pairs={{0,32},{32,0},{64,96},{96,64},{1,33},{33,1},{65,97},{97,65},{2,34}... | collective-permute-start | bytes 11059208 | tf_op jit(solution)/shard_map/ppermute | solution.py:89
  176.5 46.7 %collective-permute-start.18 = (bf16[960,1920]{1,0:T(8,128)(2,1)}, bf16[960,1920]{1,0:T(8,128)(2,1)}, u32[]{:S(2)}, u32[]{:S(2)}) collective-permute-start(bf16[960,1920]{1,0:T(8,128)(2,1)} %pad_maximum_fusion.1), channel_id=1, source_target_pairs={{0,32},{32,0},{64,96},{96,64},{1,33},{33,1},{65,97},{97,65},{2,34}... | collective-permute-start | bytes 11059208 | tf_op jit(solution)/shard_map/ppermute | solution.py:89
  186.1 16.7 %collective-permute-start.19 = (bf16[160,1920]{1,0:T(8,128)(2,1)S(1)}, bf16[160,1920]{1,0:T(8,128)(2,1)S(1)}, u32[]{:S(2)}, u32[]{:S(2)}) collective-permute-start(bf16[160,1920]{1,0:T(8,128)(2,1)S(1)} %collective-permute-done.14), channel_id=1, source_target_pairs={{0,1},{1,0},{2,3},{3,2},{4,5},{5,4},{6,7},{7,6},{8,9},{9,8},{10,11... | collective-permute-start | bytes 1843208 | tf_op jit(solution)/shard_map/ppermute | solution.py:86
  187.7 27.7 %collective-permute-start.20 = (bf16[160,1920]{1,0:T(8,128)(2,1)S(1)}, bf16[160,1920]{1,0:T(8,128)(2,1)S(1)}, u32[]{:S(2)}, u32[]{:S(2)}) collective-permute-start(bf16[160,1920]{1,0:T(8,128)(2,1)S(1)} %copy-done.13), channel_id=1, source_target_pairs={{0,1},{1,0},{2,3},{3,2},{4,5},{5,4},{6,7},{7,6},{8,9},{9,8},{10,11... | collective-permute-start | bytes 1843208 | tf_op jit(solution)/shard_map/ppermute | solution.py:86
  216.6 50.0 %collective-permute-start.21 = (bf16[320,1920]{1,0:T(8,128)(2,1)}, bf16[320,1920]{1,0:T(8,128)(2,1)}, u32[]{:S(2)}, u32[]{:S(2)}) collective-permute-start(bf16[320,1920]{1,0:T(8,128)(2,1)} %pad_maximum_fusion.4), channel_id=1, source_target_pairs={{0,32},{32,0},{64,96},{96,64},{1,33},{33,1},{65,97},{97,65},{2,34}... | collective-permute-start | bytes 3686408 | tf_op jit(solution)/shard_map/ppermute | solution.py:89
  277.2 16.9 %collective-permute-start.22 = (bf16[512,3,128]{2,0,1:T(8,128)(2,1)}, bf16[512,3,128]{2,0,1:T(8,128)(2,1)}, u32[]{:S(2)}, u32[]{:S(2)}) collective-permute-start(bf16[512,3,128]{2,0,1:T(8,128)(2,1)} %bitcast.48), channel_id=1, source_target_pairs={{0,1},{1,2},{2,3},{3,4},{7,0},{8,9},{9,10},{10,11},{11,12},{15,8},... | collective-permute-start | bytes 1179656 | tf_op jit(solution)/shard_map/ppermute | solution.py:208
  283.8 34.5 %collective-permute-start.23 = (bf16[512,3,128]{2,0,1:T(8,128)(2,1)}, bf16[512,3,128]{2,0,1:T(8,128)(2,1)}, u32[]{:S(2)}, u32[]{:S(2)}) collective-permute-start(bf16[512,3,128]{2,0,1:T(8,128)(2,1)} %bitcast.50), channel_id=1, source_target_pairs={{0,2},{1,3},{2,4},{6,0},{7,1},{8,10},{9,11},{10,12},{14,8},{15,9},... | collective-permute-start | bytes 1179656 | tf_op jit(solution)/shard_map/ppermute | solution.py:208
  287.3 33.4 %collective-permute-start.24 = (bf16[512,3,128]{2,0,1:T(8,128)(2,1)}, bf16[512,3,128]{2,0,1:T(8,128)(2,1)}, u32[]{:S(2)}, u32[]{:S(2)}) collective-permute-start(bf16[512,3,128]{2,0,1:T(8,128)(2,1)} %bitcast.52), channel_id=1, source_target_pairs={{0,3},{1,4},{5,0},{6,1},{7,2},{8,11},{9,12},{13,8},{14,9},{15,10},... | collective-permute-start | bytes 1179656 | tf_op jit(solution)/shard_map/ppermute | solution.py:208
  290.1 31.6 %collective-permute-start.25 = (bf16[512,3,128]{2,0,1:T(8,128)(2,1)}, bf16[512,3,128]{2,0,1:T(8,128)(2,1)}, u32[]{:S(2)}, u32[]{:S(2)}) collective-permute-start(bf16[512,3,128]{2,0,1:T(8,128)(2,1)} %bitcast.54), channel_id=1, source_target_pairs={{0,4},{4,0},{5,1},{6,2},{7,3},{8,12},{12,8},{13,9},{14,10},{15,11}... | collective-permute-start | bytes 1179656 | tf_op jit(solution)/shard_map/ppermute | solution.py:208
  292.3 30.5 %collective-permute-start.26 = (bf16[512,3,128]{2,0,1:T(8,128)(2,1)S(1)}, bf16[512,3,128]{2,0,1:T(8,128)(2,1)S(1)}, u32[]{:S(2)}, u32[]{:S(2)}) collective-permute-start(bf16[512,3,128]{2,0,1:T(8,128)(2,1)S(1)} %bitcast.159), channel_id=1, source_target_pairs={{3,0},{4,1},{5,2},{6,3},{7,4},{11,8},{12,9},{13,10},{14,11},{15,12... | collective-permute-start | bytes 1179656 | tf_op jit(solution)/shard_map/ppermute | solution.py:208
  294.1 28.8 %collective-permute-start.27 = (bf16[512,3,128]{2,0,1:T(8,128)(2,1)S(1)}, bf16[512,3,128]{2,0,1:T(8,128)(2,1)S(1)}, u32[]{:S(2)}, u32[]{:S(2)}) collective-permute-start(bf16[512,3,128]{2,0,1:T(8,128)(2,1)S(1)} %bitcast.158), channel_id=1, source_target_pairs={{2,0},{3,1},{4,2},{5,3},{6,4},{10,8},{11,9},{12,10},{13,11},{14,12... | collective-permute-start | bytes 1179656 | tf_op jit(solution)/shard_map/ppermute | solution.py:208
  318.3 17.4 %collective-permute-start.28 = (bf16[512,3,128]{2,0,1:T(8,128)(2,1)S(1)}, bf16[512,3,128]{2,0,1:T(8,128)(2,1)S(1)}, u32[]{:S(2)}, u32[]{:S(2)}) collective-permute-start(bf16[512,3,128]{2,0,1:T(8,128)(2,1)S(1)} %bitcast.157), channel_id=1, source_target_pairs={{1,0},{2,1},{3,2},{4,3},{5,4},{9,8},{10,9},{11,10},{12,11},{13,12}... | collective-permute-start | bytes 1179656 | tf_op jit(solution)/shard_map/ppermute | solution.py:208
  (48 other events, 397.3 us)
Sparse Core Ops, SparseCore 0:
  17.5 59.8 all-gather.2
  93.1 55.8 all-gather.4

commit v8 on v2

--- a/solution.py
+++ b/solution.py
@@ -202,10 +202,9 @@
     qkv = qkv.astype(jnp.bfloat16).reshape(group_rows, heads_here, 3, HDIM)
     active = min(heads_here, n_ctx)
     spare = n_ctx - active
-    outgoing = jnp.concatenate(
-        [qkv.transpose(1, 0, 2, 3), jnp.zeros((spare,) + qkv.shape[:1] + qkv.shape[2:], qkv.dtype)], 0
-    )
-    triple = lax.all_to_all(outgoing, "ctx", 0, 0, tiled=True)
+    by_head = qkv.transpose(1, 0, 2, 3)
+    outgoing = jnp.concatenate([by_head, jnp.zeros((spare,) + by_head.shape[1:], qkv.dtype)], 0)
+    triple = lax.all_to_all(outgoing.reshape(n_ctx, -1), "ctx", 0, 0, tiled=True).reshape(outgoing.shape)
     keys = triple[:, :, 1].reshape(-1, HDIM)
     values = triple[:, :, 2].reshape(-1, HDIM)
     inv_root = 1.0 / jnp.sqrt(jnp.float32(HDIM))

time: 405 us -> 470 us (1.16)
  other arithmetic: 35.7 us -> 74.2 us
  local copies, waits for them, and re-layouts: 82.5 us -> 118 us
  matrix products: 66.3 us -> 57.5 us
    all_to_all x0 -> x2, other arithmetic: none -> 38.5 us  [shards(): lax.all_to_all(outgoing.reshape(n_ctx, -1), 'ctx', 0, 0, tiled=True)]
    unnamed x74 -> x78, local copies, waits for them, and re-layouts: 17.8 us -> 32 us
    all_to_all x0 -> x2, local copies, waits for them, and re-layouts: none -> 8.69 us  [shards(): lax.all_to_all(outgoing.reshape(n_ctx, -1), 'ctx', 0, 0, tiled=True)]
    slice x2 -> x1, local copies, waits for them, and re-layouts: 2.45 us -> 10 us  [shards(): values = triple[:, :, 2].reshape(-1, HDIM)]
    dot_general x8, matrix products: 18.2 us -> 10.6 us  [one_block(): jnp.dot(query, keys.T, preferred_element_type=jnp.float32) * inv_root]
    reshape x0 -> x1, local copies, waits for them, and re-layouts: none -> 5.62 us  [shards(): lax.all_to_all(outgoing.reshape(n_ctx, -1), 'ctx', 0, 0, tiled=True)]
  transfers between devices with their start and end apart: 25 -> 25, of which waited for: 12 -> 12; matrix products, arithmetic and copies ran while one was open for 28% -> 24% of each run, Pallas kernels for 0% -> 0%
where the time goes in v8:
time: 470 us; the launch traced here: 465 us
  waiting for transfers between devices  141 us (30%)
  local copies, waits for them, and re-layouts  118 us (25%)
  other arithmetic  74.2 us (16%)
  matrix products  57.5 us (12%)
  starting transfers between devices  40.2 us (9%)
  blocking collectives  19.1 us (4%)
  between operations  15.2 us (3%)
    ppermute x9, waiting for transfers between devices, send(): return lax.ppermute(cells, 'ctx', [(i, step(i)) for i in range(n_ctx)])  76.1 us
    all_to_all x1, waiting for transfers between devices, shards(): lax.all_to_all(outgoing.reshape(n_ctx, -1), 'ctx', 0, 0, tiled=True)  38.8 us
    all_to_all x2, other arithmetic, shards(): lax.all_to_all(outgoing.reshape(n_ctx, -1), 'ctx', 0, 0, tiled=True)  38.5 us
    unnamed x78, local copies, waits for them, and re-layouts  32 us
    dot_general x3, matrix products, shards(): jnp.dot(jnp.concatenate(columns, 1), jnp.concatenate(weights, 0), preferr...  21.3 us
    all_to_all x1, blocking collectives, shards(): by_head = lax.all_to_all(attended, 'ctx', 0, 0, tiled=True)[:heads_here]  19.1 us
    concatenate x3, other arithmetic, shards(): jnp.concatenate([cells for cells, _, _ in s], 0)  14.7 us
    all_gather x1, waiting for transfers between devices, shards(): lax.all_gather(jnp.concatenate([patch_weight, share_parts], 0), 'ctx', ax...  14.3 us
  transfers between devices with their start and end apart: 25, of which 12 were waited for; matrix products, arithmetic and copies ran while one was open for 24% of the time, Pallas kernels for 0%

profile of v8, /device:TPU:0, one launch (start us, length us, event | category | flops | bytes accessed | tf_op | source)
XLA Modules:
  0.0 465.4 jit_solution(15103439924935601492)
XLA Ops:
  63.1 14.3 %all-gather.3.cloned.1.call-done = bf16[774,1280]{0,1:T(8,128)(2,1)} async-done(((bf16[774,160]{0,1:T(8,128)(2,1)}), bf16[774,1280]{0,1:T(8,128)(2,1)}) %all-gather.3.cloned.1.call-update) | async-done | bytes 1981456 | tf_op jit(solution)/shard_map/all_gather | solution.py:157
  104.3 24.1 %collective-permute-done.12 = bf16[320,1920]{1,0:T(8,128)(2,1)S(1)} collective-permute-done((bf16[320,1920]{1,0:T(8,128)(2,1)}, bf16[320,1920]{1,0:T(8,128)(2,1)S(1)}, u32[]{:S(2)}, u32[]{:S(2)}) %collective-permute-start.12) | collective-permute-done | bytes 1228832 | tf_op jit(solution)/shard_map/ppermute | solution.py:86
  135.1 6.4 %pad_maximum_fusion = bf16[960,1920]{1,0:T(8,128)(2,1)} fusion(bf16[320,1920]{1,0:T(8,128)(2,1)S(1)} %collective-permute-done.12, bf16[320,1920]{1,0:T(8,128)(2,1)S(1)} %collective-permute-done.11, bf16[320,1920]{1,0:T(8,128)(2,1)S(1)} %collective-permute-done.10), kind=kLoop, calls=%fused_computation.34 | loop fusion | flops 11059200 | bytes 7372800 | tf_op jit(solution)/shard_map/concatenate | solution.py:114
  141.7 27.5 %collective-permute-done.14 = bf16[160,1920]{1,0:T(8,128)(2,1)S(1)} collective-permute-done((bf16[160,1920]{1,0:T(8,128)(2,1)S(1)}, bf16[160,1920]{1,0:T(8,128)(2,1)S(1)}, u32[]{:S(2)}, u32[]{:S(2)}) %collective-permute-start.14) | collective-permute-done | bytes 614432 | tf_op jit(solution)/shard_map/ppermute | solution.py:86
  169.3 7.1 %pad_maximum_fusion.1 = bf16[960,1920]{1,0:T(8,128)(2,1)} fusion(bf16[320,1920]{1,0:T(8,128)(2,1)S(1)} %collective-permute-done.17, bf16[320,1920]{1,0:T(8,128)(2,1)S(1)} %collective-permute-done.16, bf16[160,1920]{1,0:T(8,128)(2,1)S(1)} %collective-permute-done.15, bf16[160,1920]{1,0:T(8,128)(2,1)S(1)} %collective-permute-done.14), kind=kLoop, calls=%fused_computation.35 | loop fusion | flops 14745600 | bytes 7372800 | tf_op jit(solution)/shard_map/concatenate | solution.py:114
  190.9 11.8 %collective-permute-done.19 = bf16[160,1920]{1,0:T(8,128)(2,1)S(1)} collective-permute-done((bf16[160,1920]{1,0:T(8,128)(2,1)S(1)}, bf16[160,1920]{1,0:T(8,128)(2,1)S(1)}, u32[]{:S(2)}, u32[]{:S(2)}) %collective-permute-start.19) | collective-permute-done | bytes 614432 | tf_op jit(solution)/shard_map/ppermute | solution.py:86
  202.6 12.6 %collective-permute-done.20 = bf16[160,1920]{1,0:T(8,128)(2,1)S(1)} collective-permute-done((bf16[160,1920]{1,0:T(8,128)(2,1)S(1)}, bf16[160,1920]{1,0:T(8,128)(2,1)S(1)}, u32[]{:S(2)}, u32[]{:S(2)}) %collective-permute-start.20) | collective-permute-done | bytes 614432 | tf_op jit(solution)/shard_map/ppermute | solution.py:86
  218.8 4.2 constant_dynamic-update-slice_fusion.10
  227.1 4.3 constant_dynamic-slice_fusion.3
  231.4 6.5 %constant_dynamic-slice_fusion.4 = (bf16[512,320]{1,0:T(8,128)(2,1)S(1)}, bf16[512,320]{1,0:T(8,128)(2,1)S(1)}, bf16[512,320]{1,0:T(8,128)(2,1)S(1)}, bf16[512,3...) fusion(bf16[512,5120]{1,0:T(8,128)(2,1)} %all-gather.5.cloned.1, ...), kind=kLoop, calls=%fused_computation.201 | loop fusion | bytes 6553640 | tf_op jit(solution)/shard_map/dynamic_slice | solution.py:192
  237.9 4.3 concatenate.131
  242.2 9.5 %fusion.149 = f32[512,1920]{1,0:T(8,128)} fusion(bf16[512,1920]{1,0:T(8,128)(2,1)S(1)} %concatenate.131, bf16[1920,1920]{1,0:T(8,128)(2,1)} %constant_dynamic-update-slice_fusion.15), kind=kOutput, calls=%fused_computation.260 | convolution fusion | flops 3774873600 | bytes 13271040 | tf_op jit(solution)/shard_map/dot_general | solution.py:196
  257.9 8.5 %fusion.148 = f32[512,1920]{1,0:T(8,128)S(1)} fusion(bf16[512,2560]{1,0:T(8,128)(2,1)S(1)} %concatenate.128, bf16[2560,1920]{1,0:T(8,128)(2,1)} %constant_dynamic-update-slice_fusion.10), kind=kOutput, calls=%fused_computation.259 | convolution fusion | flops 5033164800 | bytes 16384000 | tf_op jit(solution)/shard_map/dot_general | solution.py:196
  279.5 8.2 %all_to_all.12 = bf16[8,1,196608]{2,1,0:T(2,128)(2,1)} reshape(bf16[8,512,3,128]{3,2,1,0:T(4,128)(2,1)} %concatenate.137.clone) | data formatting | bytes 6291456 | tf_op jit(solution)/shard_map/all_to_all | solution.py:207
  288.2 19.7 %reduce.5 = bf16[8,196608]{1,0:T(8,128)(2,1)S(1)} reduce(bf16[8,1,196608]{2,1,0:T(2,128)(2,1)} %all_to_all.12, bf16[]{:T(256)} %broadcast.170), dimensions={1}, to_apply=%all_to_all.12.reduce_sub_computation | reduce | bytes 6291458 | tf_op jit(solution)/shard_map/all_to_all | solution.py:207
  307.9 4.5 reshape.174
  312.4 5.4 %all-to-all-start = ((bf16[8,2,98304]{2,1,0:T(2,128)(2,1)}), bf16[8,2,98304]{2,1,0:T(2,128)(2,1)S(1)}, u32[]{:S(2)}, u32[]{:S(2)}) async-start(bf16[8,2,98304]{2,1,0:T(2,128)(2,1)} %reshape.174), calls=%async_computation | async-start | bytes 6291456 | tf_op jit(solution)/shard_map/all_to_all | solution.py:207
  317.8 38.8 %all-to-all-done = bf16[8,2,98304]{2,1,0:T(2,128)(2,1)S(1)} async-done(((bf16[8,2,98304]{2,1,0:T(2,128)(2,1)}), bf16[8,2,98304]{2,1,0:T(2,128)(2,1)S(1)}, u32[]{:S(2)}, u32[]{:S(2)}) %all-to-all-start) | async-done | bytes 3145760 | tf_op jit(solution)/shard_map/all_to_all | solution.py:207
  356.6 5.3 %reshape.175 = bf16[8,1,196608]{2,1,0:T(2,128)(2,1)} reshape(bf16[8,2,98304]{2,1,0:T(2,128)(2,1)S(1)} %all-to-all-done) | data formatting | bytes 6291456
  361.9 18.8 %reduce.2 = bf16[8,196608]{1,0:T(8,128)(2,1)S(1)} reduce(bf16[8,1,196608]{2,1,0:T(2,128)(2,1)} %reshape.175, bf16[]{:T(256)} %constant.155), dimensions={1}, to_apply=%all_to_all.10.reduce_sub_computation | reduce | bytes 6291458 | tf_op jit(solution)/shard_map/all_to_all | solution.py:207
  380.7 5.6 %reshape.142 = bf16[8,512,3,128]{3,2,1,0:T(4,128)(2,1)} reshape(bf16[8,196608]{1,0:T(8,128)(2,1)S(1)} %reduce.2) | data formatting | bytes 6291456 | tf_op jit(solution)/shard_map/reshape | solution.py:207
  386.3 10.0 %fusion.142 = (bf16[8,512,1,128]{3,2,1,0:T(2,128)(2,1)S(1)}, bf16[8,512,1,128]{3,2,1,0:T(2,128)(2,1)S(1)}, bf16[8,512,1,128]{3,2,1,0:T(2,128)(2,1)S(1)}) fusion(bf16[8,512,3,128]{3,2,1,0:T(4,128)(2,1)} %reshape.142), kind=kLoop, calls=%fused_computation.253 | loop fusion | bytes 6291456 | tf_op jit(solution)/shard_map/slice | solution.py:209
  396.9 41.3 %while.10 = (s32[]{:T(128)}, bf16[8,512,128]{1,2,0:T(8,128)(2,1)}, bf16[8,512,128]{2,1,0:T(8,128)(2,1)S(1)}, bf16[4096,128]{1,0:T(8,128)(2,1)S(1)}, bf16[4096,128]{1,0:T(8,128)(2,1)S(1)}, /*index=5*/s32[]{:T(128)}) while((s32[]{:T(128)}, bf16[8,512,128]{1,2,0:T(8,128)(2,1)}, bf16[8,512,128]{2,1,0:T(8,128)(2,1)S(1)}, ...), condition=%wide.region_5.6_spmd, body=%wide.region_2.5_spmd.sunk | while | flops 1090649600 | bytes 28064328 | solution.py:220
  438.1 19.1 %all_to_all.15 = bf16[8,512,128]{1,2,0:T(8,128)(2,1)S(1)} all-to-all(bf16[8,512,128]{1,2,0:T(8,128)(2,1)} %get-tuple-element.32), channel_id=1, replica_groups=mesh['dp'=4,'head'=4,'ctx'=8] {'ctx'}, dimensions={0} | all-to-all | bytes 2097152 | tf_op jit(solution)/shard_map/all_to_all | solution.py:221
  (251 shorter events, 173.5 us)
Async XLA Ops:
  6.5 70.8 %all-gather.3.cloned.1.call-start = ((), (), s32[]{:S(2)}) async-start(), calls=%async_computation.2 | async-start | bytes 2580480 | tf_op jit(solution)/shard_map/all_gather | solution.py:157
  10.0 10.3 %collective-permute-start = (bf16[6,1,32,96]{3,2,1,0:T(8,128)(2,1)}, bf16[6,1,32,96]{3,2,1,0:T(8,128)(2,1)}, u32[]{:S(2)}, u32[]{:S(2)}) collective-permute-start(bf16[6,1,32,96]{3,2,1,0:T(8,128)(2,1)} %get-tuple-element.94), channel_id=1, source_target_pairs={{0,8},{8,16},{16,24},{1,9},{9,17},{17,25},{2,10},{10,18},{18,26},{... | collective-permute-start | bytes 110600 | tf_op jit(solution)/shard_map/ppermute | solution.py:19
  14.1 7.5 %collective-permute-start.1 = (bf16[6,1,32,96]{3,2,1,0:T(8,128)(2,1)S(1)}, bf16[6,1,32,96]{3,2,1,0:T(8,128)(2,1)}, u32[]{:S(2)}, u32[]{:S(2)}) collective-permute-start(bf16[6,1,32,96]{3,2,1,0:T(8,128)(2,1)S(1)} %get-tuple-element.93), channel_id=1, source_target_pairs={{8,0},{16,8},{24,16},{9,1},{17,9},{25,17},{10,2},{18,10},{26,18},{... | collective-permute-start | bytes 110600 | tf_op jit(solution)/shard_map/ppermute | solution.py:21
  17.4 209.7 %all-gather.5.cloned.1.call-start = ((), (), s32[]{:S(2)}) async-start(), calls=%async_computation.3 | async-start | bytes 6553600 | tf_op jit(solution)/shard_map/all_gather | solution.py:180
  22.5 5.8 %collective-permute-start.2 = (bf16[6,18,1,96]{3,2,1,0:T(2,128)(2,1)S(1)}, bf16[6,18,1,96]{3,2,1,0:T(2,128)(2,1)S(1)}, u32[]{:S(2)}, u32[]{:S(2)}) collective-permute-start(bf16[6,18,1,96]{3,2,1,0:T(2,128)(2,1)S(1)} %get-tuple-element.82), channel_id=1, source_target_pairs={{0,1},{1,2},{2,3},{3,4},{4,5},{5,6},{6,7},{8,9},{9,10},{10,11},{11... | collective-permute-start | bytes 62216 | tf_op jit(solution)/shard_map/ppermute | solution.py:19
  26.0 7.0 %collective-permute-start.3 = (bf16[6,18,1,96]{3,2,1,0:T(2,128)(2,1)S(1)}, bf16[6,18,1,96]{3,2,1,0:T(2,128)(2,1)S(1)}, u32[]{:S(2)}, u32[]{:S(2)}) collective-permute-start(bf16[6,18,1,96]{3,2,1,0:T(2,128)(2,1)S(1)} %get-tuple-element.83), channel_id=1, source_target_pairs={{1,0},{2,1},{3,2},{4,3},{5,4},{6,5},{7,6},{9,8},{10,9},{11,10},{12... | collective-permute-start | bytes 62216 | tf_op jit(solution)/shard_map/ppermute | solution.py:21
  48.6 9.8 %collective-permute-start.4 = (bf16[128,768]{1,0:T(8,128)(2,1)S(1)}, bf16[128,768]{1,0:T(8,128)(2,1)S(1)}, u32[]{:S(2)}, u32[]{:S(2)}) collective-permute-start(bf16[128,768]{1,0:T(8,128)(2,1)S(1)} %reshape.135), channel_id=1, source_target_pairs={{0,8},{8,16},{16,24},{24,0},{1,9},{9,17},{17,25},{25,1},{2,10},{10... | collective-permute-start | bytes 589832 | tf_op jit(solution)/shard_map/ppermute | solution.py:32
  51.3 9.8 %collective-permute-start.5 = (bf16[128,768]{1,0:T(8,128)(2,1)S(1)}, bf16[128,768]{1,0:T(8,128)(2,1)S(1)}, u32[]{:S(2)}, u32[]{:S(2)}) collective-permute-start(bf16[128,768]{1,0:T(8,128)(2,1)S(1)} %reshape.135), channel_id=1, source_target_pairs={{0,16},{8,24},{16,0},{24,8},{1,17},{9,25},{17,1},{25,9},{2,18},{10... | collective-permute-start | bytes 589832 | tf_op jit(solution)/shard_map/ppermute | solution.py:32
  54.1 7.1 %collective-permute-start.6 = (bf16[128,768]{1,0:T(8,128)(2,1)S(1)}, bf16[128,768]{1,0:T(8,128)(2,1)S(1)}, u32[]{:S(2)}, u32[]{:S(2)}) collective-permute-start(bf16[128,768]{1,0:T(8,128)(2,1)S(1)} %reshape.135), channel_id=1, source_target_pairs={{0,24},{8,0},{16,8},{24,16},{1,25},{9,1},{17,9},{25,17},{2,26},{10... | collective-permute-start | bytes 589832 | tf_op jit(solution)/shard_map/ppermute | solution.py:32
  81.9 6.0 %collective-permute-start.7 = (f32[3072]{0:T(1024)S(1)}, f32[3072]{0:T(1024)S(1)}, u32[]{:S(2)}, u32[]{:S(2)}) collective-permute-start(f32[3072]{0:T(1024)S(1)} %pad_maximum_fusion.8), channel_id=1, source_target_pairs={{0,8},{8,16},{16,24},{24,0},{1,9},{9,17},{17,25},{25,1},{2,10},{10... | collective-permute-start | bytes 36872 | tf_op jit(solution)/shard_map/ppermute | solution.py:32
  84.0 5.2 %collective-permute-start.8 = (f32[3072]{0:T(1024)S(1)}, f32[3072]{0:T(1024)S(1)}, u32[]{:S(2)}, u32[]{:S(2)}) collective-permute-start(f32[3072]{0:T(1024)S(1)} %pad_maximum_fusion.8), channel_id=1, source_target_pairs={{0,16},{8,24},{16,0},{24,8},{1,17},{9,25},{17,1},{25,9},{2,18},{10... | collective-permute-start | bytes 36872 | tf_op jit(solution)/shard_map/ppermute | solution.py:32
  101.0 27.4 %collective-permute-start.12 = (bf16[320,1920]{1,0:T(8,128)(2,1)}, bf16[320,1920]{1,0:T(8,128)(2,1)S(1)}, u32[]{:S(2)}, u32[]{:S(2)}) collective-permute-start(bf16[320,1920]{1,0:T(8,128)(2,1)} %copy.40), channel_id=1, source_target_pairs={{0,1},{1,0},{2,3},{3,2},{4,5},{5,4},{6,7},{7,6},{8,9},{9,8},{10,11... | collective-permute-start | bytes 3686408 | tf_op jit(solution)/shard_map/ppermute | solution.py:86
  101.1 30.6 %collective-permute-start.10 = (bf16[320,1920]{1,0:T(8,128)(2,1)}, bf16[320,1920]{1,0:T(8,128)(2,1)S(1)}, u32[]{:S(2)}, u32[]{:S(2)}) collective-permute-start(bf16[320,1920]{1,0:T(8,128)(2,1)} %copy.40), channel_id=1, source_target_pairs={{0,2},{1,3},{2,4},{3,5},{4,6},{5,7},{6,0},{7,1},{8,10},{9,11},{10,... | collective-permute-start | bytes 3686408 | tf_op jit(solution)/shard_map/ppermute | solution.py:86
  102.5 29.2 %collective-permute-start.11 = (bf16[320,1920]{1,0:T(8,128)(2,1)}, bf16[320,1920]{1,0:T(8,128)(2,1)S(1)}, u32[]{:S(2)}, u32[]{:S(2)}) collective-permute-start(bf16[320,1920]{1,0:T(8,128)(2,1)} %copy.40), channel_id=1, source_target_pairs={{0,6},{1,7},{2,0},{3,1},{4,2},{5,3},{6,4},{7,5},{8,14},{9,15},{10,... | collective-permute-start | bytes 3686408 | tf_op jit(solution)/shard_map/ppermute | solution.py:86
  128.4 40.9 %collective-permute-start.16 = (bf16[320,1920]{1,0:T(8,128)(2,1)S(1)}, bf16[320,1920]{1,0:T(8,128)(2,1)S(1)}, u32[]{:S(2)}, u32[]{:S(2)}) collective-permute-start(bf16[320,1920]{1,0:T(8,128)(2,1)S(1)} %collective-permute-done.12), channel_id=1, source_target_pairs={{0,2},{1,3},{2,4},{3,5},{4,6},{5,7},{6,0},{7,1},{8,10},{9,11},{10,... | collective-permute-start | bytes 3686408 | tf_op jit(solution)/shard_map/ppermute | solution.py:86
  128.8 40.5 %collective-permute-start.17 = (bf16[320,1920]{1,0:T(8,128)(2,1)S(1)}, bf16[320,1920]{1,0:T(8,128)(2,1)S(1)}, u32[]{:S(2)}, u32[]{:S(2)}) collective-permute-start(bf16[320,1920]{1,0:T(8,128)(2,1)S(1)} %collective-permute-done.12), channel_id=1, source_target_pairs={{0,6},{1,7},{2,0},{3,1},{4,2},{5,3},{6,4},{7,5},{8,14},{9,15},{10,... | collective-permute-start | bytes 3686408 | tf_op jit(solution)/shard_map/ppermute | solution.py:86
  131.7 37.4 %collective-permute-start.14 = (bf16[160,1920]{1,0:T(8,128)(2,1)S(1)}, bf16[160,1920]{1,0:T(8,128)(2,1)S(1)}, u32[]{:S(2)}, u32[]{:S(2)}) collective-permute-start(bf16[160,1920]{1,0:T(8,128)(2,1)S(1)} %slice.351), channel_id=1, source_target_pairs={{0,2},{1,3},{2,4},{3,5},{4,6},{5,7},{6,0},{7,1},{8,10},{9,11},{10,... | collective-permute-start | bytes 1843208 | tf_op jit(solution)/shard_map/ppermute | solution.py:86
  131.9 37.4 %collective-permute-start.15 = (bf16[160,1920]{1,0:T(8,128)(2,1)S(1)}, bf16[160,1920]{1,0:T(8,128)(2,1)S(1)}, u32[]{:S(2)}, u32[]{:S(2)}) collective-permute-start(bf16[160,1920]{1,0:T(8,128)(2,1)S(1)} %slice.352), channel_id=1, source_target_pairs={{0,6},{1,7},{2,0},{3,1},{4,2},{5,3},{6,4},{7,5},{8,14},{9,15},{10,... | collective-permute-start | bytes 1843208 | tf_op jit(solution)/shard_map/ppermute | solution.py:86
  141.6 77.2 %collective-permute-start.13 = (bf16[960,1920]{1,0:T(8,128)(2,1)}, bf16[960,1920]{1,0:T(8,128)(2,1)}, u32[]{:S(2)}, u32[]{:S(2)}) collective-permute-start(bf16[960,1920]{1,0:T(8,128)(2,1)} %pad_maximum_fusion), channel_id=1, source_target_pairs={{0,32},{32,0},{64,96},{96,64},{1,33},{33,1},{65,97},{97,65},{2,34}... | collective-permute-start | bytes 11059208 | tf_op jit(solution)/shard_map/ppermute | solution.py:89
  176.4 46.6 %collective-permute-start.18 = (bf16[960,1920]{1,0:T(8,128)(2,1)}, bf16[960,1920]{1,0:T(8,128)(2,1)}, u32[]{:S(2)}, u32[]{:S(2)}) collective-permute-start(bf16[960,1920]{1,0:T(8,128)(2,1)} %pad_maximum_fusion.1), channel_id=1, source_target_pairs={{0,32},{32,0},{64,96},{96,64},{1,33},{33,1},{65,97},{97,65},{2,34}... | collective-permute-start | bytes 11059208 | tf_op jit(solution)/shard_map/ppermute | solution.py:89
  186.0 16.7 %collective-permute-start.19 = (bf16[160,1920]{1,0:T(8,128)(2,1)S(1)}, bf16[160,1920]{1,0:T(8,128)(2,1)S(1)}, u32[]{:S(2)}, u32[]{:S(2)}) collective-permute-start(bf16[160,1920]{1,0:T(8,128)(2,1)S(1)} %collective-permute-done.14), channel_id=1, source_target_pairs={{0,1},{1,0},{2,3},{3,2},{4,5},{5,4},{6,7},{7,6},{8,9},{9,8},{10,11... | collective-permute-start | bytes 1843208 | tf_op jit(solution)/shard_map/ppermute | solution.py:86
  187.6 27.7 %collective-permute-start.20 = (bf16[160,1920]{1,0:T(8,128)(2,1)S(1)}, bf16[160,1920]{1,0:T(8,128)(2,1)S(1)}, u32[]{:S(2)}, u32[]{:S(2)}) collective-permute-start(bf16[160,1920]{1,0:T(8,128)(2,1)S(1)} %copy-done.13), channel_id=1, source_target_pairs={{0,1},{1,0},{2,3},{3,2},{4,5},{5,4},{6,7},{7,6},{8,9},{9,8},{10,11... | collective-permute-start | bytes 1843208 | tf_op jit(solution)/shard_map/ppermute | solution.py:86
  216.5 49.9 %collective-permute-start.21 = (bf16[320,1920]{1,0:T(8,128)(2,1)}, bf16[320,1920]{1,0:T(8,128)(2,1)}, u32[]{:S(2)}, u32[]{:S(2)}) collective-permute-start(bf16[320,1920]{1,0:T(8,128)(2,1)} %pad_maximum_fusion.4), channel_id=1, source_target_pairs={{0,32},{32,0},{64,96},{96,64},{1,33},{33,1},{65,97},{97,65},{2,34}... | collective-permute-start | bytes 3686408 | tf_op jit(solution)/shard_map/ppermute | solution.py:89
  312.4 44.2 %all-to-all-start = ((bf16[8,2,98304]{2,1,0:T(2,128)(2,1)}), bf16[8,2,98304]{2,1,0:T(2,128)(2,1)S(1)}, u32[]{:S(2)}, u32[]{:S(2)}) async-start(bf16[8,2,98304]{2,1,0:T(2,128)(2,1)} %reshape.174), calls=%async_computation | async-start | bytes 6291456 | tf_op jit(solution)/shard_map/all_to_all | solution.py:207
  (31 other events, 319.5 us)
Sparse Core Ops, SparseCore 0:
  17.5 59.8 all-gather.2
  93.0 55.8 all-gather.4

commit v9 on v6

--- a/solution.py
+++ b/solution.py
@@ -217,7 +217,8 @@
         accum = jnp.dot(probs.astype(jnp.bfloat16), values, preferred_element_type=jnp.float32)
         return (accum / denom[:, None]).astype(jnp.bfloat16)
 
-    attended = jnp.stack([one_block(triple[s, 0]) for s in range(triple.shape[0])])
+    queries = lax.optimization_barrier(triple[:, 0].reshape(-1, HDIM)).reshape(triple.shape[0], -1, HDIM)
+    attended = lax.map(one_block, queries)
     by_head = lax.all_to_all(attended, "ctx", 0, 0, tiled=True)[:heads_here]
     return by_head.transpose(1, 0, 2).reshape(group_rows, heads_here * HDIM)
 

time: 444 us -> 406 us (0.914)
  blocking collectives: 61.7 us -> 19.3 us
  waiting for transfers between devices: 104 us -> 141 us
  matrix products: 100 us -> 66 us
  other arithmetic: 51.5 us -> 35.8 us
  local copies, waits for them, and re-layouts: 72.7 us -> 84 us
  starting transfers between devices: 33.3 us -> 40.3 us
    all_to_all x1 -> x0, blocking collectives: 43.7 us -> none  [shards(): triple = lax.all_to_all(outgoing, 'ctx', 0, 0, tiled=True)]
    all_to_all x0 -> x1, waiting for transfers between devices: none -> 38.8 us  [shards(): triple = lax.all_to_all(outgoing, 'ctx', 0, 0, tiled=True)]
    dot_general x8, matrix products: 29.4 us -> 12 us  [one_block(): jnp.dot(probs.astype(jnp.bfloat16), values, preferred_element_type=jnp.fl...]
    reduce_sum x8, other arithmetic: 28.9 us -> 12.1 us  [one_block(): denom = jnp.sum(probs, -1)]
    dot_general x8, matrix products: 34 us -> 17.9 us  [one_block(): jnp.dot(query, keys.T, preferred_element_type=jnp.float32) * inv_root]
    dynamic_update_slice x0 -> x16, local copies, waits for them, and re-layouts: none -> 6.21 us  [shards(): attended = lax.map(one_block, queries)]
    all_to_all x0 -> x1, starting transfers between devices: none -> 5.42 us  [shards(): triple = lax.all_to_all(outgoing, 'ctx', 0, 0, tiled=True)]
    unnamed x72 -> x76, local copies, waits for them, and re-layouts: 18.2 us -> 17.8 us
  transfers between devices with their start and end apart: 24 -> 25, of which waited for: 11 -> 12; matrix products, arithmetic and copies ran while one was open for 25% -> 28% of each run, Pallas kernels for 0% -> 0%
where the time goes in v9:
time: 406 us; the launch traced here: 401 us
  waiting for transfers between devices  141 us (35%)
  local copies, waits for them, and re-layouts  84 us (21%)
  matrix products  66 us (16%)
  starting transfers between devices  40.3 us (10%)
  other arithmetic  35.8 us (9%)
  blocking collectives  19.3 us (5%)
  between operations  15.2 us (4%)
    ppermute x9, waiting for transfers between devices, send(): return lax.ppermute(cells, 'ctx', [(i, step(i)) for i in range(n_ctx)])  76.1 us
    all_to_all x1, waiting for transfers between devices, shards(): triple = lax.all_to_all(outgoing, 'ctx', 0, 0, tiled=True)  38.8 us
    dot_general x3, matrix products, shards(): jnp.dot(jnp.concatenate(columns, 1), jnp.concatenate(weights, 0), preferr...  22.6 us
    all_to_all x1, blocking collectives, shards(): by_head = lax.all_to_all(attended, 'ctx', 0, 0, tiled=True)[:heads_here]  19.3 us
    dot_general x8, matrix products, one_block(): jnp.dot(query, keys.T, preferred_element_type=jnp.float32) * inv_root  17.9 us
    unnamed x76, local copies, waits for them, and re-layouts  17.8 us
    concatenate x3, other arithmetic, shards(): jnp.concatenate([cells for cells, _, _ in s], 0)  14.7 us
    all_gather x1, waiting for transfers between devices, shards(): lax.all_gather(jnp.concatenate([patch_weight, share_parts], 0), 'ctx', ax...  13.8 us
  transfers between devices with their start and end apart: 25, of which 12 were waited for; matrix products, arithmetic and copies ran while one was open for 28% of the time, Pallas kernels for 0%

profile of v9, /device:TPU:0, one launch (start us, length us, event | category | flops | bytes accessed | tf_op | source)
XLA Modules:
  0.0 401.3 jit_solution(15853145881550267706)
XLA Ops:
  10.0 4.1 %collective-permute-start = (bf16[6,1,32,96]{3,2,1,0:T(8,128)(2,1)}, bf16[6,1,32,96]{3,2,1,0:T(8,128)(2,1)}, u32[]{:S(2)}, u32[]{:S(2)}) collective-permute-start(bf16[6,1,32,96]{3,2,1,0:T(8,128)(2,1)} %get-tuple-element.94), channel_id=1, source_target_pairs={{0,8},{8,16},{16,24},{1,9},{9,17},{17,25},{2,10},{10,18},{18,26},{... | collective-permute-start | bytes 110600 | tf_op jit(solution)/shard_map/ppermute | solution.py:19
  22.6 3.5 collective-permute-start.2
  57.7 4.0 collective-permute-done.5
  63.6 13.8 %all-gather.3.cloned.1.call-done = bf16[774,1280]{0,1:T(8,128)(2,1)} async-done(((bf16[774,160]{0,1:T(8,128)(2,1)}), bf16[774,1280]{0,1:T(8,128)(2,1)}) %all-gather.3.cloned.1.call-update) | async-done | bytes 1981456 | tf_op jit(solution)/shard_map/all_gather | solution.py:157
  92.9 3.9 copy.43
  104.3 24.1 %collective-permute-done.12 = bf16[320,1920]{1,0:T(8,128)(2,1)S(1)} collective-permute-done((bf16[320,1920]{1,0:T(8,128)(2,1)}, bf16[320,1920]{1,0:T(8,128)(2,1)S(1)}, u32[]{:S(2)}, u32[]{:S(2)}) %collective-permute-start.12) | collective-permute-done | bytes 1228832 | tf_op jit(solution)/shard_map/ppermute | solution.py:86
  135.1 6.4 %pad_maximum_fusion = bf16[960,1920]{1,0:T(8,128)(2,1)} fusion(bf16[320,1920]{1,0:T(8,128)(2,1)S(1)} %collective-permute-done.12, bf16[320,1920]{1,0:T(8,128)(2,1)S(1)} %collective-permute-done.11, bf16[320,1920]{1,0:T(8,128)(2,1)S(1)} %collective-permute-done.10), kind=kLoop, calls=%fused_computation.34 | loop fusion | flops 11059200 | bytes 7372800 | tf_op jit(solution)/shard_map/concatenate | solution.py:114
  141.7 27.5 %collective-permute-done.14 = bf16[160,1920]{1,0:T(8,128)(2,1)S(1)} collective-permute-done((bf16[160,1920]{1,0:T(8,128)(2,1)S(1)}, bf16[160,1920]{1,0:T(8,128)(2,1)S(1)}, u32[]{:S(2)}, u32[]{:S(2)}) %collective-permute-start.14) | collective-permute-done | bytes 614432 | tf_op jit(solution)/shard_map/ppermute | solution.py:86
  169.4 7.1 %pad_maximum_fusion.1 = bf16[960,1920]{1,0:T(8,128)(2,1)} fusion(bf16[320,1920]{1,0:T(8,128)(2,1)S(1)} %collective-permute-done.17, bf16[320,1920]{1,0:T(8,128)(2,1)S(1)} %collective-permute-done.16, bf16[160,1920]{1,0:T(8,128)(2,1)S(1)} %collective-permute-done.15, bf16[160,1920]{1,0:T(8,128)(2,1)S(1)} %collective-permute-done.14), kind=kLoop, calls=%fused_computation.35 | loop fusion | flops 14745600 | bytes 7372800 | tf_op jit(solution)/shard_map/concatenate | solution.py:114
  190.9 11.7 %collective-permute-done.19 = bf16[160,1920]{1,0:T(8,128)(2,1)S(1)} collective-permute-done((bf16[160,1920]{1,0:T(8,128)(2,1)S(1)}, bf16[160,1920]{1,0:T(8,128)(2,1)S(1)}, u32[]{:S(2)}, u32[]{:S(2)}) %collective-permute-start.19) | collective-permute-done | bytes 614432 | tf_op jit(solution)/shard_map/ppermute | solution.py:86
  202.7 12.6 %collective-permute-done.20 = bf16[160,1920]{1,0:T(8,128)(2,1)S(1)} collective-permute-done((bf16[160,1920]{1,0:T(8,128)(2,1)S(1)}, bf16[160,1920]{1,0:T(8,128)(2,1)S(1)}, u32[]{:S(2)}, u32[]{:S(2)}) %collective-permute-start.20) | collective-permute-done | bytes 614432 | tf_op jit(solution)/shard_map/ppermute | solution.py:86
  218.8 4.2 %constant_dynamic-update-slice_fusion.10 = bf16[2560,1920]{1,0:T(8,128)(2,1)} fusion(bf16[2560,1920]{1,0:T(8,128)(2,1)} %constant_dynamic-update-slice_fusion.11, bf16[960,1920]{1,0:T(8,128)(2,1)} %collective-permute-done.13), kind=kLoop, calls=%fused_computation.176 | loop fusion | bytes 7372800 | tf_op jit(solution)/shard_map/concatenate | solution.py:198
  223.0 4.1 %constant_dynamic-update-slice_fusion.15 = bf16[1920,1920]{1,0:T(8,128)(2,1)} fusion(bf16[1920,1920]{1,0:T(8,128)(2,1)} %constant_dynamic-update-slice_fusion.16, bf16[960,1920]{1,0:T(8,128)(2,1)} %collective-permute-done.18), kind=kLoop, calls=%fused_computation.181 | loop fusion | bytes 7372800 | tf_op jit(solution)/shard_map/concatenate | solution.py:198
  227.1 4.5 %constant_dynamic-slice_fusion.3 = (bf16[512,160]{1,0:T(8,128)(2,1)}, bf16[512,160]{1,0:T(8,128)(2,1)}, bf16[512,160]{1,0:T(8,128)(2,1)}, bf16[512,160]{1,0:T(8,...) fusion(bf16[512,5120]{1,0:T(8,128)(2,1)} %all-gather.5.cloned.1, ...), kind=kLoop, calls=%fused_computation.199 | loop fusion | bytes 2621472 | tf_op jit(solution)/shard_map/dynamic_slice | solution.py:192
  231.6 6.4 %constant_dynamic-slice_fusion.4 = (bf16[512,320]{1,0:T(8,128)(2,1)S(1)}, bf16[512,320]{1,0:T(8,128)(2,1)S(1)}, bf16[512,320]{1,0:T(8,128)(2,1)S(1)}, bf16[512,3...) fusion(bf16[512,5120]{1,0:T(8,128)(2,1)} %all-gather.5.cloned.1, ...), kind=kLoop, calls=%fused_computation.200 | loop fusion | bytes 6553640 | tf_op jit(solution)/shard_map/dynamic_slice | solution.py:192
  238.0 4.2 %concatenate.131 = bf16[512,1920]{1,0:T(8,128)(2,1)S(1)} concatenate(bf16[512,160]{1,0:T(8,128)(2,1)} %get-tuple-element.52, bf16[512,160]{1,0:T(8,128)(2,1)} %get-tuple-element.51, bf16[512,320]{1,0:T(8,128)(2,1)} %get-tuple-element.56, bf16[512,320]{1,0:T(8,128)(2,1)S(1)} %get-tuple-element.55, bf16[512,160]{1,0:T(8,128)(2,1)} %get-tuple-element.50, ...), dimensions={1} | concatenate | bytes 3932160 | tf_op jit(solution)/shard_map/concatenate | solution.py:197
  242.2 9.5 %fusion.149 = f32[512,1920]{1,0:T(8,128)} fusion(bf16[512,1920]{1,0:T(8,128)(2,1)S(1)} %concatenate.131, bf16[1920,1920]{1,0:T(8,128)(2,1)} %constant_dynamic-update-slice_fusion.15), kind=kOutput, calls=%fused_computation.259 | convolution fusion | flops 3774873600 | bytes 13271040 | tf_op jit(solution)/shard_map/dot_general | solution.py:196
  253.7 4.1 %concatenate.128 = bf16[512,2560]{1,0:T(8,128)(2,1)S(1)} concatenate(bf16[512,640]{1,0:T(8,128)(2,1)} %constant_dynamic-slice_fusion.19, bf16[512,320]{1,0:T(8,128)(2,1)} %get-tuple-element.62, bf16[512,320]{1,0:T(8,128)(2,1)} %get-tuple-element.61, bf16[512,320]{1,0:T(8,128)(2,1)} %get-tuple-element.60, bf16[512,320]{1,0:T(8,128)(2,1)} %get-tuple-element.59, ...), dimensions={1} | concatenate | bytes 5242880 | tf_op jit(solution)/shard_map/concatenate | solution.py:197
  257.9 8.5 %fusion.148 = f32[512,1920]{1,0:T(8,128)S(1)} fusion(bf16[512,2560]{1,0:T(8,128)(2,1)S(1)} %concatenate.128, bf16[2560,1920]{1,0:T(8,128)(2,1)} %constant_dynamic-update-slice_fusion.10), kind=kOutput, calls=%fused_computation.258 | convolution fusion | flops 5033164800 | bytes 16384000 | tf_op jit(solution)/shard_map/dot_general | solution.py:196
  266.5 4.6 %add_convert_fusion = bf16[512,1920]{1,0:T(8,128)(2,1)} fusion(f32[512,1920]{1,0:T(8,128)S(1)} %fusion.148, f32[512,1920]{1,0:T(8,128)S(1)} %copy-done.31, bf16[320,1920]{1,0:T(8,128)(2,1)} %collective-permute-done.21, bf16[160,1920]{1,0:T(8,128)(2,1)S(1)} %copy-done.21, bf16[160,1920]{1,0:T(8,128)(2,1)S(1)} %copy-done.19, ...), kind=kOutput, calls=%fused_computation.17 | convolution fusion | flops 1271234560 | bytes 12943360 | tf_op jit(solution)/shard_map/dot_general | solution.py:196
  275.7 5.4 %all-to-all-start = ((bf16[8,3,512,128]{2,3,1,0:T(8,128)(2,1)}), bf16[8,3,512,128]{2,3,1,0:T(8,128)(2,1)S(1)}, u32[]{:S(2)}, u32[]{:S(2)}) async-start(bf16[8,3,512,128]{2,3,1,0:T(8,128)(2,1)} %concatenate.137), calls=%async_computation | async-start | bytes 6291456 | tf_op jit(solution)/shard_map/all_to_all | solution.py:207
  281.1 38.8 %all-to-all-done = bf16[8,3,512,128]{2,3,1,0:T(8,128)(2,1)S(1)} async-done(((bf16[8,3,512,128]{2,3,1,0:T(8,128)(2,1)}), bf16[8,3,512,128]{2,3,1,0:T(8,128)(2,1)S(1)}, u32[]{:S(2)}, u32[]{:S(2)}) %all-to-all-start) | async-done | bytes 3145760 | tf_op jit(solution)/shard_map/all_to_all | solution.py:207
  325.5 48.3 %while.10 = (s32[]{:T(128)}, bf16[8,512,128]{1,2,0:T(8,128)(2,1)}, bf16[8,512,128]{2,1,0:T(8,128)(2,1)}, bf16[4096,128]{1,0:T(8,128)(2,1)S(1)}, bf16[4096,128]{1,0:T(8,128)(2,1)S(1)}, /*index=5*/s32[]{:T(128)}) while((s32[]{:T(128)}, bf16[8,512,128]{1,2,0:T(8,128)(2,1)}, bf16[8,512,128]{2,1,0:T(8,128)(2,1)}, bf16[4096,128]{1,0:T(8,128)(2,1)S(1)}, ...), condition=%wide.region_5.6_spmd, body=%wide.region_2.5_spmd.sunk | while | flops 1090649600 | bytes 28064836 | solution.py:221
  373.8 19.3 %all_to_all.10 = bf16[8,512,128]{1,2,0:T(8,128)(2,1)S(1)} all-to-all(bf16[8,512,128]{1,2,0:T(8,128)(2,1)} %get-tuple-element.32), channel_id=1, replica_groups=mesh['dp'=4,'head'=4,'ctx'=8] {'ctx'}, dimensions={0} | all-to-all | bytes 2097152 | tf_op jit(solution)/shard_map/all_to_all | solution.py:222
  (247 shorter events, 153.7 us)
Async XLA Ops:
  6.5 70.9 %all-gather.3.cloned.1.call-start = ((), (), s32[]{:S(2)}) async-start(), calls=%async_computation.2 | async-start | bytes 2580480 | tf_op jit(solution)/shard_map/all_gather | solution.py:157
  10.0 10.3 %collective-permute-start = (bf16[6,1,32,96]{3,2,1,0:T(8,128)(2,1)}, bf16[6,1,32,96]{3,2,1,0:T(8,128)(2,1)}, u32[]{:S(2)}, u32[]{:S(2)}) collective-permute-start(bf16[6,1,32,96]{3,2,1,0:T(8,128)(2,1)} %get-tuple-element.94), channel_id=1, source_target_pairs={{0,8},{8,16},{16,24},{1,9},{9,17},{17,25},{2,10},{10,18},{18,26},{... | collective-permute-start | bytes 110600 | tf_op jit(solution)/shard_map/ppermute | solution.py:19
  14.1 7.6 %collective-permute-start.1 = (bf16[6,1,32,96]{3,2,1,0:T(8,128)(2,1)S(1)}, bf16[6,1,32,96]{3,2,1,0:T(8,128)(2,1)}, u32[]{:S(2)}, u32[]{:S(2)}) collective-permute-start(bf16[6,1,32,96]{3,2,1,0:T(8,128)(2,1)S(1)} %get-tuple-element.93), channel_id=1, source_target_pairs={{8,0},{16,8},{24,16},{9,1},{17,9},{25,17},{10,2},{18,10},{26,18},{... | collective-permute-start | bytes 110600 | tf_op jit(solution)/shard_map/ppermute | solution.py:21
  17.4 209.8 %all-gather.5.cloned.1.call-start = ((), (), s32[]{:S(2)}) async-start(), calls=%async_computation.3 | async-start | bytes 6553600 | tf_op jit(solution)/shard_map/all_gather | solution.py:180
  22.6 5.8 %collective-permute-start.2 = (bf16[6,18,1,96]{3,2,1,0:T(2,128)(2,1)S(1)}, bf16[6,18,1,96]{3,2,1,0:T(2,128)(2,1)S(1)}, u32[]{:S(2)}, u32[]{:S(2)}) collective-permute-start(bf16[6,18,1,96]{3,2,1,0:T(2,128)(2,1)S(1)} %get-tuple-element.82), channel_id=1, source_target_pairs={{0,1},{1,2},{2,3},{3,4},{4,5},{5,6},{6,7},{8,9},{9,10},{10,11},{11... | collective-permute-start | bytes 62216 | tf_op jit(solution)/shard_map/ppermute | solution.py:19
  26.1 7.0 %collective-permute-start.3 = (bf16[6,18,1,96]{3,2,1,0:T(2,128)(2,1)S(1)}, bf16[6,18,1,96]{3,2,1,0:T(2,128)(2,1)S(1)}, u32[]{:S(2)}, u32[]{:S(2)}) collective-permute-start(bf16[6,18,1,96]{3,2,1,0:T(2,128)(2,1)S(1)} %get-tuple-element.83), channel_id=1, source_target_pairs={{1,0},{2,1},{3,2},{4,3},{5,4},{6,5},{7,6},{9,8},{10,9},{11,10},{12... | collective-permute-start | bytes 62216 | tf_op jit(solution)/shard_map/ppermute | solution.py:21
  48.7 9.1 %collective-permute-start.4 = (bf16[128,768]{1,0:T(8,128)(2,1)S(1)}, bf16[128,768]{1,0:T(8,128)(2,1)S(1)}, u32[]{:S(2)}, u32[]{:S(2)}) collective-permute-start(bf16[128,768]{1,0:T(8,128)(2,1)S(1)} %reshape.130), channel_id=1, source_target_pairs={{0,8},{8,16},{16,24},{24,0},{1,9},{9,17},{17,25},{25,1},{2,10},{10... | collective-permute-start | bytes 589832 | tf_op jit(solution)/shard_map/ppermute | solution.py:32
  51.4 10.3 %collective-permute-start.5 = (bf16[128,768]{1,0:T(8,128)(2,1)S(1)}, bf16[128,768]{1,0:T(8,128)(2,1)S(1)}, u32[]{:S(2)}, u32[]{:S(2)}) collective-permute-start(bf16[128,768]{1,0:T(8,128)(2,1)S(1)} %reshape.130), channel_id=1, source_target_pairs={{0,16},{8,24},{16,0},{24,8},{1,17},{9,25},{17,1},{25,9},{2,18},{10... | collective-permute-start | bytes 589832 | tf_op jit(solution)/shard_map/ppermute | solution.py:32
  54.2 7.5 %collective-permute-start.6 = (bf16[128,768]{1,0:T(8,128)(2,1)S(1)}, bf16[128,768]{1,0:T(8,128)(2,1)S(1)}, u32[]{:S(2)}, u32[]{:S(2)}) collective-permute-start(bf16[128,768]{1,0:T(8,128)(2,1)S(1)} %reshape.130), channel_id=1, source_target_pairs={{0,24},{8,0},{16,8},{24,16},{1,25},{9,1},{17,9},{25,17},{2,26},{10... | collective-permute-start | bytes 589832 | tf_op jit(solution)/shard_map/ppermute | solution.py:32
  82.0 6.0 %collective-permute-start.7 = (f32[3072]{0:T(1024)S(1)}, f32[3072]{0:T(1024)S(1)}, u32[]{:S(2)}, u32[]{:S(2)}) collective-permute-start(f32[3072]{0:T(1024)S(1)} %pad_maximum_fusion.8), channel_id=1, source_target_pairs={{0,8},{8,16},{16,24},{24,0},{1,9},{9,17},{17,25},{25,1},{2,10},{10... | collective-permute-start | bytes 36872 | tf_op jit(solution)/shard_map/ppermute | solution.py:32
  84.0 5.2 %collective-permute-start.8 = (f32[3072]{0:T(1024)S(1)}, f32[3072]{0:T(1024)S(1)}, u32[]{:S(2)}, u32[]{:S(2)}) collective-permute-start(f32[3072]{0:T(1024)S(1)} %pad_maximum_fusion.8), channel_id=1, source_target_pairs={{0,16},{8,24},{16,0},{24,8},{1,17},{9,25},{17,1},{25,9},{2,18},{10... | collective-permute-start | bytes 36872 | tf_op jit(solution)/shard_map/ppermute | solution.py:32
  101.1 27.4 %collective-permute-start.12 = (bf16[320,1920]{1,0:T(8,128)(2,1)}, bf16[320,1920]{1,0:T(8,128)(2,1)S(1)}, u32[]{:S(2)}, u32[]{:S(2)}) collective-permute-start(bf16[320,1920]{1,0:T(8,128)(2,1)} %copy.44), channel_id=1, source_target_pairs={{0,1},{1,0},{2,3},{3,2},{4,5},{5,4},{6,7},{7,6},{8,9},{9,8},{10,11... | collective-permute-start | bytes 3686408 | tf_op jit(solution)/shard_map/ppermute | solution.py:86
  101.1 30.6 %collective-permute-start.10 = (bf16[320,1920]{1,0:T(8,128)(2,1)}, bf16[320,1920]{1,0:T(8,128)(2,1)S(1)}, u32[]{:S(2)}, u32[]{:S(2)}) collective-permute-start(bf16[320,1920]{1,0:T(8,128)(2,1)} %copy.44), channel_id=1, source_target_pairs={{0,2},{1,3},{2,4},{3,5},{4,6},{5,7},{6,0},{7,1},{8,10},{9,11},{10,... | collective-permute-start | bytes 3686408 | tf_op jit(solution)/shard_map/ppermute | solution.py:86
  102.6 29.2 %collective-permute-start.11 = (bf16[320,1920]{1,0:T(8,128)(2,1)}, bf16[320,1920]{1,0:T(8,128)(2,1)S(1)}, u32[]{:S(2)}, u32[]{:S(2)}) collective-permute-start(bf16[320,1920]{1,0:T(8,128)(2,1)} %copy.44), channel_id=1, source_target_pairs={{0,6},{1,7},{2,0},{3,1},{4,2},{5,3},{6,4},{7,5},{8,14},{9,15},{10,... | collective-permute-start | bytes 3686408 | tf_op jit(solution)/shard_map/ppermute | solution.py:86
  128.4 40.9 %collective-permute-start.16 = (bf16[320,1920]{1,0:T(8,128)(2,1)S(1)}, bf16[320,1920]{1,0:T(8,128)(2,1)S(1)}, u32[]{:S(2)}, u32[]{:S(2)}) collective-permute-start(bf16[320,1920]{1,0:T(8,128)(2,1)S(1)} %collective-permute-done.12), channel_id=1, source_target_pairs={{0,2},{1,3},{2,4},{3,5},{4,6},{5,7},{6,0},{7,1},{8,10},{9,11},{10,... | collective-permute-start | bytes 3686408 | tf_op jit(solution)/shard_map/ppermute | solution.py:86
  128.8 40.5 %collective-permute-start.17 = (bf16[320,1920]{1,0:T(8,128)(2,1)S(1)}, bf16[320,1920]{1,0:T(8,128)(2,1)S(1)}, u32[]{:S(2)}, u32[]{:S(2)}) collective-permute-start(bf16[320,1920]{1,0:T(8,128)(2,1)S(1)} %collective-permute-done.12), channel_id=1, source_target_pairs={{0,6},{1,7},{2,0},{3,1},{4,2},{5,3},{6,4},{7,5},{8,14},{9,15},{10,... | collective-permute-start | bytes 3686408 | tf_op jit(solution)/shard_map/ppermute | solution.py:86
  131.7 37.4 %collective-permute-start.14 = (bf16[160,1920]{1,0:T(8,128)(2,1)S(1)}, bf16[160,1920]{1,0:T(8,128)(2,1)S(1)}, u32[]{:S(2)}, u32[]{:S(2)}) collective-permute-start(bf16[160,1920]{1,0:T(8,128)(2,1)S(1)} %slice.351), channel_id=1, source_target_pairs={{0,2},{1,3},{2,4},{3,5},{4,6},{5,7},{6,0},{7,1},{8,10},{9,11},{10,... | collective-permute-start | bytes 1843208 | tf_op jit(solution)/shard_map/ppermute | solution.py:86
  131.9 37.5 %collective-permute-start.15 = (bf16[160,1920]{1,0:T(8,128)(2,1)S(1)}, bf16[160,1920]{1,0:T(8,128)(2,1)S(1)}, u32[]{:S(2)}, u32[]{:S(2)}) collective-permute-start(bf16[160,1920]{1,0:T(8,128)(2,1)S(1)} %slice.352), channel_id=1, source_target_pairs={{0,6},{1,7},{2,0},{3,1},{4,2},{5,3},{6,4},{7,5},{8,14},{9,15},{10,... | collective-permute-start | bytes 1843208 | tf_op jit(solution)/shard_map/ppermute | solution.py:86
  141.6 77.2 %collective-permute-start.13 = (bf16[960,1920]{1,0:T(8,128)(2,1)}, bf16[960,1920]{1,0:T(8,128)(2,1)}, u32[]{:S(2)}, u32[]{:S(2)}) collective-permute-start(bf16[960,1920]{1,0:T(8,128)(2,1)} %pad_maximum_fusion), channel_id=1, source_target_pairs={{0,32},{32,0},{64,96},{96,64},{1,33},{33,1},{65,97},{97,65},{2,34}... | collective-permute-start | bytes 11059208 | tf_op jit(solution)/shard_map/ppermute | solution.py:89
  176.4 46.6 %collective-permute-start.18 = (bf16[960,1920]{1,0:T(8,128)(2,1)}, bf16[960,1920]{1,0:T(8,128)(2,1)}, u32[]{:S(2)}, u32[]{:S(2)}) collective-permute-start(bf16[960,1920]{1,0:T(8,128)(2,1)} %pad_maximum_fusion.1), channel_id=1, source_target_pairs={{0,32},{32,0},{64,96},{96,64},{1,33},{33,1},{65,97},{97,65},{2,34}... | collective-permute-start | bytes 11059208 | tf_op jit(solution)/shard_map/ppermute | solution.py:89
  186.0 16.7 %collective-permute-start.19 = (bf16[160,1920]{1,0:T(8,128)(2,1)S(1)}, bf16[160,1920]{1,0:T(8,128)(2,1)S(1)}, u32[]{:S(2)}, u32[]{:S(2)}) collective-permute-start(bf16[160,1920]{1,0:T(8,128)(2,1)S(1)} %collective-permute-done.14), channel_id=1, source_target_pairs={{0,1},{1,0},{2,3},{3,2},{4,5},{5,4},{6,7},{7,6},{8,9},{9,8},{10,11... | collective-permute-start | bytes 1843208 | tf_op jit(solution)/shard_map/ppermute | solution.py:86
  187.5 27.7 %collective-permute-start.20 = (bf16[160,1920]{1,0:T(8,128)(2,1)S(1)}, bf16[160,1920]{1,0:T(8,128)(2,1)S(1)}, u32[]{:S(2)}, u32[]{:S(2)}) collective-permute-start(bf16[160,1920]{1,0:T(8,128)(2,1)S(1)} %copy-done.15), channel_id=1, source_target_pairs={{0,1},{1,0},{2,3},{3,2},{4,5},{5,4},{6,7},{7,6},{8,9},{9,8},{10,11... | collective-permute-start | bytes 1843208 | tf_op jit(solution)/shard_map/ppermute | solution.py:86
  216.5 50.0 %collective-permute-start.21 = (bf16[320,1920]{1,0:T(8,128)(2,1)}, bf16[320,1920]{1,0:T(8,128)(2,1)}, u32[]{:S(2)}, u32[]{:S(2)}) collective-permute-start(bf16[320,1920]{1,0:T(8,128)(2,1)} %pad_maximum_fusion.4), channel_id=1, source_target_pairs={{0,32},{32,0},{64,96},{96,64},{1,33},{33,1},{65,97},{97,65},{2,34}... | collective-permute-start | bytes 3686408 | tf_op jit(solution)/shard_map/ppermute | solution.py:89
  275.7 44.3 %all-to-all-start = ((bf16[8,3,512,128]{2,3,1,0:T(8,128)(2,1)}), bf16[8,3,512,128]{2,3,1,0:T(8,128)(2,1)S(1)}, u32[]{:S(2)}, u32[]{:S(2)}) async-start(bf16[8,3,512,128]{2,3,1,0:T(8,128)(2,1)} %concatenate.137), calls=%async_computation | async-start | bytes 6291456 | tf_op jit(solution)/shard_map/all_to_all | solution.py:207
  (33 other events, 325.1 us)
Sparse Core Ops, SparseCore 0:
  17.5 59.8 all-gather.2
  93.0 55.8 all-gather.4

commit v10 on v3

--- a/solution.py
+++ b/solution.py
@@ -211,7 +211,7 @@
 
     def one_block(query):
         scores = jnp.dot(query, keys.T, preferred_element_type=jnp.float32) * inv_root
-        best = jnp.maximum(jnp.float32(-1e30), jnp.max(scores, -1))
+        best = jnp.max(scores, -1)
         probs = jnp.exp(scores - best[:, None])
         denom = jnp.sum(probs, -1)
         accum = jnp.dot(probs.astype(jnp.bfloat16), values, preferred_element_type=jnp.float32)

time: 405 us -> 405 us (level)
  no operation moved by 1% of the time
where the time goes in v10:
time: 405 us; the launch traced here: 400 us
  waiting for transfers between devices  141 us (35%)
  local copies, waits for them, and re-layouts  82.5 us (20%)
  matrix products  66.3 us (16%)
  starting transfers between devices  40.5 us (10%)
  other arithmetic  35.6 us (9%)
  blocking collectives  19.3 us (5%)
  between operations  15.2 us (4%)
    ppermute x9, waiting for transfers between devices, send(): return lax.ppermute(cells, 'ctx', [(i, step(i)) for i in range(n_ctx)])  76.1 us
    all_to_all x1, waiting for transfers between devices, shards(): triple = lax.all_to_all(outgoing, 'ctx', 0, 0, tiled=True)  38.9 us
    dot_general x3, matrix products, shards(): jnp.dot(jnp.concatenate(columns, 1), jnp.concatenate(weights, 0), preferr...  22.6 us
    all_to_all x1, blocking collectives, shards(): by_head = lax.all_to_all(attended, 'ctx', 0, 0, tiled=True)[:heads_here]  19.3 us
    dot_general x8, matrix products, one_block(): jnp.dot(query, keys.T, preferred_element_type=jnp.float32) * inv_root  18.1 us
    unnamed x74, local copies, waits for them, and re-layouts  17.8 us
    concatenate x3, other arithmetic, shards(): jnp.concatenate([cells for cells, _, _ in s], 0)  14.7 us
    all_gather x1, waiting for transfers between devices, shards(): lax.all_gather(jnp.concatenate([patch_weight, share_parts], 0), 'ctx', ax...  14.3 us
  transfers between devices with their start and end apart: 25, of which 12 were waited for; matrix products, arithmetic and copies ran while one was open for 28% of the time, Pallas kernels for 0%

profile of v10, /device:TPU:0, one launch (start us, length us, event | category | flops | bytes accessed | tf_op | source)
XLA Modules:
  0.0 400.4 jit_solution(9151874077539278294)
XLA Ops:
  10.0 4.1 %collective-permute-start = (bf16[6,1,32,96]{3,2,1,0:T(8,128)(2,1)}, bf16[6,1,32,96]{3,2,1,0:T(8,128)(2,1)}, u32[]{:S(2)}, u32[]{:S(2)}) collective-permute-start(bf16[6,1,32,96]{3,2,1,0:T(8,128)(2,1)} %get-tuple-element.109), channel_id=1, source_target_pairs={{0,8},{8,16},{16,24},{1,9},{9,17},{17,25},{2,10},{10,18},{18,26},{... | collective-permute-start | bytes 110600 | tf_op jit(solution)/shard_map/ppermute | solution.py:19
  22.5 3.5 collective-permute-start.2
  63.0 14.3 %all-gather.3.cloned.1.call-done = bf16[774,1280]{0,1:T(8,128)(2,1)} async-done(((bf16[774,160]{0,1:T(8,128)(2,1)}), bf16[774,1280]{0,1:T(8,128)(2,1)}) %all-gather.3.cloned.1.call-update) | async-done | bytes 1981456 | tf_op jit(solution)/shard_map/all_gather | solution.py:157
  92.9 3.9 copy.42
  104.3 24.1 %collective-permute-done.12 = bf16[320,1920]{1,0:T(8,128)(2,1)S(1)} collective-permute-done((bf16[320,1920]{1,0:T(8,128)(2,1)}, bf16[320,1920]{1,0:T(8,128)(2,1)S(1)}, u32[]{:S(2)}, u32[]{:S(2)}) %collective-permute-start.12) | collective-permute-done | bytes 1228832 | tf_op jit(solution)/shard_map/ppermute | solution.py:86
  135.2 6.4 %pad_maximum_fusion = bf16[960,1920]{1,0:T(8,128)(2,1)} fusion(bf16[320,1920]{1,0:T(8,128)(2,1)S(1)} %collective-permute-done.12, bf16[320,1920]{1,0:T(8,128)(2,1)S(1)} %collective-permute-done.11, bf16[320,1920]{1,0:T(8,128)(2,1)S(1)} %collective-permute-done.10), kind=kLoop, calls=%fused_computation.33 | loop fusion | flops 11059200 | bytes 7372800 | tf_op jit(solution)/shard_map/concatenate | solution.py:114
  141.7 27.5 %collective-permute-done.14 = bf16[160,1920]{1,0:T(8,128)(2,1)S(1)} collective-permute-done((bf16[160,1920]{1,0:T(8,128)(2,1)S(1)}, bf16[160,1920]{1,0:T(8,128)(2,1)S(1)}, u32[]{:S(2)}, u32[]{:S(2)}) %collective-permute-start.14) | collective-permute-done | bytes 614432 | tf_op jit(solution)/shard_map/ppermute | solution.py:86
  169.3 7.1 %pad_maximum_fusion.1 = bf16[960,1920]{1,0:T(8,128)(2,1)} fusion(bf16[320,1920]{1,0:T(8,128)(2,1)S(1)} %collective-permute-done.17, bf16[320,1920]{1,0:T(8,128)(2,1)S(1)} %collective-permute-done.16, bf16[160,1920]{1,0:T(8,128)(2,1)S(1)} %collective-permute-done.15, bf16[160,1920]{1,0:T(8,128)(2,1)S(1)} %collective-permute-done.14), kind=kLoop, calls=%fused_computation.34 | loop fusion | flops 14745600 | bytes 7372800 | tf_op jit(solution)/shard_map/concatenate | solution.py:114
  179.6 3.4 constant_dynamic-update-slice_fusion.14
  190.8 11.8 %collective-permute-done.19 = bf16[160,1920]{1,0:T(8,128)(2,1)S(1)} collective-permute-done((bf16[160,1920]{1,0:T(8,128)(2,1)S(1)}, bf16[160,1920]{1,0:T(8,128)(2,1)S(1)}, u32[]{:S(2)}, u32[]{:S(2)}) %collective-permute-start.19) | collective-permute-done | bytes 614432 | tf_op jit(solution)/shard_map/ppermute | solution.py:86
  202.6 12.6 %collective-permute-done.20 = bf16[160,1920]{1,0:T(8,128)(2,1)S(1)} collective-permute-done((bf16[160,1920]{1,0:T(8,128)(2,1)S(1)}, bf16[160,1920]{1,0:T(8,128)(2,1)S(1)}, u32[]{:S(2)}, u32[]{:S(2)}) %collective-permute-start.20) | collective-permute-done | bytes 614432 | tf_op jit(solution)/shard_map/ppermute | solution.py:86
  218.7 4.2 %constant_dynamic-update-slice_fusion.10 = bf16[2560,1920]{1,0:T(8,128)(2,1)} fusion(bf16[2560,1920]{1,0:T(8,128)(2,1)} %constant_dynamic-update-slice_fusion.11, bf16[960,1920]{1,0:T(8,128)(2,1)} %collective-permute-done.13), kind=kLoop, calls=%fused_computation.176 | loop fusion | bytes 7372800 | tf_op jit(solution)/shard_map/concatenate | solution.py:198
  223.0 4.1 %constant_dynamic-update-slice_fusion.15 = bf16[1920,1920]{1,0:T(8,128)(2,1)} fusion(bf16[1920,1920]{1,0:T(8,128)(2,1)} %constant_dynamic-update-slice_fusion.16, bf16[960,1920]{1,0:T(8,128)(2,1)} %collective-permute-done.18), kind=kLoop, calls=%fused_computation.181 | loop fusion | bytes 7372800 | tf_op jit(solution)/shard_map/concatenate | solution.py:198
  227.1 4.3 %constant_dynamic-slice_fusion.3 = (bf16[512,160]{1,0:T(8,128)(2,1)}, bf16[512,160]{1,0:T(8,128)(2,1)}, bf16[512,160]{1,0:T(8,128)(2,1)}, bf16[512,160]{1,0:T(8,...) fusion(bf16[512,5120]{1,0:T(8,128)(2,1)} %all-gather.5.cloned.1, ...), kind=kLoop, calls=%fused_computation.199 | loop fusion | bytes 2621472 | tf_op jit(solution)/shard_map/dynamic_slice | solution.py:192
  231.3 6.5 %constant_dynamic-slice_fusion.4 = (bf16[512,320]{1,0:T(8,128)(2,1)S(1)}, bf16[512,320]{1,0:T(8,128)(2,1)S(1)}, bf16[512,320]{1,0:T(8,128)(2,1)S(1)}, bf16[512,3...) fusion(bf16[512,5120]{1,0:T(8,128)(2,1)} %all-gather.5.cloned.1, ...), kind=kLoop, calls=%fused_computation.200 | loop fusion | bytes 6553640 | tf_op jit(solution)/shard_map/dynamic_slice | solution.py:192
  237.8 4.2 %concatenate.131 = bf16[512,1920]{1,0:T(8,128)(2,1)S(1)} concatenate(bf16[512,160]{1,0:T(8,128)(2,1)} %get-tuple-element.67, bf16[512,160]{1,0:T(8,128)(2,1)} %get-tuple-element.66, bf16[512,320]{1,0:T(8,128)(2,1)} %get-tuple-element.71, bf16[512,320]{1,0:T(8,128)(2,1)S(1)} %get-tuple-element.70, bf16[512,160]{1,0:T(8,128)(2,1)} %get-tuple-element.65, ...), dimensions={1} | concatenate | bytes 3932160 | tf_op jit(solution)/shard_map/concatenate | solution.py:197
  242.1 9.5 %fusion.149 = f32[512,1920]{1,0:T(8,128)} fusion(bf16[512,1920]{1,0:T(8,128)(2,1)S(1)} %concatenate.131, bf16[1920,1920]{1,0:T(8,128)(2,1)} %constant_dynamic-update-slice_fusion.15), kind=kOutput, calls=%fused_computation.259 | convolution fusion | flops 3774873600 | bytes 13271040 | tf_op jit(solution)/shard_map/dot_general | solution.py:196
  253.6 4.1 %concatenate.128 = bf16[512,2560]{1,0:T(8,128)(2,1)S(1)} concatenate(bf16[512,640]{1,0:T(8,128)(2,1)} %constant_dynamic-slice_fusion.19, bf16[512,320]{1,0:T(8,128)(2,1)} %get-tuple-element.77, bf16[512,320]{1,0:T(8,128)(2,1)} %get-tuple-element.76, bf16[512,320]{1,0:T(8,128)(2,1)} %get-tuple-element.75, bf16[512,320]{1,0:T(8,128)(2,1)} %get-tuple-element.74, ...), dimensions={1} | concatenate | bytes 5242880 | tf_op jit(solution)/shard_map/concatenate | solution.py:197
  257.8 8.5 %fusion.148 = f32[512,1920]{1,0:T(8,128)S(1)} fusion(bf16[512,2560]{1,0:T(8,128)(2,1)S(1)} %concatenate.128, bf16[2560,1920]{1,0:T(8,128)(2,1)} %constant_dynamic-update-slice_fusion.10), kind=kOutput, calls=%fused_computation.258 | convolution fusion | flops 5033164800 | bytes 16384000 | tf_op jit(solution)/shard_map/dot_general | solution.py:196
  266.4 4.6 %add_convert_fusion = bf16[512,1920]{1,0:T(8,128)(2,1)} fusion(f32[512,1920]{1,0:T(8,128)S(1)} %fusion.148, f32[512,1920]{1,0:T(8,128)S(1)} %copy-done.30, bf16[320,1920]{1,0:T(8,128)(2,1)} %collective-permute-done.21, bf16[160,1920]{1,0:T(8,128)(2,1)S(1)} %copy-done.20, bf16[160,1920]{1,0:T(8,128)(2,1)S(1)} %copy-done.18, ...), kind=kOutput, calls=%fused_computation.16 | convolution fusion | flops 1271234560 | bytes 12943360 | tf_op jit(solution)/shard_map/dot_general | solution.py:196
  275.5 5.8 %all-to-all-start = ((bf16[8,3,512,128]{2,3,1,0:T(8,128)(2,1)}), bf16[8,3,512,128]{2,3,1,0:T(8,128)(2,1)S(1)}, u32[]{:S(2)}, u32[]{:S(2)}) async-start(bf16[8,3,512,128]{2,3,1,0:T(8,128)(2,1)} %concatenate.137), calls=%async_computation | async-start | bytes 6291456 | tf_op jit(solution)/shard_map/all_to_all | solution.py:207
  281.3 38.9 %all-to-all-done = bf16[8,3,512,128]{2,3,1,0:T(8,128)(2,1)S(1)} async-done(((bf16[8,3,512,128]{2,3,1,0:T(8,128)(2,1)}), bf16[8,3,512,128]{2,3,1,0:T(8,128)(2,1)S(1)}, u32[]{:S(2)}, u32[]{:S(2)}) %all-to-all-start) | async-done | bytes 3145760 | tf_op jit(solution)/shard_map/all_to_all | solution.py:207
  324.3 48.6 %while.10 = (s32[]{:T(128)}, bf16[8,512,128]{1,2,0:T(8,128)(2,1)}, bf16[8,512,128]{1,2,0:T(8,128)(2,1)}, bf16[4096,128]{1,0:T(8,128)(2,1)S(1)}, bf16[4096,128]{1,0:T(8,128)(2,1)S(1)}, /*index=5*/s32[]{:T(128)}) while((s32[]{:T(128)}, bf16[8,512,128]{1,2,0:T(8,128)(2,1)}, bf16[8,512,128]{1,2,0:T(8,128)(2,1)}, bf16[4096,128]{1,0:T(8,128)(2,1)S(1)}, ...), condition=%wide.region_5.6_spmd, body=%wide.region_2.5_spmd.sunk | while | flops 1090649088 | bytes 28060740 | solution.py:220
  372.9 19.3 %all_to_all.10 = bf16[8,512,128]{1,2,0:T(8,128)(2,1)S(1)} all-to-all(bf16[8,512,128]{1,2,0:T(8,128)(2,1)} %get-tuple-element.32), channel_id=1, replica_groups=mesh['dp'=4,'head'=4,'ctx'=8] {'ctx'}, dimensions={0} | all-to-all | bytes 2097152 | tf_op jit(solution)/shard_map/all_to_all | solution.py:221
  (236 shorter events, 152.6 us)
Async XLA Ops:
  6.5 70.8 %all-gather.3.cloned.1.call-start = ((), (), s32[]{:S(2)}) async-start(), calls=%async_computation.2 | async-start | bytes 2580480 | tf_op jit(solution)/shard_map/all_gather | solution.py:157
  10.0 10.3 %collective-permute-start = (bf16[6,1,32,96]{3,2,1,0:T(8,128)(2,1)}, bf16[6,1,32,96]{3,2,1,0:T(8,128)(2,1)}, u32[]{:S(2)}, u32[]{:S(2)}) collective-permute-start(bf16[6,1,32,96]{3,2,1,0:T(8,128)(2,1)} %get-tuple-element.109), channel_id=1, source_target_pairs={{0,8},{8,16},{16,24},{1,9},{9,17},{17,25},{2,10},{10,18},{18,26},{... | collective-permute-start | bytes 110600 | tf_op jit(solution)/shard_map/ppermute | solution.py:19
  14.1 7.5 %collective-permute-start.1 = (bf16[6,1,32,96]{3,2,1,0:T(8,128)(2,1)S(1)}, bf16[6,1,32,96]{3,2,1,0:T(8,128)(2,1)}, u32[]{:S(2)}, u32[]{:S(2)}) collective-permute-start(bf16[6,1,32,96]{3,2,1,0:T(8,128)(2,1)S(1)} %get-tuple-element.108), channel_id=1, source_target_pairs={{8,0},{16,8},{24,16},{9,1},{17,9},{25,17},{10,2},{18,10},{26,18},{... | collective-permute-start | bytes 110600 | tf_op jit(solution)/shard_map/ppermute | solution.py:21
  17.4 209.7 %all-gather.5.cloned.1.call-start = ((), (), s32[]{:S(2)}) async-start(), calls=%async_computation.3 | async-start | bytes 6553600 | tf_op jit(solution)/shard_map/all_gather | solution.py:180
  22.5 5.8 %collective-permute-start.2 = (bf16[6,18,1,96]{3,2,1,0:T(2,128)(2,1)S(1)}, bf16[6,18,1,96]{3,2,1,0:T(2,128)(2,1)S(1)}, u32[]{:S(2)}, u32[]{:S(2)}) collective-permute-start(bf16[6,18,1,96]{3,2,1,0:T(2,128)(2,1)S(1)} %get-tuple-element.97), channel_id=1, source_target_pairs={{0,1},{1,2},{2,3},{3,4},{4,5},{5,6},{6,7},{8,9},{9,10},{10,11},{11... | collective-permute-start | bytes 62216 | tf_op jit(solution)/shard_map/ppermute | solution.py:19
  26.0 7.0 %collective-permute-start.3 = (bf16[6,18,1,96]{3,2,1,0:T(2,128)(2,1)S(1)}, bf16[6,18,1,96]{3,2,1,0:T(2,128)(2,1)S(1)}, u32[]{:S(2)}, u32[]{:S(2)}) collective-permute-start(bf16[6,18,1,96]{3,2,1,0:T(2,128)(2,1)S(1)} %get-tuple-element.98), channel_id=1, source_target_pairs={{1,0},{2,1},{3,2},{4,3},{5,4},{6,5},{7,6},{9,8},{10,9},{11,10},{12... | collective-permute-start | bytes 62216 | tf_op jit(solution)/shard_map/ppermute | solution.py:21
  48.6 9.7 %collective-permute-start.4 = (bf16[128,768]{1,0:T(8,128)(2,1)S(1)}, bf16[128,768]{1,0:T(8,128)(2,1)S(1)}, u32[]{:S(2)}, u32[]{:S(2)}) collective-permute-start(bf16[128,768]{1,0:T(8,128)(2,1)S(1)} %reshape.125), channel_id=1, source_target_pairs={{0,8},{8,16},{16,24},{24,0},{1,9},{9,17},{17,25},{25,1},{2,10},{10... | collective-permute-start | bytes 589832 | tf_op jit(solution)/shard_map/ppermute | solution.py:32
  51.3 9.8 %collective-permute-start.5 = (bf16[128,768]{1,0:T(8,128)(2,1)S(1)}, bf16[128,768]{1,0:T(8,128)(2,1)S(1)}, u32[]{:S(2)}, u32[]{:S(2)}) collective-permute-start(bf16[128,768]{1,0:T(8,128)(2,1)S(1)} %reshape.125), channel_id=1, source_target_pairs={{0,16},{8,24},{16,0},{24,8},{1,17},{9,25},{17,1},{25,9},{2,18},{10... | collective-permute-start | bytes 589832 | tf_op jit(solution)/shard_map/ppermute | solution.py:32
  54.1 7.0 %collective-permute-start.6 = (bf16[128,768]{1,0:T(8,128)(2,1)S(1)}, bf16[128,768]{1,0:T(8,128)(2,1)S(1)}, u32[]{:S(2)}, u32[]{:S(2)}) collective-permute-start(bf16[128,768]{1,0:T(8,128)(2,1)S(1)} %reshape.125), channel_id=1, source_target_pairs={{0,24},{8,0},{16,8},{24,16},{1,25},{9,1},{17,9},{25,17},{2,26},{10... | collective-permute-start | bytes 589832 | tf_op jit(solution)/shard_map/ppermute | solution.py:32
  81.9 6.0 %collective-permute-start.7 = (f32[3072]{0:T(1024)S(1)}, f32[3072]{0:T(1024)S(1)}, u32[]{:S(2)}, u32[]{:S(2)}) collective-permute-start(f32[3072]{0:T(1024)S(1)} %pad_maximum_fusion.8), channel_id=1, source_target_pairs={{0,8},{8,16},{16,24},{24,0},{1,9},{9,17},{17,25},{25,1},{2,10},{10... | collective-permute-start | bytes 36872 | tf_op jit(solution)/shard_map/ppermute | solution.py:32
  84.0 5.2 %collective-permute-start.8 = (f32[3072]{0:T(1024)S(1)}, f32[3072]{0:T(1024)S(1)}, u32[]{:S(2)}, u32[]{:S(2)}) collective-permute-start(f32[3072]{0:T(1024)S(1)} %pad_maximum_fusion.8), channel_id=1, source_target_pairs={{0,16},{8,24},{16,0},{24,8},{1,17},{9,25},{17,1},{25,9},{2,18},{10... | collective-permute-start | bytes 36872 | tf_op jit(solution)/shard_map/ppermute | solution.py:32
  101.1 27.4 %collective-permute-start.12 = (bf16[320,1920]{1,0:T(8,128)(2,1)}, bf16[320,1920]{1,0:T(8,128)(2,1)S(1)}, u32[]{:S(2)}, u32[]{:S(2)}) collective-permute-start(bf16[320,1920]{1,0:T(8,128)(2,1)} %copy.43), channel_id=1, source_target_pairs={{0,1},{1,0},{2,3},{3,2},{4,5},{5,4},{6,7},{7,6},{8,9},{9,8},{10,11... | collective-permute-start | bytes 3686408 | tf_op jit(solution)/shard_map/ppermute | solution.py:86
  101.1 30.6 %collective-permute-start.10 = (bf16[320,1920]{1,0:T(8,128)(2,1)}, bf16[320,1920]{1,0:T(8,128)(2,1)S(1)}, u32[]{:S(2)}, u32[]{:S(2)}) collective-permute-start(bf16[320,1920]{1,0:T(8,128)(2,1)} %copy.43), channel_id=1, source_target_pairs={{0,2},{1,3},{2,4},{3,5},{4,6},{5,7},{6,0},{7,1},{8,10},{9,11},{10,... | collective-permute-start | bytes 3686408 | tf_op jit(solution)/shard_map/ppermute | solution.py:86
  102.6 29.3 %collective-permute-start.11 = (bf16[320,1920]{1,0:T(8,128)(2,1)}, bf16[320,1920]{1,0:T(8,128)(2,1)S(1)}, u32[]{:S(2)}, u32[]{:S(2)}) collective-permute-start(bf16[320,1920]{1,0:T(8,128)(2,1)} %copy.43), channel_id=1, source_target_pairs={{0,6},{1,7},{2,0},{3,1},{4,2},{5,3},{6,4},{7,5},{8,14},{9,15},{10,... | collective-permute-start | bytes 3686408 | tf_op jit(solution)/shard_map/ppermute | solution.py:86
  128.5 40.8 %collective-permute-start.16 = (bf16[320,1920]{1,0:T(8,128)(2,1)S(1)}, bf16[320,1920]{1,0:T(8,128)(2,1)S(1)}, u32[]{:S(2)}, u32[]{:S(2)}) collective-permute-start(bf16[320,1920]{1,0:T(8,128)(2,1)S(1)} %collective-permute-done.12), channel_id=1, source_target_pairs={{0,2},{1,3},{2,4},{3,5},{4,6},{5,7},{6,0},{7,1},{8,10},{9,11},{10,... | collective-permute-start | bytes 3686408 | tf_op jit(solution)/shard_map/ppermute | solution.py:86
  128.8 40.5 %collective-permute-start.17 = (bf16[320,1920]{1,0:T(8,128)(2,1)S(1)}, bf16[320,1920]{1,0:T(8,128)(2,1)S(1)}, u32[]{:S(2)}, u32[]{:S(2)}) collective-permute-start(bf16[320,1920]{1,0:T(8,128)(2,1)S(1)} %collective-permute-done.12), channel_id=1, source_target_pairs={{0,6},{1,7},{2,0},{3,1},{4,2},{5,3},{6,4},{7,5},{8,14},{9,15},{10,... | collective-permute-start | bytes 3686408 | tf_op jit(solution)/shard_map/ppermute | solution.py:86
  131.7 37.4 %collective-permute-start.14 = (bf16[160,1920]{1,0:T(8,128)(2,1)S(1)}, bf16[160,1920]{1,0:T(8,128)(2,1)S(1)}, u32[]{:S(2)}, u32[]{:S(2)}) collective-permute-start(bf16[160,1920]{1,0:T(8,128)(2,1)S(1)} %slice.351), channel_id=1, source_target_pairs={{0,2},{1,3},{2,4},{3,5},{4,6},{5,7},{6,0},{7,1},{8,10},{9,11},{10,... | collective-permute-start | bytes 1843208 | tf_op jit(solution)/shard_map/ppermute | solution.py:86
  131.9 37.4 %collective-permute-start.15 = (bf16[160,1920]{1,0:T(8,128)(2,1)S(1)}, bf16[160,1920]{1,0:T(8,128)(2,1)S(1)}, u32[]{:S(2)}, u32[]{:S(2)}) collective-permute-start(bf16[160,1920]{1,0:T(8,128)(2,1)S(1)} %slice.352), channel_id=1, source_target_pairs={{0,6},{1,7},{2,0},{3,1},{4,2},{5,3},{6,4},{7,5},{8,14},{9,15},{10,... | collective-permute-start | bytes 1843208 | tf_op jit(solution)/shard_map/ppermute | solution.py:86
  141.6 77.2 %collective-permute-start.13 = (bf16[960,1920]{1,0:T(8,128)(2,1)}, bf16[960,1920]{1,0:T(8,128)(2,1)}, u32[]{:S(2)}, u32[]{:S(2)}) collective-permute-start(bf16[960,1920]{1,0:T(8,128)(2,1)} %pad_maximum_fusion), channel_id=1, source_target_pairs={{0,32},{32,0},{64,96},{96,64},{1,33},{33,1},{65,97},{97,65},{2,34}... | collective-permute-start | bytes 11059208 | tf_op jit(solution)/shard_map/ppermute | solution.py:89
  176.4 46.6 %collective-permute-start.18 = (bf16[960,1920]{1,0:T(8,128)(2,1)}, bf16[960,1920]{1,0:T(8,128)(2,1)}, u32[]{:S(2)}, u32[]{:S(2)}) collective-permute-start(bf16[960,1920]{1,0:T(8,128)(2,1)} %pad_maximum_fusion.1), channel_id=1, source_target_pairs={{0,32},{32,0},{64,96},{96,64},{1,33},{33,1},{65,97},{97,65},{2,34}... | collective-permute-start | bytes 11059208 | tf_op jit(solution)/shard_map/ppermute | solution.py:89
  185.9 16.7 %collective-permute-start.19 = (bf16[160,1920]{1,0:T(8,128)(2,1)S(1)}, bf16[160,1920]{1,0:T(8,128)(2,1)S(1)}, u32[]{:S(2)}, u32[]{:S(2)}) collective-permute-start(bf16[160,1920]{1,0:T(8,128)(2,1)S(1)} %collective-permute-done.14), channel_id=1, source_target_pairs={{0,1},{1,0},{2,3},{3,2},{4,5},{5,4},{6,7},{7,6},{8,9},{9,8},{10,11... | collective-permute-start | bytes 1843208 | tf_op jit(solution)/shard_map/ppermute | solution.py:86
  187.6 27.6 %collective-permute-start.20 = (bf16[160,1920]{1,0:T(8,128)(2,1)S(1)}, bf16[160,1920]{1,0:T(8,128)(2,1)S(1)}, u32[]{:S(2)}, u32[]{:S(2)}) collective-permute-start(bf16[160,1920]{1,0:T(8,128)(2,1)S(1)} %copy-done.14), channel_id=1, source_target_pairs={{0,1},{1,0},{2,3},{3,2},{4,5},{5,4},{6,7},{7,6},{8,9},{9,8},{10,11... | collective-permute-start | bytes 1843208 | tf_op jit(solution)/shard_map/ppermute | solution.py:86
  216.4 49.9 %collective-permute-start.21 = (bf16[320,1920]{1,0:T(8,128)(2,1)}, bf16[320,1920]{1,0:T(8,128)(2,1)}, u32[]{:S(2)}, u32[]{:S(2)}) collective-permute-start(bf16[320,1920]{1,0:T(8,128)(2,1)} %pad_maximum_fusion.4), channel_id=1, source_target_pairs={{0,32},{32,0},{64,96},{96,64},{1,33},{33,1},{65,97},{97,65},{2,34}... | collective-permute-start | bytes 3686408 | tf_op jit(solution)/shard_map/ppermute | solution.py:89
  275.5 44.6 %all-to-all-start = ((bf16[8,3,512,128]{2,3,1,0:T(8,128)(2,1)}), bf16[8,3,512,128]{2,3,1,0:T(8,128)(2,1)S(1)}, u32[]{:S(2)}, u32[]{:S(2)}) async-start(bf16[8,3,512,128]{2,3,1,0:T(8,128)(2,1)} %concatenate.137), calls=%async_computation | async-start | bytes 6291456 | tf_op jit(solution)/shard_map/all_to_all | solution.py:207
  (32 other events, 321.3 us)
Sparse Core Ops, SparseCore 0:
  17.5 59.8 all-gather.2
  93.0 55.8 all-gather.4
